TPU v7x, 256 devices: a whole 4x4x8 slice. The times are simulated.
256 devices in a mesh: seq: 32 (over y, x, core), resp: 8 (over z).
Axes of the slice: x: 4, y: 4, z: 8, core: 2. Of those that a mesh axis runs over, the one named last changes fastest.
Arguments:
- prompt_grad: bfloat16 [32768, 4096], P('seq', 'resp'), may hold values from -0.119628906 to 0.119628906
- prompt_keys: bfloat16 [32768, 128], P('seq'), may hold values from -6 to 6
- prompt_queries: bfloat16 [32768, 128], P('seq'), may hold values from -0.52734375 to 0.52734375
- prompt_decay: float32 [64, 32768], P('resp', 'seq'), may hold values from -2 to 0
- resp_grad: bfloat16 [32768, 4096], P('resp', 'seq'), may hold values from -0.119628906 to 0.119628906
- resp_keys: bfloat16 [32768, 128], P('resp'), may hold values from -6 to 6
- resp_queries: bfloat16 [32768, 128], P('resp'), may hold values from -0.52734375 to 0.52734375
- resp_decay: float32 [64, 32768], P('seq', 'resp'), may hold values from -2 to 0
- resp_segment: int32 [32768], P('resp'), may hold values from 0 to 8, as said below
Outputs:
- prompt_dx: bfloat16 [32768, 4096], P('seq', 'resp')
- resp_dx: bfloat16 [32768, 4096], P('resp', 'seq')
Inputs may be any that keep to these rules, and one draw needn't show every extreme that they name: `resp_segment`: each aligned block of 4096 slots holds responses 0 to 7 in this order, each of one slot or more, then padding slots marked 8; a block holds 1024 live slots or more, and some block has no padding.
All inputs are finite; a program needn't handle non-finite values.
Results may differ from a plain program's by a relative error of at most 0.0057.
Values sent between devices are 32-bit elements; how exact they have to be, the bound alone decides.
No kernel may reach another device: no remote copies, remote signals or barrier semaphores. Data moves between devices by JAX's collectives and lax.ppermute only.
A program may use at most 64 MiB of HBM per device.

v0:
```python
import jax
import jax.numpy as jnp
from jax import lax
from jax.sharding import PartitionSpec as P

P_SIZE = 64
N = 128
GROUP = 256
RESP_DEV = 8


def group_parts(out_grad, queries, decay, segment, alive_mask):
    tokens = out_grad.shape[0]
    head_count = decay.shape[0]
    groups = tokens // GROUP
    cum_sums = jnp.cumsum(decay, axis=1)
    cum_group = cum_sums.reshape(head_count, groups, GROUP).transpose(1, 0, 2)
    decay_group = decay.reshape(head_count, groups, GROUP).transpose(1, 0, 2)
    before = cum_group[:, :, 0] - decay_group[:, :, 0]
    seg_group = segment.reshape(groups, GROUP)
    alive_group = alive_mask.reshape(groups, GROUP)
    first_label = seg_group[:, 0]
    last_label = seg_group[:, -1]
    grad_group = out_grad.reshape(groups, GROUP, head_count, P_SIZE)
    query_group = queries.reshape(groups, GROUP, N)
    keep_mask = (seg_group == first_label[:, None]) & alive_group
    factor = jnp.where(keep_mask[:, None, :], jnp.exp(cum_group - before[:, :, None]), 0.0)
    weighted = (factor.transpose(0, 2, 1)[:, :, :, None] * grad_group).astype(jnp.bfloat16)
    states = jnp.einsum("clhp,cln->chpn", weighted, query_group, preferred_element_type=jnp.float32)
    group_gains = jnp.exp(cum_group[:, :, -1] - before)
    joined = (first_label == last_label).astype(jnp.float32)
    linked = jnp.concatenate(
        [jnp.ones((1,), jnp.float32), (last_label[:-1] == first_label[1:]).astype(jnp.float32)]
    )

    def backstep(later_grad, pieces):
        group_state, group_gain, whole_seg, link_flag = pieces
        updated = group_state + (whole_seg * group_gain)[:, None, None] * later_grad
        return (link_flag * updated, later_grad)

    start_grad, end_grads = lax.scan(
        backstep,
        jnp.zeros((head_count, P_SIZE, N), jnp.float32),
        (states, group_gains, joined, linked),
        reverse=True,
    )
    return (
        cum_sums,
        cum_group,
        seg_group,
        alive_group,
        last_label,
        grad_group,
        end_grads,
        start_grad,
    )


def group_output(key_rows, queries, parts):
    cum_sums, cum_group, seg_group, alive_group, last_label, grad_group, end_grads, start_grad = (
        parts
    )
    groups = seg_group.shape[0]
    head_count = cum_group.shape[1]
    key_group = key_rows.reshape(groups, GROUP, N)
    query_group = queries.reshape(groups, GROUP, N)
    scores = jnp.einsum("csn,ctn->cst", query_group, key_group, preferred_element_type=jnp.float32)
    row_index = lax.broadcasted_iota(jnp.int32, (GROUP, GROUP), 0)
    col_index = lax.broadcasted_iota(jnp.int32, (GROUP, GROUP), 1)
    keep_mask = (
        (row_index >= col_index)[None]
        & (seg_group[:, :, None] == seg_group[:, None, :])
        & alive_group[:, :, None]
    )
    spread = cum_group[:, :, :, None] - cum_group[:, :, None, :]
    decays = jnp.exp(jnp.where(keep_mask[:, None], spread, -jnp.inf))
    mixing = (scores[:, None] * decays).astype(jnp.bfloat16)
    inner_part = jnp.einsum(
        "chst,cshp->cthp", mixing, grad_group, preferred_element_type=jnp.float32
    )
    across = jnp.einsum(
        "chpn,ctn->cthp",
        end_grads.astype(jnp.bfloat16),
        key_group,
        preferred_element_type=jnp.float32,
    )
    reach_weight = jnp.where(
        (seg_group == last_label[:, None])[:, None, :],
        jnp.exp(cum_group[:, :, -1:] - cum_group),
        0.0,
    )
    summed_parts = inner_part + across * reach_weight.transpose(0, 2, 1)[:, :, :, None]
    return summed_parts.reshape(groups * GROUP, head_count * P_SIZE)


def initial_state(out_grad, queries, decay, segment, alive_mask, cum_sums):
    tokens = out_grad.shape[0]
    head_count = decay.shape[0]
    firsts = jnp.concatenate([jnp.ones((1,), jnp.bool_), segment[1:] != segment[:-1]])
    labels = jnp.arange(RESP_DEV + 1, dtype=jnp.int32)
    member = segment[:, None] == labels[None, :]
    opening = cum_sums - decay
    base_label = jnp.sum(
        jnp.where((member & firsts[:, None])[None], opening[:, :, None], 0.0), axis=1
    )
    base_token = jnp.sum(jnp.where(member[None], base_label[:, None, :], 0.0), axis=2)
    factor = jnp.where(alive_mask[None], jnp.exp(cum_sums - base_token), 0.0)
    weighted = (factor.T[:, :, None] * out_grad.reshape(tokens, head_count, P_SIZE)).astype(
        jnp.bfloat16
    )
    return jnp.einsum("thp,tn->hpn", weighted, queries, preferred_element_type=jnp.float32)


def on_device(
    prompt_grad,
    prompt_keys,
    prompt_queries,
    prompt_decay,
    resp_grad,
    resp_keys,
    resp_queries,
    resp_decay,
    resp_segment,
):
    resp_alive = resp_segment < RESP_DEV
    resp_parts = group_parts(resp_grad, resp_queries, resp_decay, resp_segment, resp_alive)
    resp_dx = group_output(resp_keys, resp_queries, resp_parts).astype(jnp.bfloat16)
    partial_state = initial_state(
        resp_grad, resp_queries, resp_decay, resp_segment, resp_alive, resp_parts[0]
    )
    summed_state = lax.psum(partial_state, "resp")
    head_count = prompt_decay.shape[0]
    prompt_len = prompt_grad.shape[0]
    zero_label = jnp.zeros((prompt_len,), jnp.int32)
    all_alive = jnp.ones((prompt_len,), jnp.bool_)
    prompt_parts = group_parts(prompt_grad, prompt_queries, prompt_decay, zero_label, all_alive)
    cum_sums = prompt_parts[0]
    start_grad = prompt_parts[7]
    shard_total = cum_sums[:, -1]
    seq_index = lax.axis_index("seq")
    every_head = lax.all_gather(summed_state, "seq", axis=0, tiled=True)
    my_heads = lax.dynamic_slice_in_dim(
        every_head, lax.axis_index("resp") * head_count, head_count, 0
    )
    all_totals = lax.all_gather(shard_total[None, :], "seq", axis=0, tiled=True)
    inclusive = jnp.cumsum(all_totals, axis=0)
    exclusive = inclusive - all_totals
    my_inclusive = lax.dynamic_index_in_dim(inclusive, seq_index, 0, keepdims=False)
    piece = lax.all_gather(start_grad[None], "seq", axis=0, tiled=True)
    span_len = piece.shape[0]
    order = jnp.arange(span_len, dtype=jnp.int32)
    weight = jnp.exp(
        jnp.where((order > seq_index)[:, None], exclusive - my_inclusive[None, :], -jnp.inf)
    )
    gathered = jnp.sum(weight[:, :, None, None] * piece, axis=0)
    incoming = gathered + jnp.exp(inclusive[-1] - my_inclusive)[:, None, None] * my_heads
    local_part = group_output(prompt_keys, prompt_queries, prompt_parts)
    carry_term = jnp.einsum(
        "hpn,tn->thp",
        incoming.astype(jnp.bfloat16),
        prompt_keys,
        preferred_element_type=jnp.float32,
    )
    carry_term = carry_term * jnp.exp(shard_total[:, None] - cum_sums).T[:, :, None]
    prompt_dx = (local_part + carry_term.reshape(prompt_len, head_count * P_SIZE)).astype(
        jnp.bfloat16
    )
    return (prompt_dx, resp_dx)


def solution(mesh):
    return jax.shard_map(
        on_device,
        mesh=mesh,
        in_specs=(
            P("seq", "resp"),
            P("seq", None),
            P("seq", None),
            P("resp", "seq"),
            P("resp", "seq"),
            P("resp", None),
            P("resp", None),
            P("seq", "resp"),
            P("resp"),
        ),
        out_specs=(P("seq", "resp"), P("resp", "seq")),
        check_vma=False,
    )
```

profile of v0, /device:TPU:1, one launch (start us, length us, event | category | flops | bytes accessed | tf_op | source)
XLA Modules:
  0.0 233.4 jit_solution(16602394450113765104)
XLA Ops:
  16.8 2.3 reduce-window.14
  26.3 1.9 reshape.225
  30.7 3.2 %while.34 = (s32[]{:T(128)}, f32[8,64,128]{2,1,0:T(8,128)S(1)}, bf16[4,8,64,128]{3,2,1,0:T(8,128)(2,1)}, f32[4,8,64,128]{3,2,1,0:T(8,128)S(1)}, f32[4,8]{1,0:T(4,128)S(1)}, /*index=5*/s32[]{:T(128)}, s32[]{:T(128)}, s32[]{:T(128)}) while((s32[]{:T(128)}, f32[8,64,128]{2,1,0:T(8,128)S(1)}, bf16[4,8,64,128]{3,2,1,0:T(8,128)(2,1)}, ...), condition=%wide.region_3.4_spmd.clone, body=%wide.region_2.3_spmd.clone.sunk | while | flops 262148 | bytes 1179864 | solution.py:41
  39.3 66.1 %all-reduce = f32[256]{0:T(256)S(1)} all-reduce(f32[256]{0:T(256)S(1)} %bitcast_dynamic-update-slice_fusion.2), channel_id=2, replica_groups=mesh['seq'=32,'resp'=8] {'seq'}, use_global_device_ids=true, to_apply=%add | all-reduce | flops 256 | bytes 2048
  113.4 1.6 fusion.26
  115.2 55.5 %while.35 = (s32[]{:T(128)}, f32[2,64,128]{2,1,0:T(8,128)S(1)}, bf16[16,2,64,128]{3,2,1,0:T(8,128)(2,1)S(1)}, f32[16]{0:T(128)S(1)}, f32[16,2,64,128]{3,2,1,0:T(...) while((s32[]{:T(128)}, f32[2,64,128]{2,1,0:T(8,128)S(1)}, ...), condition=%wide.region_12.13_spmd.clone, body=%wide.region_11.12_spmd.clone.sunk | while | flops 81926 | bytes 295104 | solution.py:41
  117.1 1.6 fusion.83
  120.5 1.6 fusion.83
  124.0 1.6 fusion.83
  127.5 1.6 fusion.83
  130.9 1.6 fusion.83
  134.4 1.6 fusion.83
  137.9 1.6 fusion.83
  141.3 1.6 fusion.83
  144.8 1.6 fusion.83
  148.3 1.6 fusion.83
  151.7 1.6 fusion.83
  155.2 1.6 fusion.83
  158.7 1.6 fusion.83
  162.2 1.6 fusion.83
  165.6 1.6 fusion.83
  169.1 1.6 fusion.83
  171.1 1.5 fusion.65
  172.6 2.2 fusion.22
  176.2 1.8 copy.159
  180.6 3.8 %fusion.7 = f32[16,2,256,64]{2,3,1,0:T(8,128)S(1)} fusion(f32[16,2,256]{2,1,0:T(2,128)S(1)} %bitcast.222, f32[16,256,256]{2,1,0:T(8,128)S(1)} %fusion.64, pred[16,256,256]{2,1,0:T(8,128)(4,1)S(1)} %and_and_fusion, bf16[16,256,2,64]{1,0,3,2:T(8,128)(2,1)S(1)} %bitcast.201), kind=kOutput, calls=%fused_computation.16 | convolution fusion | flops 276824064 | bytes 8421376 | tf_op jit(solution)/shard_map/chst,cshp->cthp/dot_general | solution.py:78
  185.8 4.5 %copy.156 = bf16[16,256,2,64]{3,2,1,0:T(2,128)(2,1)S(1)} copy(bf16[16,256,2,64]{1,3,2,0:T(8,128)(2,1)} %fusion.20) | data formatting | bytes 2097152
  190.4 1.8 reshape.250
  192.4 4.8 %multiply_reduce_fusion = f32[8,64,128]{2,1,0:T(8,128)} fusion(f32[32,8,64,128]{3,2,1,0:T(8,128)} %bitcast.193, f32[32,8]{1,0:T(8,128)S(1)} %select_exponential_fusion), kind=kLoop, calls=%fused_computation.12 | loop fusion | flops 4128768 | bytes 8651776 | tf_op jit(solution)/shard_map/reduce_sum | solution.py:155
  197.1 23.7 %all-gather.5.cloned.1.call-done = f32[64,64,128]{2,1,0:T(8,128)} async-done(((f32[2,64,128]{2,1,0:T(8,128)}), f32[64,64,128]{2,1,0:T(8,128)}) %all-gather.5.cloned.1.call-update) | async-done | bytes 2097168 | tf_op jit(solution)/shard_map/all_gather | solution.py:141
  220.8 1.5 bitcast_multiply_fusion.1
  223.7 2.3 copy.146
  (216 shorter events, 71.7 us)
Async XLA Ops:
  8.0 171.4 %copy-start = (bf16[4096,128]{1,0:T(8,128)(2,1)S(1)}, bf16[4096,128]{1,0:T(8,128)(2,1)}, u32[]{:S(2)}) copy-start(bf16[4096,128]{1,0:T(8,128)(2,1)} %param.18) | copy-start | bytes 3145732
  8.0 162.7 %all-reduce.3.cloned.1.call-start = ((), (), s32[]{:S(2)}) async-start(), calls=%async_computation | async-start | bytes 131072 | tf_op jit(solution)/shard_map/psum | solution.py:131
  9.7 5.8 %copy-start.19 = (pred[4096]{0:T(1024)(128)(4,1)}, pred[4096]{0:T(1024)(128)(4,1)S(1)}, u32[]{:S(2)}) copy-start(pred[4096]{0:T(1024)(128)(4,1)S(1)} %broadcast_compare_fusion.1) | copy-start | bytes 12292
  11.4 0.5 copy-start.25
  11.4 4.2 %copy-start.3 = (bf16[4096,128]{1,0:T(8,128)(2,1)S(1)}, bf16[4096,128]{1,0:T(8,128)(2,1)}, u32[]{:S(2)}) copy-start(bf16[4096,128]{1,0:T(8,128)(2,1)} %param.19) | copy-start | bytes 3145732
  15.1 1.6 copy-start.6
  15.1 1.7 copy-start.16
  16.7 175.7 %all-gather.7.cloned.1.call-start = ((), (), s32[]{:S(2)}) async-start(), calls=%async_computation.2 | async-start | bytes 8650752 | tf_op jit(solution)/shard_map/all_gather | solution.py:149
  16.7 8.2 %copy-start.11 = (bf16[1024,512]{1,0:T(8,128)(2,1)S(1)}, bf16[1024,512]{1,0:T(8,128)(2,1)}, u32[]{:S(2)}) copy-start(bf16[1024,512]{1,0:T(8,128)(2,1)} %param.13) | copy-start | bytes 3145732
  19.4 8.8 %copy-start.21 = (f32[8,9]{1,0:T(8,128)}, f32[8,9]{1,0:T(8,128)S(1)}, u32[]{:S(2)}) copy-start(f32[8,9]{1,0:T(8,128)S(1)} %reduce-window.15) | copy-start | bytes 868
  28.2 1.0 copy-start.4
  28.2 1.1 copy-start.12
  30.7 4.0 %copy-start.14 = (s32[4096]{0:T(1024)S(1)}, s32[4096]{0:T(1024)}, u32[]{:S(2)}) copy-start(s32[4096]{0:T(1024)} %param.21) | copy-start | bytes 49156
  30.7 4.0 %copy-start.20 = (pred[4096]{0:T(1024)(128)(4,1)S(1)}, pred[4096]{0:T(1024)(128)(4,1)}, u32[]{:S(2)}) copy-start(pred[4096]{0:T(1024)(128)(4,1)} %copy-done.19) | copy-start | bytes 12292
  30.7 4.1 %copy-start.26 = (f32[2,33]{1,0:T(2,128)S(1)}, f32[2,33]{1,0:T(2,128)}, u32[]{:S(2)}) copy-start(f32[2,33]{1,0:T(2,128)} %copy-done.25) | copy-start | bytes 796
  33.9 0.7 copy-start.1
  33.9 76.5 %copy-start.7 = (bf16[4096,128]{0,1:T(8,128)(2,1)S(1)}, bf16[4096,128]{0,1:T(8,128)(2,1)}, u32[]{:S(2)}) copy-start(bf16[4096,128]{0,1:T(8,128)(2,1)} %copy-done.6) | copy-start | bytes 3145732
  34.6 186.2 %all-gather.5.cloned.1.call-start = ((), (), s32[]{:S(2)}) async-start(), calls=%async_computation.1 | async-start | bytes 2162688 | tf_op jit(solution)/shard_map/all_gather | solution.py:141
  34.7 78.7 %copy-start.17 = (pred[16,256]{1,0:T(8,128)(4,1)}, pred[16,256]{1,0:T(8,128)(4,1)S(1)}, u32[]{:S(2)}) copy-start(pred[16,256]{1,0:T(8,128)(4,1)S(1)} %and.54) | copy-start | bytes 12292
  37.3 71.3 %copy-start.27 = (f32[8,1]{0,1:T(1,128)}, f32[8,1]{0,1:T(1,128)S(1)}, u32[]{:S(2)}) copy-start(f32[8,1]{0,1:T(1,128)S(1)} %copy.158) | copy-start | bytes 100
  113.4 57.3 %copy-start.9 = (bf16[1024,128]{1,0:T(8,128)(2,1)S(1)}, bf16[1024,128]{1,0:T(8,128)(2,1)}, u32[]{:S(2)}) copy-start(bf16[1024,128]{1,0:T(8,128)(2,1)} %param.14) | copy-start | bytes 786436
  113.4 57.3 %copy-start.13 = (bf16[1024,128]{1,0:T(8,128)(2,1)S(1)}, bf16[1024,128]{1,0:T(8,128)(2,1)}, u32[]{:S(2)}) copy-start(bf16[1024,128]{1,0:T(8,128)(2,1)} %param.15) | copy-start | bytes 786436
  170.7 1.8 copy-start.5
  170.7 1.8 copy-start.22
  170.7 1.8 copy-start.24
  176.2 1.8 copy-start.18
  179.4 1.2 copy-start.8
  179.4 1.2 copy-start.23
  180.6 3.8 %copy-start.15 = (f32[16,256,2]{1,2,0:T(2,128)S(1)}, f32[16,256,2]{1,2,0:T(2,128)}, u32[]{:S(2)}) copy-start(f32[16,256,2]{1,2,0:T(2,128)} %get-tuple-element.368) | copy-start | bytes 98308
  190.3 1.9 copy-start.28
  192.4 28.4 %copy-start.10 = (bf16[1024,128]{1,0:T(8,128)(2,1)S(1)}, bf16[1024,128]{1,0:T(8,128)(2,1)}, u32[]{:S(2)}) copy-start(bf16[1024,128]{1,0:T(8,128)(2,1)} %param.14) | copy-start | bytes 786436
  197.1 25.2 %copy-start.2 = (f32[64,8,4,256]{3,1,2,0:T(8,128)S(1)}, f32[64,8,4,256]{3,1,2,0:T(8,128)}, u32[]{:S(2)}) copy-start(f32[64,8,4,256]{3,1,2,0:T(8,128)} %copy.159) | copy-start | bytes 6291460
Sparse Core Ops, SparseCore 0:
  16.8 72.1 all-reduce.2
Sparse Core Ops, SparseCore 1:
  34.7 62.0 all-gather.6
  170.8 49.9 all-gather.4
where the time goes:
time: 235 us; the launch traced here: 233 us
  blocking collectives  66.1 us (28%)
  other arithmetic  59.8 us (25%)
  local copies, waits for them, and re-layouts  51.7 us (22%)
  waiting for transfers between devices  23.8 us (10%)
  between operations  16.7 us (7%)
  matrix products  14.5 us (6%)
    unnamed x1, blocking collectives  66.1 us
    mul x16, other arithmetic, backstep(): return (link_flag * updated, later_grad)  24.8 us
    all_gather x1, waiting for transfers between devices, on_device(): every_head = lax.all_gather(summed_state, 'seq', axis=0, tiled=True)  23.7 us
    unnamed x73, local copies, waits for them, and re-layouts  20 us
    dynamic_slice x32, local copies, waits for them, and re-layouts, group_parts(): lax.scan(backstep, jnp.zeros((head_count, P_SIZE, N), jnp.float32), (stat...  19.5 us
    mul x16, other arithmetic, backstep(): updated = group_state + (whole_seg * group_gain)[:, None, None] * later_grad  10.2 us
    dot_general x2, matrix products, group_output(): jnp.einsum('chst,cshp->cthp', mixing, grad_group, preferred_element_type=...  6 us
    reduce_sum x1, other arithmetic, on_device(): gathered = jnp.sum(weight[:, :, None, None] * piece, axis=0)  4.76 us
  transfers between devices with their start and end apart: 3, of which 1 were waited for; matrix products, arithmetic and copies ran while one was open for 47% of the time, Pallas kernels for 0%

commit v1 on v0

--- a/solution.py
+++ b/solution.py
@@ -33,17 +33,21 @@
         [jnp.ones((1,), jnp.float32), (last_label[:-1] == first_label[1:]).astype(jnp.float32)]
     )
 
-    def backstep(later_grad, pieces):
-        group_state, group_gain, whole_seg, link_flag = pieces
-        updated = group_state + (whole_seg * group_gain)[:, None, None] * later_grad
-        return (link_flag * updated, later_grad)
-
-    start_grad, end_grads = lax.scan(
-        backstep,
-        jnp.zeros((head_count, P_SIZE, N), jnp.float32),
-        (states, group_gains, joined, linked),
-        reverse=True,
-    )
+    flow = joined[:, None] * group_gains * jnp.concatenate(
+        [linked[1:], jnp.zeros((1,), jnp.float32)]
+    )[:, None]
+    carry_at = jnp.arange(groups + 1)[:, None, None]
+    state_at = jnp.arange(groups)[None, :, None]
+    step_at = jnp.arange(groups)[None, None, :]
+    inside = (carry_at <= step_at) & (step_at < state_at)
+    spans = jnp.prod(jnp.where(inside[None], flow.T[:, None, None, :], 1.0), axis=3)
+    link_at = jnp.concatenate([linked, jnp.zeros((1,), jnp.float32)])
+    coef = jnp.where((carry_at[:, :, 0] <= state_at[:, :, 0])[None], spans, 0.0) * link_at[None, :, None]
+    carries = jnp.einsum(
+        "hcd,dhpn->chpn", coef, states, precision=lax.Precision.HIGHEST
+    )
+    start_grad = carries[0]
+    end_grads = carries[1:]
     return (
         cum_sums,
         cum_group,
@@ -138,22 +142,38 @@
     start_grad = prompt_parts[7]
     shard_total = cum_sums[:, -1]
     seq_index = lax.axis_index("seq")
-    every_head = lax.all_gather(summed_state, "seq", axis=0, tiled=True)
-    my_heads = lax.dynamic_slice_in_dim(
-        every_head, lax.axis_index("resp") * head_count, head_count, 0
-    )
-    all_totals = lax.all_gather(shard_total[None, :], "seq", axis=0, tiled=True)
-    inclusive = jnp.cumsum(all_totals, axis=0)
-    exclusive = inclusive - all_totals
-    my_inclusive = lax.dynamic_index_in_dim(inclusive, seq_index, 0, keepdims=False)
-    piece = lax.all_gather(start_grad[None], "seq", axis=0, tiled=True)
-    span_len = piece.shape[0]
-    order = jnp.arange(span_len, dtype=jnp.int32)
-    weight = jnp.exp(
-        jnp.where((order > seq_index)[:, None], exclusive - my_inclusive[None, :], -jnp.inf)
-    )
-    gathered = jnp.sum(weight[:, :, None, None] * piece, axis=0)
-    incoming = gathered + jnp.exp(inclusive[-1] - my_inclusive)[:, None, None] * my_heads
+    resp_index = lax.axis_index("resp")
+    first_head = seq_index * summed_state.shape[0]
+    owned = first_head // head_count == resp_index
+    slots = lax.dynamic_update_slice_in_dim(
+        jnp.zeros((head_count,) + summed_state.shape[1:], jnp.float32),
+        summed_state,
+        first_head % head_count,
+        0,
+    )
+    my_heads = lax.psum(jnp.where(owned, slots, 0.0), "seq")
+    span_len = lax.axis_size("seq")
+    whole_b = start_grad
+    whole_a = jnp.exp(shard_total)
+    later_b = jnp.zeros_like(start_grad)
+    later_a = jnp.ones_like(whole_a)
+    shift = 1
+    while shift < span_len:
+        pairs = [(k + shift, k) for k in range(span_len - shift)]
+        message = jnp.concatenate(
+            [whole_b, jnp.broadcast_to(whole_a[:, None, None], (head_count, 1, N))], axis=1
+        )
+        got = lax.ppermute(message, "seq", pairs)
+        valid = seq_index + shift < span_len
+        got_b = jnp.where(valid, got[:, :P_SIZE], 0.0)
+        got_a = jnp.where(valid, got[:, P_SIZE, 0], 1.0)
+        later_b = later_b + later_a[:, None, None] * got_b
+        later_a = later_a * got_a
+        if shift * 2 < span_len:
+            whole_b = whole_b + whole_a[:, None, None] * got_b
+            whole_a = whole_a * got_a
+        shift *= 2
+    incoming = later_b + later_a[:, None, None] * my_heads
     local_part = group_output(prompt_keys, prompt_queries, prompt_parts)
     carry_term = jnp.einsum(
         "hpn,tn->thp",

time: 235 us -> 241 us (1.026)
  the two profiles are of different devices: /device:TPU:1 before, /device:TPU:14 now
where the time goes in v1:
time: 241 us; the launch traced here: 237 us
  waiting for transfers between devices  126 us (52%)
  local copies, waits for them, and re-layouts  36.5 us (15%)
  other arithmetic  26.3 us (11%)
  matrix products  23.4 us (10%)
  between operations  14.6 us (6%)
  starting transfers between devices  10.6 us (4%)
    psum x1, waiting for transfers between devices, on_device(): my_heads = lax.psum(jnp.where(owned, slots, 0.0), 'seq')  101 us
    ppermute x5, waiting for transfers between devices, on_device(): got = lax.ppermute(message, 'seq', pairs)  22.4 us
    unnamed x57, local copies, waits for them, and re-layouts  17.3 us
    ppermute x5, starting transfers between devices, on_device(): got = lax.ppermute(message, 'seq', pairs)  10.5 us
    dot_general x2, matrix products, group_output(): jnp.einsum('chst,cshp->cthp', mixing, grad_group, preferred_element_type=...  7.47 us
    dot_general x2, matrix products, group_parts(): jnp.einsum('hcd,dhpn->chpn', coef, states, precision=lax.Precision.HIGHEST)  5.81 us
  transfers between devices with their start and end apart: 7, of which 5 were waited for; matrix products, arithmetic and copies ran while one was open for 27% of the time, Pallas kernels for 0%

profile of v1, /device:TPU:14, one launch (start us, length us, event | category | flops | bytes accessed | tf_op | source)
XLA Modules:
  0.0 237.0 jit_solution(917676850013422105)
XLA Ops:
  8.2 2.3 reduce-window.14
  17.5 3.8 %convolution_bitcast_fusion = f32[5,8,64,128]{3,0,2,1:T(8,128)} fusion(f32[8,5,4,1]{1,2,3,0:T(4,128)S(1)} %copy.138, f32[4,8,64,128]{3,2,1,0:T(8,128)S(1)} %fusion.28), kind=kOutput, calls=%fused_computation.29 | convolution fusion | flops 15728640 | bytes 2359936 | tf_op jit(solution)/shard_map/hcd,dhpn->chpn/dot_general | solution.py:46
  21.4 1.8 slice.133
  24.0 2.2 collective-permute-start
  26.3 2.4 copy.120
  30.0 1.3 reduce-window.16
  31.8 1.3 fusion.96
  33.2 2.3 fusion.20
  35.5 2.7 %slice.252 = bf16[4,8,64,128]{3,0,2,1:T(4,128)(2,1)} slice(f32[5,8,64,128]{3,0,2,1:T(8,128)} %convolution_bitcast_fusion), slice={[1:5], [0:8], [0:64], [0:128]} | slice | bytes 1048576 | tf_op jit(solution)/shard_map/slice | solution.py:50
  44.8 2.4 %copy.156 = bf16[16,8,16,256]{3,2,1,0:T(8,128)(2,1)} copy(bf16[16,8,16,256]{3,1,2,0:T(8,128)(2,1)} %bitcast.176) | data formatting | bytes 2097152
  49.6 2.7 %and_and_fusion = pred[16,256,256]{2,1,0:T(8,128)(4,1)S(1)} fusion(s32[16,256]{1,0:T(8,128)S(1)} %eq.84, pred[16,256]{1,0:T(8,128)(4,1)S(1)} %and.103, pred[256,256]{1,0:T(8,128)(4,1)} %iota_compare_fusion.1), kind=kLoop, calls=%fused_computation.15 | loop fusion | flops 3145728 | bytes 1134592 | tf_op jit(solution)/shard_map/and | solution.py:75
  53.9 1.5 fusion.33
  56.8 3.6 %fusion.18 = f32[4,256,8,64]{1,3,2,0:T(8,128)} fusion(f32[4,8,64,256]{3,2,1,0:T(8,128)S(1)} %fusion.33, f32[4,8,256]{2,1,0:T(8,128)S(1)} %copy-done.20, f32[4,256,256]{2,1,0:T(8,128)S(1)} %fusion.97, pred[256,256]{1,0:T(8,128)(4,1)S(1)} %copy-done.17, bf16[4,256,8,64]{1,0,3,2:T(4,128)(2,1)S(1)} %reshape.320, f32[4,256,8]{1,2,0:T(8,128)S(1)} %copy-done.18), kind=kOutput, calls=%fused_computation.26 | convolution fusion | flops 277872640 | bytes 6422528 | tf_op jit(solution)/shard_map/chst,cshp->cthp/dot_general | solution.py:82
  60.4 3.8 %fusion.3 = f32[16,2,256,64]{2,3,1,0:T(8,128)} fusion(f32[16,2,256]{2,1,0:T(2,128)S(1)} %bitcast.201, f32[16,256,256]{2,1,0:T(8,128)S(1)} %fusion.98, pred[16,256,256]{2,1,0:T(8,128)(4,1)S(1)} %and_and_fusion, bf16[16,256,2,64]{1,0,3,2:T(8,128)(2,1)S(1)} %bitcast.177), kind=kOutput, calls=%fused_computation.5 | convolution fusion | flops 276824064 | bytes 8421376 | tf_op jit(solution)/shard_map/chst,cshp->cthp/dot_general | solution.py:82
  66.5 2.7 %collective-permute-start.1 = (f32[8,65,128]{2,1,0:T(8,128)S(1)}, f32[8,65,128]{2,1,0:T(8,128)S(1)}, u32[]{:S(2)}, u32[]{:S(2)}) collective-permute-start(f32[8,65,128]{2,1,0:T(8,128)S(1)} %pad_maximum_fusion.1), channel_id=1, source_target_pairs={{16,0},{24,8},{32,16},{40,24},{48,32},{56,40},{64,48},{72,56},{80,... | collective-permute-start | bytes 798728 | tf_op jit(solution)/shard_map/ppermute | solution.py:166
  69.7 9.9 %collective-permute-done.1 = f32[8,65,128]{2,1,0:T(8,128)S(1)} collective-permute-done((f32[8,65,128]{2,1,0:T(8,128)S(1)}, f32[8,65,128]{2,1,0:T(8,128)S(1)}, u32[]{:S(2)}, u32[]{:S(2)}) %collective-permute-start.1) | collective-permute-done | bytes 266272 | tf_op jit(solution)/shard_map/ppermute | solution.py:166
  81.5 2.0 collective-permute-start.2
  83.5 2.0 fusion.19
  86.5 8.0 %collective-permute-done.2 = f32[8,65,128]{2,1,0:T(8,128)} collective-permute-done((f32[8,65,128]{2,1,0:T(8,128)}, f32[8,65,128]{2,1,0:T(8,128)}, u32[]{:S(2)}, u32[]{:S(2)}) %collective-permute-start.2) | collective-permute-done | bytes 266272 | tf_op jit(solution)/shard_map/ppermute | solution.py:166
  96.6 2.4 collective-permute-start.3
  99.0 2.5 %fusion.16 = bf16[16,256,2,64]{1,3,2,0:T(8,128)(2,1)} fusion(f32[16,2,256,64]{2,3,1,0:T(8,128)S(1)} %copy-done.6, bf16[16,256,128,1]{2,1,3,0:T(8,128)(2,1)S(1)} %bitcast.170, f32[16,256,2]{1,2,0:T(2,128)S(1)} %get-tuple-element.33, bf16[16,2,64,128]{3,0,2,1:T(8,128)(2,1)} %slice.153), kind=kOutput, calls=%fused_computation.21 | convolution fusion | flops 135790592 | bytes 4751360 | tf_op jit(solution)/shard_map/chpn,ctn->cthp/dot_general | solution.py:85
  101.5 4.5 %collective-permute-done.3 = f32[8,65,128]{2,1,0:T(8,128)S(1)} collective-permute-done((f32[8,65,128]{2,1,0:T(8,128)S(1)}, f32[8,65,128]{2,1,0:T(8,128)S(1)}, u32[]{:S(2)}, u32[]{:S(2)}) %collective-permute-start.3) | collective-permute-done | bytes 266272 | tf_op jit(solution)/shard_map/ppermute | solution.py:166
  107.0 1.3 collective-permute-start.4
  108.3 2.6 %all-reduce.3.cloned.1.call-done = f32[2,64,128]{2,1,0:T(8,128)} async-done(((f32[2,64,128]{2,1,0:T(8,128)}), f32[2,64,128]{2,1,0:T(8,128)}) %all-reduce.3.cloned.1.call-update) | async-done | bytes 65552 | tf_op jit(solution)/shard_map/psum | solution.py:135
  111.8 2.9 %copy.117 = f32[4,256,8,64]{1,0,3,2:T(4,128)S(1)} copy(f32[4,256,8,64]{1,3,2,0:T(8,128)} %fusion.18) | data formatting | bytes 4194304 | tf_op jit(solution)/shard_map/add | solution.py:96
  114.8 1.8 copy.152
  116.6 4.5 %copy.149 = bf16[16,256,2,64]{3,2,1,0:T(2,128)(2,1)S(1)} copy(bf16[16,256,2,64]{1,3,2,0:T(8,128)(2,1)} %fusion.16) | data formatting | bytes 2097152
  121.2 1.8 reshape.341
  124.0 100.5 %all-reduce.5.cloned.1.call-done = f32[8,64,128]{2,1,0:T(8,128)} async-done(((f32[8,64,128]{2,1,0:T(8,128)}), f32[8,64,128]{2,1,0:T(8,128)}) %all-reduce.5.cloned.1.call-update) | async-done | bytes 262160 | tf_op jit(solution)/shard_map/psum | solution.py:154
  224.5 1.8 bitcast_multiply_fusion.1
  226.4 1.4 fusion.17
  227.9 2.3 copy.135
  (145 shorter events, 33.4 us)
Async XLA Ops:
  7.2 48.6 %copy-start = (bf16[4096,128]{1,0:T(8,128)(2,1)S(1)}, bf16[4096,128]{1,0:T(8,128)(2,1)}, u32[]{:S(2)}) copy-start(bf16[4096,128]{1,0:T(8,128)(2,1)} %param.14) | copy-start | bytes 3145732
  7.2 6.7 %copy-start.7 = (bf16[1024,512]{1,0:T(8,128)(2,1)S(1)}, bf16[1024,512]{1,0:T(8,128)(2,1)}, u32[]{:S(2)}) copy-start(bf16[1024,512]{1,0:T(8,128)(2,1)} %param.9) | copy-start | bytes 3145732
  7.2 103.8 %all-reduce.3.cloned.1.call-start = ((), (), s32[]{:S(2)}) async-start(), calls=%async_computation | async-start | bytes 131072 | tf_op jit(solution)/shard_map/psum | solution.py:135
  10.9 5.0 %copy-start.15 = (f32[1,8,8,128]{3,2,1,0:T(8,128)}, f32[1,8,8,128]{3,2,1,0:T(8,128)S(1)}, u32[]{:S(2)}) copy-start(f32[1,8,8,128]{3,2,1,0:T(8,128)S(1)} %fusion.109) | copy-start | bytes 98308
  14.4 2.7 %copy-start.8 = (bf16[1024,128]{1,0:T(8,128)(2,1)S(1)}, bf16[1024,128]{1,0:T(8,128)(2,1)}, u32[]{:S(2)}) copy-start(bf16[1024,128]{1,0:T(8,128)(2,1)} %param.11) | copy-start | bytes 786436
  17.5 8.6 %copy-start.13 = (s32[4096]{0:T(1024)S(1)}, s32[4096]{0:T(1024)}, u32[]{:S(2)}) copy-start(s32[4096]{0:T(1024)} %param.17) | copy-start | bytes 49156
  21.4 8.0 %copy-start.14 = (f32[2,4096]{1,0:T(2,128)S(1)}, f32[2,4096]{1,0:T(2,128)}, u32[]{:S(2)}) copy-start(f32[2,4096]{1,0:T(2,128)} %param.16) | copy-start | bytes 98308
  24.0 40.5 %collective-permute-start = (f32[8,65,128]{2,1,0:T(8,128)}, f32[8,65,128]{2,1,0:T(8,128)}, u32[]{:S(2)}, u32[]{:S(2)}) collective-permute-start(f32[8,65,128]{2,1,0:T(8,128)} %pad_maximum_fusion), channel_id=1, source_target_pairs={{8,0},{16,8},{24,16},{32,24},{40,32},{48,40},{56,48},{64,56},{72,6... | collective-permute-start | bytes 798728 | tf_op jit(solution)/shard_map/ppermute | solution.py:166
  26.3 6.9 %copy-start.2 = (bf16[4096,128]{1,0:T(8,128)(2,1)S(1)}, bf16[4096,128]{1,0:T(8,128)(2,1)}, u32[]{:S(2)}) copy-start(bf16[4096,128]{1,0:T(8,128)(2,1)} %param.15) | copy-start | bytes 3145732
  35.5 189.1 %all-reduce.5.cloned.1.call-start = ((), (), s32[]{:S(2)}) async-start(), calls=%async_computation.1 | async-start | bytes 524288 | tf_op jit(solution)/shard_map/psum | solution.py:154
  41.0 11.3 %copy-start.21 = (f32[15]{0:T(128)}, f32[15]{0:T(128)S(1)}, u32[]{:S(2)}) copy-start(f32[15]{0:T(128)S(1)} %convert_reduce_fusion) | copy-start | bytes 184
  49.6 5.8 %copy-start.4 = (bf16[1024,128]{1,0:T(8,128)(2,1)S(1)}, bf16[1024,128]{1,0:T(8,128)(2,1)}, u32[]{:S(2)}) copy-start(bf16[1024,128]{1,0:T(8,128)(2,1)} %param.10) | copy-start | bytes 786436
  49.6 5.8 %copy-start.9 = (bf16[1024,128]{1,0:T(8,128)(2,1)S(1)}, bf16[1024,128]{1,0:T(8,128)(2,1)}, u32[]{:S(2)}) copy-start(bf16[1024,128]{1,0:T(8,128)(2,1)} %param.11) | copy-start | bytes 786436
  55.7 1.0 copy-start.17
  55.7 1.0 copy-start.18
  55.7 1.0 copy-start.20
  56.7 3.7 %copy-start.3 = (bf16[16,8,16,256]{3,2,1,0:T(8,128)(2,1)S(1)}, bf16[16,8,16,256]{3,2,1,0:T(8,128)(2,1)}, u32[]{:S(2)}) copy-start(bf16[16,8,16,256]{3,2,1,0:T(8,128)(2,1)} %copy.156) | copy-start | bytes 3145732
  56.8 3.7 %copy-start.19 = (f32[2,16,256]{2,0,1:T(2,128)S(1)}, f32[2,16,256]{2,0,1:T(2,128)}, u32[]{:S(2)}) copy-start(f32[2,16,256]{2,0,1:T(2,128)} %copy.189) | copy-start | bytes 98308
  64.2 1.1 copy-start.22
  66.5 13.2 %collective-permute-start.1 = (f32[8,65,128]{2,1,0:T(8,128)S(1)}, f32[8,65,128]{2,1,0:T(8,128)S(1)}, u32[]{:S(2)}, u32[]{:S(2)}) collective-permute-start(f32[8,65,128]{2,1,0:T(8,128)S(1)} %pad_maximum_fusion.1), channel_id=1, source_target_pairs={{16,0},{24,8},{32,16},{40,24},{48,32},{56,40},{64,48},{72,56},{80,... | collective-permute-start | bytes 798728 | tf_op jit(solution)/shard_map/ppermute | solution.py:166
  79.7 5.9 %copy-start.11 = (f32[8,65,128]{2,1,0:T(8,128)}, f32[8,65,128]{2,1,0:T(8,128)S(1)}, u32[]{:S(2)}) copy-start(f32[8,65,128]{2,1,0:T(8,128)S(1)} %collective-permute-done.1) | copy-start | bytes 798724
  81.5 17.5 %copy-start.6 = (f32[16,2,256,64]{2,3,1,0:T(8,128)S(1)}, f32[16,2,256,64]{2,3,1,0:T(8,128)}, u32[]{:S(2)}) copy-start(f32[16,2,256,64]{2,3,1,0:T(8,128)} %fusion.3) | copy-start | bytes 6291460
  81.5 13.0 %collective-permute-start.2 = (f32[8,65,128]{2,1,0:T(8,128)}, f32[8,65,128]{2,1,0:T(8,128)}, u32[]{:S(2)}, u32[]{:S(2)}) collective-permute-start(f32[8,65,128]{2,1,0:T(8,128)} %pad_maximum_fusion.2), channel_id=1, source_target_pairs={{32,0},{40,8},{48,16},{56,24},{64,32},{72,40},{80,48},{88,56},{96,... | collective-permute-start | bytes 798728 | tf_op jit(solution)/shard_map/ppermute | solution.py:166
  96.6 9.3 %collective-permute-start.3 = (f32[8,65,128]{2,1,0:T(8,128)S(1)}, f32[8,65,128]{2,1,0:T(8,128)S(1)}, u32[]{:S(2)}, u32[]{:S(2)}) collective-permute-start(f32[8,65,128]{2,1,0:T(8,128)S(1)} %pad_maximum_fusion.3), channel_id=1, source_target_pairs={{64,0},{72,8},{80,16},{88,24},{96,32},{104,40},{112,48},{120,56},{... | collective-permute-start | bytes 798728 | tf_op jit(solution)/shard_map/ppermute | solution.py:166
  99.0 12.7 %copy-start.16 = (f32[1,8,8,128]{3,2,1,0:T(8,128)S(1)}, f32[1,8,8,128]{3,2,1,0:T(8,128)}, u32[]{:S(2)}) copy-start(f32[1,8,8,128]{3,2,1,0:T(8,128)} %copy-done.15) | copy-start | bytes 98308
  106.0 1.1 copy-start.12
  107.0 15.9 %collective-permute-start.4 = (f32[8,65,128]{2,1,0:T(8,128)}, f32[8,65,128]{2,1,0:T(8,128)}, u32[]{:S(2)}, u32[]{:S(2)}) collective-permute-start(f32[8,65,128]{2,1,0:T(8,128)} %pad_maximum_fusion.4), channel_id=1, source_target_pairs={{128,0},{136,8},{144,16},{152,24},{160,32},{168,40},{176,48},{184,... | collective-permute-start | bytes 798728 | tf_op jit(solution)/shard_map/ppermute | solution.py:166
  111.0 0.7 copy-start.10
  121.1 103.4 %copy-start.5 = (bf16[1024,128]{1,0:T(8,128)(2,1)S(1)}, bf16[1024,128]{1,0:T(8,128)(2,1)}, u32[]{:S(2)}) copy-start(bf16[1024,128]{1,0:T(8,128)(2,1)} %param.10) | copy-start | bytes 786436
  122.9 103.5 %copy-start.1 = (f32[64,8,4,256]{3,1,2,0:T(8,128)S(1)}, f32[64,8,4,256]{3,1,2,0:T(8,128)}, u32[]{:S(2)}) copy-start(f32[64,8,4,256]{3,1,2,0:T(8,128)} %copy.152) | copy-start | bytes 6291460
Sparse Core Ops, SparseCore 0:
  35.6 75.3 all-reduce.2
  114.2 110.3 all-reduce.4

commit v2 on v1

--- a/solution.py
+++ b/solution.py
@@ -132,7 +132,14 @@
     partial_state = initial_state(
         resp_grad, resp_queries, resp_decay, resp_segment, resp_alive, resp_parts[0]
     )
-    summed_state = lax.psum(partial_state, "resp")
+    resp_len = lax.axis_size("resp")
+    shift = 1
+    summed_state = partial_state
+    while shift < resp_len:
+        summed_state = summed_state + lax.ppermute(
+            summed_state, "resp", [(k, k ^ shift) for k in range(resp_len)]
+        )
+        shift *= 2
     head_count = prompt_decay.shape[0]
     prompt_len = prompt_grad.shape[0]
     zero_label = jnp.zeros((prompt_len,), jnp.int32)
@@ -142,16 +149,20 @@
     start_grad = prompt_parts[7]
     shard_total = cum_sums[:, -1]
     seq_index = lax.axis_index("seq")
-    resp_index = lax.axis_index("resp")
-    first_head = seq_index * summed_state.shape[0]
-    owned = first_head // head_count == resp_index
-    slots = lax.dynamic_update_slice_in_dim(
-        jnp.zeros((head_count,) + summed_state.shape[1:], jnp.float32),
-        summed_state,
-        first_head % head_count,
-        0,
-    )
-    my_heads = lax.psum(jnp.where(owned, slots, 0.0), "seq")
+    seq_len = lax.axis_size("seq")
+    share = head_count // summed_state.shape[0]
+    pieces = []
+    for turn in range(share):
+        pairs = []
+        for src_seq in range(seq_len):
+            for src_resp in range(resp_len):
+                dst_seq = share * src_resp + (src_seq % share + turn) % share
+                dst_resp = src_seq // share
+                pairs.append((src_seq * resp_len + src_resp, dst_seq * resp_len + dst_resp))
+        pieces.append(lax.ppermute(summed_state, ("seq", "resp"), pairs))
+    pieces = jnp.stack(pieces)
+    order = (seq_index % share - jnp.arange(share)) % share
+    my_heads = jnp.take(pieces, order, axis=0).reshape((head_count,) + summed_state.shape[1:])
     span_len = lax.axis_size("seq")
     whole_b = start_grad
     whole_a = jnp.exp(shard_total)

time: 241 us -> 155 us (0.64)
  the two profiles are of different devices: /device:TPU:14 before, /device:TPU:31 now
where the time goes in v2:
time: 155 us; the launch traced here: 153 us
  starting transfers between devices  45 us (29%)
  local copies, waits for them, and re-layouts  32.6 us (21%)
  other arithmetic  29.4 us (19%)
  waiting for transfers between devices  25.4 us (16%)
  matrix products  19.5 us (13%)
    ppermute x5, starting transfers between devices, on_device(): got = lax.ppermute(message, 'seq', pairs)  20.5 us
    ppermute x4, waiting for transfers between devices, on_device(): pieces.append(lax.ppermute(summed_state, ('seq', 'resp'), pairs))  16.1 us
    unnamed x59, local copies, waits for them, and re-layouts  16.1 us
    ppermute x4, starting transfers between devices, on_device(): pieces.append(lax.ppermute(summed_state, ('seq', 'resp'), pairs))  14.3 us
    ppermute x3, starting transfers between devices, on_device(): lax.ppermute(summed_state, 'resp', [(k, k ^ shift) for k in range(resp_le...  10.2 us
    ppermute x5, waiting for transfers between devices, on_device(): got = lax.ppermute(message, 'seq', pairs)  7.59 us
    dot_general x2, matrix products, group_output(): jnp.einsum('chst,cshp->cthp', mixing, grad_group, preferred_element_type=...  7.42 us
    another operation x6, other arithmetic  4.68 us
  transfers between devices with their start and end apart: 12, of which 7 were waited for; matrix products, arithmetic and copies ran while one was open for 41% of the time, Pallas kernels for 0%

profile of v2, /device:TPU:31, one launch (start us, length us, event | category | flops | bytes accessed | tf_op | source)
XLA Modules:
  0.0 153.3 jit_solution(4351921963364014326)
XLA Ops:
  1.6 2.3 %reduce-window.14 = f32[8,8,128]{2,1,0:T(8,128)S(1)} reduce-window(f32[8,8,128]{2,1,0:T(8,128)S(1)} %copy.104, f32[]{:T(128)} %constant.35.clone.1), window={size=1x1x128 pad=0_0x0_0x127_0}, to_apply=%region_0.0 | reduce-window | flops 1040384 | bytes 65540 | tf_op jit(solution)/shard_map/reduce-window
  11.0 2.5 %convolution_bitcast_fusion = f32[5,8,64,128]{3,0,2,1:T(8,128)S(1)} fusion(f32[8,5,4,1]{1,2,3,0:T(4,128)S(1)} %copy.138, f32[4,8,64,128]{3,2,1,0:T(8,128)S(1)} %fusion.28), kind=kOutput, calls=%fused_computation.30 | convolution fusion | flops 15728640 | bytes 2359936 | tf_op jit(solution)/shard_map/hcd,dhpn->chpn/dot_general | solution.py:46
  14.8 3.3 %collective-permute-start = (f32[8,65,128]{2,1,0:T(8,128)}, f32[8,65,128]{2,1,0:T(8,128)}, u32[]{:S(2)}, u32[]{:S(2)}) collective-permute-start(f32[8,65,128]{2,1,0:T(8,128)} %pad_maximum_fusion), channel_id=1, source_target_pairs={{8,0},{16,8},{24,16},{32,24},{40,32},{48,40},{56,48},{64,56},{72,6... | collective-permute-start | bytes 798728 | tf_op jit(solution)/shard_map/ppermute | solution.py:177
  18.2 2.4 %copy.120 = bf16[4096,128]{0,1:T(8,128)(2,1)} copy(bf16[4096,128]{1,0:T(8,128)(2,1)} %param.13) | data formatting | bytes 2097152 | tf_op args[4]
  25.1 2.3 %fusion.20 = f32[2,64,128]{2,1,0:T(8,128)} fusion(bf16[4096,2,64]{0,2,1:T(8,128)(2,1)} %bitcast.188, bf16[4096,128]{1,0:T(8,128)(2,1)S(1)} %copy-done.2, f32[4096,2]{0,1:T(2,128)S(1)} %fusion.47), kind=kOutput, calls=%fused_computation.33 | convolution fusion | flops 135790592 | bytes 2195456 | tf_op jit(solution)/shard_map/thp,tn->hpn/dot_general | solution.py:115
  27.3 1.6 %collective-permute-start.5 = (f32[2,64,128]{2,1,0:T(8,128)}, f32[2,64,128]{2,1,0:T(8,128)}, u32[]{:S(2)}, u32[]{:S(2)}) collective-permute-start(f32[2,64,128]{2,1,0:T(8,128)} %fusion.20), channel_id=1, source_target_pairs={{0,1},{1,0},{2,3},{3,2},{4,5},{5,4},{6,7},{7,6},{8,9},{9,8},{10,11... | collective-permute-start | bytes 196616 | tf_op jit(solution)/shard_map/ppermute | solution.py:139
  29.0 2.7 %slice.249 = bf16[4,8,64,128]{3,0,2,1:T(4,128)(2,1)} slice(f32[5,8,64,128]{3,0,2,1:T(8,128)} %copy-done.4), slice={[1:5], [0:8], [0:64], [0:128]} | slice | bytes 1048576 | tf_op jit(solution)/shard_map/slice | solution.py:50
  38.2 2.4 %copy.156 = bf16[16,8,16,256]{3,2,1,0:T(8,128)(2,1)} copy(bf16[16,8,16,256]{3,1,2,0:T(8,128)(2,1)} %bitcast.189) | data formatting | bytes 2097152
  43.1 2.7 %and_and_fusion = pred[16,256,256]{2,1,0:T(8,128)(4,1)S(1)} fusion(s32[16,256]{1,0:T(8,128)S(1)} %eq.82, pred[16,256]{1,0:T(8,128)(4,1)S(1)} %and.129, pred[256,256]{1,0:T(8,128)(4,1)} %iota_compare_fusion.1), kind=kLoop, calls=%fused_computation.16 | loop fusion | flops 3145728 | bytes 1134592 | tf_op jit(solution)/shard_map/and | solution.py:75
  46.7 1.5 %fusion.33 = f32[4,8,64,256]{3,2,1,0:T(8,128)S(1)} fusion(bf16[4,256,128,1]{2,1,3,0:T(8,128)(2,1)} %bitcast.194, bf16[4,8,64,128]{3,0,2,1:T(4,128)(2,1)} %slice.249), kind=kOutput, calls=%fused_computation.46 | convolution fusion | flops 134217728 | bytes 2883584 | tf_op jit(solution)/shard_map/chpn,ctn->cthp/dot_general | solution.py:85
  50.3 3.8 %fusion.3 = f32[16,2,256,64]{2,3,1,0:T(8,128)S(1)} fusion(f32[16,2,256]{2,1,0:T(2,128)S(1)} %bitcast.218, f32[16,256,256]{2,1,0:T(8,128)S(1)} %fusion.89, pred[16,256,256]{2,1,0:T(8,128)(4,1)S(1)} %and_and_fusion, bf16[16,256,2,64]{1,0,3,2:T(8,128)(2,1)S(1)} %bitcast.191), kind=kOutput, calls=%fused_computation.6 | convolution fusion | flops 276824064 | bytes 8421376 | tf_op jit(solution)/shard_map/chst,cshp->cthp/dot_general | solution.py:82
  54.1 3.6 %fusion.18 = f32[4,256,8,64]{1,3,2,0:T(8,128)} fusion(f32[4,8,64,256]{3,2,1,0:T(8,128)S(1)} %fusion.33, f32[4,8,256]{2,1,0:T(8,128)S(1)} %copy-done.20, f32[4,256,256]{2,1,0:T(8,128)S(1)} %fusion.88, pred[256,256]{1,0:T(8,128)(4,1)S(1)} %copy-done.18, bf16[4,256,8,64]{1,0,3,2:T(4,128)(2,1)S(1)} %reshape.377, f32[4,256,8]{1,2,0:T(8,128)S(1)} %copy-done.19), kind=kOutput, calls=%fused_computation.27 | convolution fusion | flops 277872640 | bytes 6422528 | tf_op jit(solution)/shard_map/chst,cshp->cthp/dot_general | solution.py:82
  60.3 1.8 %collective-permute-start.1 = (f32[8,65,128]{2,1,0:T(8,128)S(1)}, f32[8,65,128]{2,1,0:T(8,128)S(1)}, u32[]{:S(2)}, u32[]{:S(2)}) collective-permute-start(f32[8,65,128]{2,1,0:T(8,128)S(1)} %pad_maximum_fusion.1), channel_id=1, source_target_pairs={{16,0},{24,8},{32,16},{40,24},{48,32},{56,40},{64,48},{72,56},{80,... | collective-permute-start | bytes 798728 | tf_op jit(solution)/shard_map/ppermute | solution.py:177
  62.1 2.0 %fusion.19 = bf16[17,2,64,128]{3,0,2,1:T(8,128)(2,1)S(1)} fusion(f32[16,2,64,128]{3,2,1,0:T(8,128)S(1)} %fusion.24, f32[2,17,16]{1,2,0:T(8,128)S(1)} %select_reduce_fusion.1, f32[17]{0:T(128)S(1)} %pad_maximum_fusion.7, pred[17,16]{0,1:T(8,128)(4,1)S(1)} %iota_compare_fusion.3), kind=kOutput, calls=%fused_computation.32 | convolution fusion | flops 53756992 | bytes 1608148 | tf_op jit(solution)/shard_map/hcd,dhpn->chpn/dot_general | solution.py:46
  64.3 3.8 %collective-permute-done.1 = f32[8,65,128]{2,1,0:T(8,128)S(1)} collective-permute-done((f32[8,65,128]{2,1,0:T(8,128)S(1)}, f32[8,65,128]{2,1,0:T(8,128)S(1)}, u32[]{:S(2)}, u32[]{:S(2)}) %collective-permute-start.1) | collective-permute-done | bytes 266272 | tf_op jit(solution)/shard_map/ppermute | solution.py:177
  69.3 4.7 %collective-permute-start.2 = (f32[8,65,128]{2,1,0:T(8,128)S(1)}, f32[8,65,128]{2,1,0:T(8,128)S(1)}, u32[]{:S(2)}, u32[]{:S(2)}) collective-permute-start(f32[8,65,128]{2,1,0:T(8,128)S(1)} %pad_maximum_fusion.2), channel_id=1, source_target_pairs={{32,0},{40,8},{48,16},{56,24},{64,32},{72,40},{80,48},{88,56},{96,... | collective-permute-start | bytes 798728 | tf_op jit(solution)/shard_map/ppermute | solution.py:177
  75.4 3.7 %collective-permute-done.2 = f32[8,65,128]{2,1,0:T(8,128)S(1)} collective-permute-done((f32[8,65,128]{2,1,0:T(8,128)S(1)}, f32[8,65,128]{2,1,0:T(8,128)S(1)}, u32[]{:S(2)}, u32[]{:S(2)}) %collective-permute-start.2) | collective-permute-done | bytes 266272 | tf_op jit(solution)/shard_map/ppermute | solution.py:177
  81.0 8.1 %collective-permute-start.3 = (f32[8,65,128]{2,1,0:T(8,128)}, f32[8,65,128]{2,1,0:T(8,128)}, u32[]{:S(2)}, u32[]{:S(2)}) collective-permute-start(f32[8,65,128]{2,1,0:T(8,128)} %pad_maximum_fusion.3), channel_id=1, source_target_pairs={{64,0},{72,8},{80,16},{88,24},{96,32},{104,40},{112,48},{120,56},{... | collective-permute-start | bytes 798728 | tf_op jit(solution)/shard_map/ppermute | solution.py:177
  90.2 3.1 %collective-permute-start.6 = (f32[2,64,128]{2,1,0:T(8,128)S(1)}, f32[2,64,128]{2,1,0:T(8,128)S(1)}, u32[]{:S(2)}, u32[]{:S(2)}) collective-permute-start(f32[2,64,128]{2,1,0:T(8,128)S(1)} %add.113), channel_id=1, source_target_pairs={{0,2},{1,3},{2,0},{3,1},{4,6},{5,7},{6,4},{7,5},{8,10},{9,11},{10,... | collective-permute-start | bytes 196616 | tf_op jit(solution)/shard_map/ppermute | solution.py:139
  93.9 1.8 %collective-permute-done.6 = f32[2,64,128]{2,1,0:T(8,128)S(1)} collective-permute-done((f32[2,64,128]{2,1,0:T(8,128)S(1)}, f32[2,64,128]{2,1,0:T(8,128)S(1)}, u32[]{:S(2)}, u32[]{:S(2)}) %collective-permute-start.6) | collective-permute-done | bytes 65568 | tf_op jit(solution)/shard_map/ppermute | solution.py:139
  95.6 5.5 %collective-permute-start.7 = (f32[2,64,128]{2,1,0:T(8,128)S(1)}, f32[2,64,128]{2,1,0:T(8,128)}, u32[]{:S(2)}, u32[]{:S(2)}) collective-permute-start(f32[2,64,128]{2,1,0:T(8,128)S(1)} %add.114), channel_id=1, source_target_pairs={{0,4},{1,5},{2,6},{3,7},{4,0},{5,1},{6,2},{7,3},{8,12},{9,13},{10,... | collective-permute-start | bytes 196616 | tf_op jit(solution)/shard_map/ppermute | solution.py:139
  103.9 2.6 %collective-permute-start.4 = (f32[8,65,128]{2,1,0:T(8,128)}, f32[8,65,128]{2,1,0:T(8,128)}, u32[]{:S(2)}, u32[]{:S(2)}) collective-permute-start(f32[8,65,128]{2,1,0:T(8,128)} %pad_maximum_fusion.4), channel_id=1, source_target_pairs={{128,0},{136,8},{144,16},{152,24},{160,32},{168,40},{176,48},{184,... | collective-permute-start | bytes 798728 | tf_op jit(solution)/shard_map/ppermute | solution.py:177
  107.8 1.8 %copy.152 = f32[64,8,4,256]{3,1,2,0:T(8,128)} copy(f32[64,8,4,256]{3,2,1,0:T(4,128)S(1)} %bitcast.185) | data formatting | bytes 4194304
  110.2 4.5 %copy.149 = bf16[16,256,2,64]{3,2,1,0:T(2,128)(2,1)S(1)} copy(bf16[16,256,2,64]{1,3,2,0:T(8,128)(2,1)} %fusion.16) | data formatting | bytes 2097152
  114.8 1.8 %reshape.406 = bf16[4096,128]{1,0:T(8,128)(2,1)} reshape(bf16[16,256,2,64]{3,2,1,0:T(2,128)(2,1)S(1)} %copy.149) | data formatting | bytes 2097152
  117.8 9.4 %collective-permute-start.10 = (f32[2,64,128]{2,1,0:T(8,128)S(1)}, f32[2,64,128]{2,1,0:T(8,128)S(1)}, u32[]{:S(2)}, u32[]{:S(2)}) collective-permute-start(f32[2,64,128]{2,1,0:T(8,128)S(1)} %add.115), channel_id=1, source_target_pairs={{0,16},{1,48},{2,80},{3,112},{4,144},{5,176},{6,208},{7,240},{8,24... | collective-permute-start | bytes 196616 | tf_op jit(solution)/shard_map/ppermute | solution.py:162
  127.2 2.7 %collective-permute-start.9 = (f32[2,64,128]{2,1,0:T(8,128)S(1)}, f32[2,64,128]{2,1,0:T(8,128)S(1)}, u32[]{:S(2)}, u32[]{:S(2)}) collective-permute-start(f32[2,64,128]{2,1,0:T(8,128)S(1)} %add.115), channel_id=1, source_target_pairs={{0,8},{1,40},{2,72},{3,104},{4,136},{5,168},{6,200},{7,232},{8,16}... | collective-permute-start | bytes 196616 | tf_op jit(solution)/shard_map/ppermute | solution.py:162
  129.9 1.9 %collective-permute-start.8 = (f32[2,64,128]{2,1,0:T(8,128)S(1)}, f32[2,64,128]{2,1,0:T(8,128)S(1)}, u32[]{:S(2)}, u32[]{:S(2)}) collective-permute-start(f32[2,64,128]{2,1,0:T(8,128)S(1)} %add.115), channel_id=1, source_target_pairs={{0,0},{1,32},{2,64},{3,96},{4,128},{5,160},{6,192},{7,224},{8,8},{... | collective-permute-start | bytes 196616 | tf_op jit(solution)/shard_map/ppermute | solution.py:162
  131.8 11.2 %collective-permute-done.11 = f32[2,64,128]{2,1,0:T(8,128)S(1)} collective-permute-done((f32[2,64,128]{2,1,0:T(8,128)S(1)}, f32[2,64,128]{2,1,0:T(8,128)S(1)}, u32[]{:S(2)}, u32[]{:S(2)}) %collective-permute-start.11) | collective-permute-done | bytes 65568 | tf_op jit(solution)/shard_map/ppermute | solution.py:162
  143.0 2.7 %collective-permute-done.10 = f32[2,64,128]{2,1,0:T(8,128)S(1)} collective-permute-done((f32[2,64,128]{2,1,0:T(8,128)S(1)}, f32[2,64,128]{2,1,0:T(8,128)S(1)}, u32[]{:S(2)}, u32[]{:S(2)}) %collective-permute-start.10) | collective-permute-done | bytes 65568 | tf_op jit(solution)/shard_map/ppermute | solution.py:162
  145.9 2.0 %collective-permute-done.8 = f32[2,64,128]{2,1,0:T(8,128)S(1)} collective-permute-done((f32[2,64,128]{2,1,0:T(8,128)S(1)}, f32[2,64,128]{2,1,0:T(8,128)S(1)}, u32[]{:S(2)}, u32[]{:S(2)}) %collective-permute-start.8) | collective-permute-done | bytes 65568 | tf_op jit(solution)/shard_map/ppermute | solution.py:162
  149.5 1.6 %fusion.40 = bf16[8,64,128]{2,1,0:T(8,128)(2,1)S(1)} fusion(f32[8,65,128]{2,1,0:T(8,128)} %collective-permute-done.4, f32[4,2,64,128]{3,2,1,0:T(8,128)S(1)} %gather_fusion, f32[8,65,128]{2,1,0:T(8,128)} %collective-permute-done, f32[8,65,128]{2,1,0:T(8,128)S(1)} %copy-done.12, f32[8,65,128]{2,1,0:T(8,128)} %copy-done.13, ...), kind=kLoop, calls=%fused_computation.60 | loop fusion | flops 1114112 | bytes 1704109 | tf_op jit(solution)/shard_map/convert_element_type | solution.py:191
  (164 shorter events, 44.3 us)
Async XLA Ops:
  0.6 47.9 %copy-start = (bf16[4096,128]{1,0:T(8,128)(2,1)S(1)}, bf16[4096,128]{1,0:T(8,128)(2,1)}, u32[]{:S(2)}) copy-start(bf16[4096,128]{1,0:T(8,128)(2,1)} %param.14) | copy-start | bytes 3145732
  0.6 6.7 %copy-start.8 = (bf16[1024,512]{1,0:T(8,128)(2,1)S(1)}, bf16[1024,512]{1,0:T(8,128)(2,1)}, u32[]{:S(2)}) copy-start(bf16[1024,512]{1,0:T(8,128)(2,1)} %param.9) | copy-start | bytes 3145732
  4.3 5.0 %copy-start.16 = (f32[1,8,8,128]{3,2,1,0:T(8,128)}, f32[1,8,8,128]{3,2,1,0:T(8,128)S(1)}, u32[]{:S(2)}) copy-start(f32[1,8,8,128]{3,2,1,0:T(8,128)S(1)} %fusion.101) | copy-start | bytes 98308
  7.8 2.7 %copy-start.9 = (bf16[1024,128]{1,0:T(8,128)(2,1)S(1)}, bf16[1024,128]{1,0:T(8,128)(2,1)}, u32[]{:S(2)}) copy-start(bf16[1024,128]{1,0:T(8,128)(2,1)} %param.11) | copy-start | bytes 786436
  11.0 7.1 %copy-start.14 = (s32[4096]{0:T(1024)S(1)}, s32[4096]{0:T(1024)}, u32[]{:S(2)}) copy-start(s32[4096]{0:T(1024)} %param.17) | copy-start | bytes 49156
  13.5 4.6 %copy-start.4 = (f32[5,8,64,128]{3,0,2,1:T(8,128)}, f32[5,8,64,128]{3,0,2,1:T(8,128)S(1)}, u32[]{:S(2)}) copy-start(f32[5,8,64,128]{3,0,2,1:T(8,128)S(1)} %convolution_bitcast_fusion) | copy-start | bytes 3932164
  13.6 7.8 %copy-start.15 = (f32[2,4096]{1,0:T(2,128)S(1)}, f32[2,4096]{1,0:T(2,128)}, u32[]{:S(2)}) copy-start(f32[2,4096]{1,0:T(2,128)} %param.16) | copy-start | bytes 98308
  14.8 43.5 %collective-permute-start = (f32[8,65,128]{2,1,0:T(8,128)}, f32[8,65,128]{2,1,0:T(8,128)}, u32[]{:S(2)}, u32[]{:S(2)}) collective-permute-start(f32[8,65,128]{2,1,0:T(8,128)} %pad_maximum_fusion), channel_id=1, source_target_pairs={{8,0},{16,8},{24,16},{32,24},{40,32},{48,40},{56,48},{64,56},{72,6... | collective-permute-start | bytes 798728 | tf_op jit(solution)/shard_map/ppermute | solution.py:177
  18.2 6.9 %copy-start.2 = (bf16[4096,128]{1,0:T(8,128)(2,1)S(1)}, bf16[4096,128]{1,0:T(8,128)(2,1)}, u32[]{:S(2)}) copy-start(bf16[4096,128]{1,0:T(8,128)(2,1)} %param.15) | copy-start | bytes 3145732
  27.3 61.9 %collective-permute-start.5 = (f32[2,64,128]{2,1,0:T(8,128)}, f32[2,64,128]{2,1,0:T(8,128)}, u32[]{:S(2)}, u32[]{:S(2)}) collective-permute-start(f32[2,64,128]{2,1,0:T(8,128)} %fusion.20), channel_id=1, source_target_pairs={{0,1},{1,0},{2,3},{3,2},{4,5},{5,4},{6,7},{7,6},{8,9},{9,8},{10,11... | collective-permute-start | bytes 196616 | tf_op jit(solution)/shard_map/ppermute | solution.py:139
  43.1 5.1 %copy-start.5 = (bf16[1024,128]{1,0:T(8,128)(2,1)S(1)}, bf16[1024,128]{1,0:T(8,128)(2,1)}, u32[]{:S(2)}) copy-start(bf16[1024,128]{1,0:T(8,128)(2,1)} %param.10) | copy-start | bytes 786436
  43.1 5.1 %copy-start.10 = (bf16[1024,128]{1,0:T(8,128)(2,1)S(1)}, bf16[1024,128]{1,0:T(8,128)(2,1)}, u32[]{:S(2)}) copy-start(bf16[1024,128]{1,0:T(8,128)(2,1)} %param.11) | copy-start | bytes 786436
  50.2 3.8 %copy-start.18 = (pred[256,256]{1,0:T(8,128)(4,1)S(1)}, pred[256,256]{1,0:T(8,128)(4,1)}, u32[]{:S(2)}) copy-start(pred[256,256]{1,0:T(8,128)(4,1)} %iota_compare_fusion.1) | copy-start | bytes 196612
  50.3 3.8 %copy-start.19 = (f32[4,256,8]{1,2,0:T(8,128)S(1)}, f32[4,256,8]{1,2,0:T(8,128)}, u32[]{:S(2)}) copy-start(f32[4,256,8]{1,2,0:T(8,128)} %get-tuple-element.34) | copy-start | bytes 98308
  50.3 3.8 %copy-start.20 = (f32[4,8,256]{2,1,0:T(8,128)S(1)}, f32[4,8,256]{2,1,0:T(8,128)}, u32[]{:S(2)}) copy-start(f32[4,8,256]{2,1,0:T(8,128)} %copy.106) | copy-start | bytes 98308
  60.3 7.8 %collective-permute-start.1 = (f32[8,65,128]{2,1,0:T(8,128)S(1)}, f32[8,65,128]{2,1,0:T(8,128)S(1)}, u32[]{:S(2)}, u32[]{:S(2)}) collective-permute-start(f32[8,65,128]{2,1,0:T(8,128)S(1)} %pad_maximum_fusion.1), channel_id=1, source_target_pairs={{16,0},{24,8},{32,16},{40,24},{48,32},{56,40},{64,48},{72,56},{80,... | collective-permute-start | bytes 798728 | tf_op jit(solution)/shard_map/ppermute | solution.py:177
  68.2 11.0 %copy-start.11 = (f32[8,65,128]{2,1,0:T(8,128)}, f32[8,65,128]{2,1,0:T(8,128)S(1)}, u32[]{:S(2)}) copy-start(f32[8,65,128]{2,1,0:T(8,128)S(1)} %collective-permute-done.1) | copy-start | bytes 798724
  69.3 9.9 %collective-permute-start.2 = (f32[8,65,128]{2,1,0:T(8,128)S(1)}, f32[8,65,128]{2,1,0:T(8,128)S(1)}, u32[]{:S(2)}, u32[]{:S(2)}) collective-permute-start(f32[8,65,128]{2,1,0:T(8,128)S(1)} %pad_maximum_fusion.2), channel_id=1, source_target_pairs={{32,0},{40,8},{48,16},{56,24},{64,32},{72,40},{80,48},{88,56},{96,... | collective-permute-start | bytes 798728 | tf_op jit(solution)/shard_map/ppermute | solution.py:177
  74.0 15.2 %copy-start.17 = (f32[1,8,8,128]{3,2,1,0:T(8,128)S(1)}, f32[1,8,8,128]{3,2,1,0:T(8,128)}, u32[]{:S(2)}) copy-start(f32[1,8,8,128]{3,2,1,0:T(8,128)} %copy-done.16) | copy-start | bytes 98308
  75.4 31.1 %copy-start.7 = (f32[4,256,8,64]{1,3,2,0:T(8,128)S(1)}, f32[4,256,8,64]{1,3,2,0:T(8,128)}, u32[]{:S(2)}) copy-start(f32[4,256,8,64]{1,3,2,0:T(8,128)} %fusion.18) | copy-start | bytes 6291460
  81.0 20.1 %collective-permute-start.3 = (f32[8,65,128]{2,1,0:T(8,128)}, f32[8,65,128]{2,1,0:T(8,128)}, u32[]{:S(2)}, u32[]{:S(2)}) collective-permute-start(f32[8,65,128]{2,1,0:T(8,128)} %pad_maximum_fusion.3), channel_id=1, source_target_pairs={{64,0},{72,8},{80,16},{88,24},{96,32},{104,40},{112,48},{120,56},{... | collective-permute-start | bytes 798728 | tf_op jit(solution)/shard_map/ppermute | solution.py:177
  90.2 5.4 %collective-permute-start.6 = (f32[2,64,128]{2,1,0:T(8,128)S(1)}, f32[2,64,128]{2,1,0:T(8,128)S(1)}, u32[]{:S(2)}, u32[]{:S(2)}) collective-permute-start(f32[2,64,128]{2,1,0:T(8,128)S(1)} %add.113), channel_id=1, source_target_pairs={{0,2},{1,3},{2,0},{3,1},{4,6},{5,7},{6,4},{7,5},{8,10},{9,11},{10,... | collective-permute-start | bytes 196616 | tf_op jit(solution)/shard_map/ppermute | solution.py:139
  95.6 21.0 %collective-permute-start.7 = (f32[2,64,128]{2,1,0:T(8,128)S(1)}, f32[2,64,128]{2,1,0:T(8,128)}, u32[]{:S(2)}, u32[]{:S(2)}) collective-permute-start(f32[2,64,128]{2,1,0:T(8,128)S(1)} %add.114), channel_id=1, source_target_pairs={{0,4},{1,5},{2,6},{3,7},{4,0},{5,1},{6,2},{7,3},{8,12},{9,13},{10,... | collective-permute-start | bytes 196616 | tf_op jit(solution)/shard_map/ppermute | solution.py:139
  103.9 44.7 %collective-permute-start.4 = (f32[8,65,128]{2,1,0:T(8,128)}, f32[8,65,128]{2,1,0:T(8,128)}, u32[]{:S(2)}, u32[]{:S(2)}) collective-permute-start(f32[8,65,128]{2,1,0:T(8,128)} %pad_maximum_fusion.4), channel_id=1, source_target_pairs={{128,0},{136,8},{144,16},{152,24},{160,32},{168,40},{176,48},{184,... | collective-permute-start | bytes 798728 | tf_op jit(solution)/shard_map/ppermute | solution.py:177
  114.8 17.0 %copy-start.23 = (s32[4]{0:T(128)S(1)}, s32[4]{0:T(128)}, u32[]{:S(2)}) copy-start(s32[4]{0:T(128)} %fusion.66) | copy-start | bytes 52
  114.8 34.7 %copy-start.12 = (f32[8,65,128]{2,1,0:T(8,128)S(1)}, f32[8,65,128]{2,1,0:T(8,128)}, u32[]{:S(2)}) copy-start(f32[8,65,128]{2,1,0:T(8,128)} %copy-done.11) | copy-start | bytes 798724
  116.6 34.5 %copy-start.6 = (bf16[1024,128]{1,0:T(8,128)(2,1)S(1)}, bf16[1024,128]{1,0:T(8,128)(2,1)}, u32[]{:S(2)}) copy-start(bf16[1024,128]{1,0:T(8,128)(2,1)} %param.10) | copy-start | bytes 786436
  117.5 25.5 %collective-permute-start.11 = (f32[2,64,128]{2,1,0:T(8,128)S(1)}, f32[2,64,128]{2,1,0:T(8,128)S(1)}, u32[]{:S(2)}, u32[]{:S(2)}) collective-permute-start(f32[2,64,128]{2,1,0:T(8,128)S(1)} %add.115), channel_id=1, source_target_pairs={{0,24},{1,56},{2,88},{3,120},{4,152},{5,184},{6,216},{7,248},{8,0}... | collective-permute-start | bytes 196616 | tf_op jit(solution)/shard_map/ppermute | solution.py:162
  117.8 27.9 %collective-permute-start.10 = (f32[2,64,128]{2,1,0:T(8,128)S(1)}, f32[2,64,128]{2,1,0:T(8,128)S(1)}, u32[]{:S(2)}, u32[]{:S(2)}) collective-permute-start(f32[2,64,128]{2,1,0:T(8,128)S(1)} %add.115), channel_id=1, source_target_pairs={{0,16},{1,48},{2,80},{3,112},{4,144},{5,176},{6,208},{7,240},{8,24... | collective-permute-start | bytes 196616 | tf_op jit(solution)/shard_map/ppermute | solution.py:162
  127.2 18.7 %collective-permute-start.9 = (f32[2,64,128]{2,1,0:T(8,128)S(1)}, f32[2,64,128]{2,1,0:T(8,128)S(1)}, u32[]{:S(2)}, u32[]{:S(2)}) collective-permute-start(f32[2,64,128]{2,1,0:T(8,128)S(1)} %add.115), channel_id=1, source_target_pairs={{0,8},{1,40},{2,72},{3,104},{4,136},{5,168},{6,200},{7,232},{8,16}... | collective-permute-start | bytes 196616 | tf_op jit(solution)/shard_map/ppermute | solution.py:162
  129.9 18.0 %collective-permute-start.8 = (f32[2,64,128]{2,1,0:T(8,128)S(1)}, f32[2,64,128]{2,1,0:T(8,128)S(1)}, u32[]{:S(2)}, u32[]{:S(2)}) collective-permute-start(f32[2,64,128]{2,1,0:T(8,128)S(1)} %add.115), channel_id=1, source_target_pairs={{0,0},{1,32},{2,64},{3,96},{4,128},{5,160},{6,192},{7,224},{8,8},{... | collective-permute-start | bytes 196616 | tf_op jit(solution)/shard_map/ppermute | solution.py:162
  149.5 2.0 %copy-start.1 = (f32[64,8,4,256]{3,1,2,0:T(8,128)S(1)}, f32[64,8,4,256]{3,1,2,0:T(8,128)}, u32[]{:S(2)}) copy-start(f32[64,8,4,256]{3,1,2,0:T(8,128)} %copy.152) | copy-start | bytes 6291460
  (4 other events, 4.7 us)

commit v3 on v2

--- a/solution.py
+++ b/solution.py
@@ -133,13 +133,6 @@
         resp_grad, resp_queries, resp_decay, resp_segment, resp_alive, resp_parts[0]
     )
     resp_len = lax.axis_size("resp")
-    shift = 1
-    summed_state = partial_state
-    while shift < resp_len:
-        summed_state = summed_state + lax.ppermute(
-            summed_state, "resp", [(k, k ^ shift) for k in range(resp_len)]
-        )
-        shift *= 2
     head_count = prompt_decay.shape[0]
     prompt_len = prompt_grad.shape[0]
     zero_label = jnp.zeros((prompt_len,), jnp.int32)
@@ -150,7 +143,7 @@
     shard_total = cum_sums[:, -1]
     seq_index = lax.axis_index("seq")
     seq_len = lax.axis_size("seq")
-    share = head_count // summed_state.shape[0]
+    share = head_count // partial_state.shape[0]
     pieces = []
     for turn in range(share):
         pairs = []
@@ -159,28 +152,29 @@
                 dst_seq = share * src_resp + (src_seq % share + turn) % share
                 dst_resp = src_seq // share
                 pairs.append((src_seq * resp_len + src_resp, dst_seq * resp_len + dst_resp))
-        pieces.append(lax.ppermute(summed_state, ("seq", "resp"), pairs))
+        pieces.append(lax.ppermute(partial_state, ("seq", "resp"), pairs))
     pieces = jnp.stack(pieces)
     order = (seq_index % share - jnp.arange(share)) % share
-    my_heads = jnp.take(pieces, order, axis=0).reshape((head_count,) + summed_state.shape[1:])
-    span_len = lax.axis_size("seq")
+    my_heads = jnp.take(pieces, order, axis=0).reshape((head_count,) + partial_state.shape[1:])
     whole_b = start_grad
     whole_a = jnp.exp(shard_total)
     later_b = jnp.zeros_like(start_grad)
     later_a = jnp.ones_like(whole_a)
     shift = 1
-    while shift < span_len:
-        pairs = [(k + shift, k) for k in range(span_len - shift)]
-        message = jnp.concatenate(
-            [whole_b, jnp.broadcast_to(whole_a[:, None, None], (head_count, 1, N))], axis=1
-        )
-        got = lax.ppermute(message, "seq", pairs)
-        valid = seq_index + shift < span_len
+    while shift < seq_len:
+        pairs = [((k + shift) % seq_len, k) for k in range(seq_len)]
+        parts = [whole_b, jnp.broadcast_to(whole_a[:, None, None], (head_count, 1, N))]
+        if shift >= share:
+            parts.append(my_heads)
+        got = lax.ppermute(jnp.concatenate(parts, axis=1), "seq", pairs)
+        valid = seq_index + shift < seq_len
         got_b = jnp.where(valid, got[:, :P_SIZE], 0.0)
         got_a = jnp.where(valid, got[:, P_SIZE, 0], 1.0)
+        if shift >= share:
+            my_heads = my_heads + got[:, P_SIZE + 1 :]
         later_b = later_b + later_a[:, None, None] * got_b
         later_a = later_a * got_a
-        if shift * 2 < span_len:
+        if shift * 2 < seq_len:
             whole_b = whole_b + whole_a[:, None, None] * got_b
             whole_a = whole_a * got_a
         shift *= 2

time: 155 us -> 150 us (0.968)
  the two profiles are of different devices: /device:TPU:31 before, /device:TPU:94 now
where the time goes in v3:
time: 150 us; the launch traced here: 149 us
  local copies, waits for them, and re-layouts  42.5 us (28%)
  waiting for transfers between devices  33.7 us (22%)
  other arithmetic  27.9 us (19%)
  matrix products  22.2 us (15%)
  starting transfers between devices  21.4 us (14%)
    ppermute x5, waiting for transfers between devices, on_device(): got = lax.ppermute(jnp.concatenate(parts, axis=1), 'seq', pairs)  33.7 us
    ppermute x4, starting transfers between devices, on_device(): pieces.append(lax.ppermute(partial_state, ('seq', 'resp'), pairs))  21 us
    unnamed x74, local copies, waits for them, and re-layouts  18.1 us
    dot_general x2, matrix products, group_output(): jnp.einsum('chst,cshp->cthp', mixing, grad_group, preferred_element_type=...  7.39 us
    dot_general x2, matrix products, group_parts(): jnp.einsum('hcd,dhpn->chpn', coef, states, precision=lax.Precision.HIGHEST)  4.5 us
    slice x5, local copies, waits for them, and re-layouts, on_device(): got_b = jnp.where(valid, got[:, :P_SIZE], 0.0)  4.26 us
    another operation x6, other arithmetic  4 us
    and x1, other arithmetic, group_output(): (row_index >= col_index)[None]  3.61 us
  transfers between devices with their start and end apart: 9, of which 4 were waited for; matrix products, arithmetic and copies ran while one was open for 47% of the time, Pallas kernels for 0%

profile of v3, /device:TPU:94, one launch (start us, length us, event | category | flops | bytes accessed | tf_op | source)
XLA Modules:
  0.0 149.0 jit_solution(9990415820448184024)
XLA Ops:
  2.3 1.6 %copy.345 = bf16[4096,128]{0,1:T(8,128)(2,1)S(1)} copy(bf16[4096,128]{1,0:T(8,128)(2,1)} %param.13) | data formatting | bytes 2097152 | tf_op args[4]
  6.7 5.0 %collective-permute-start.5 = (f32[2,64,128]{2,1,0:T(8,128)}, f32[2,64,128]{2,1,0:T(8,128)}, u32[]{:S(2)}, u32[]{:S(2)}) collective-permute-start(f32[2,64,128]{2,1,0:T(8,128)} %fusion.20), channel_id=1, source_target_pairs={{0,24},{1,56},{2,88},{3,120},{4,152},{5,184},{6,216},{7,248},{8,0}... | collective-permute-start | bytes 196616 | tf_op jit(solution)/shard_map/ppermute | solution.py:155
  11.7 4.0 %collective-permute-start.4 = (f32[2,64,128]{2,1,0:T(8,128)}, f32[2,64,128]{2,1,0:T(8,128)}, u32[]{:S(2)}, u32[]{:S(2)}) collective-permute-start(f32[2,64,128]{2,1,0:T(8,128)} %fusion.20), channel_id=1, source_target_pairs={{0,16},{1,48},{2,80},{3,112},{4,144},{5,176},{6,208},{7,240},{8,24... | collective-permute-start | bytes 196616 | tf_op jit(solution)/shard_map/ppermute | solution.py:155
  15.7 5.2 %collective-permute-start.3 = (f32[2,64,128]{2,1,0:T(8,128)}, f32[2,64,128]{2,1,0:T(8,128)}, u32[]{:S(2)}, u32[]{:S(2)}) collective-permute-start(f32[2,64,128]{2,1,0:T(8,128)} %fusion.20), channel_id=1, source_target_pairs={{0,8},{1,40},{2,72},{3,104},{4,136},{5,168},{6,200},{7,232},{8,16}... | collective-permute-start | bytes 196616 | tf_op jit(solution)/shard_map/ppermute | solution.py:155
  20.9 6.8 %collective-permute-start.2 = (f32[2,64,128]{2,1,0:T(8,128)}, f32[2,64,128]{2,1,0:T(8,128)}, u32[]{:S(2)}, u32[]{:S(2)}) collective-permute-start(f32[2,64,128]{2,1,0:T(8,128)} %fusion.20), channel_id=1, source_target_pairs={{0,0},{1,32},{2,64},{3,96},{4,128},{5,160},{6,192},{7,224},{8,8},{... | collective-permute-start | bytes 196616 | tf_op jit(solution)/shard_map/ppermute | solution.py:155
  27.7 2.3 %reduce-window.14 = f32[8,8,128]{2,1,0:T(8,128)S(1)} reduce-window(f32[8,8,128]{2,1,0:T(8,128)S(1)} %copy.323, f32[]{:T(128)} %constant.35.clone.1), window={size=1x1x128 pad=0_0x0_0x127_0}, to_apply=%region_0.0 | reduce-window | flops 1040384 | bytes 65540 | tf_op jit(solution)/shard_map/reduce-window
  34.9 2.3 %copy.327 = bf16[1024,512]{0,1:T(8,128)(2,1)} copy(bf16[1024,512]{1,0:T(8,128)(2,1)} %param.9) | data formatting | bytes 2097152 | tf_op args[0]
  37.2 2.7 %reshape.377 = bf16[4,256,8,64]{1,0,3,2:T(4,128)(2,1)} reshape(bf16[1024,512]{0,1:T(8,128)(2,1)} %copy.327) | data formatting | bytes 2097152 | tf_op jit(solution)/shard_map/reshape | solution.py:24
  42.1 1.6 %multiply_convert_fusion.5 = bf16[4,256,8,64]{1,0,3,2:T(4,128)(2,1)S(1)} fusion(bf16[4,256,8,64]{1,0,3,2:T(4,128)(2,1)} %reshape.377, f32[4,256,8]{1,0,2:T(4,128)} %copy.331), kind=kLoop, calls=%fused_computation.29 | loop fusion | flops 1572864 | bytes 2129920 | tf_op jit(solution)/shard_map/convert_element_type | solution.py:28
  44.2 2.5 %convolution_bitcast_fusion = f32[5,8,64,128]{3,0,2,1:T(8,128)S(1)} fusion(f32[8,5,4,1]{1,2,3,0:T(4,128)S(1)} %copy.378, f32[4,8,64,128]{3,2,1,0:T(8,128)S(1)} %fusion.28), kind=kOutput, calls=%fused_computation.30 | convolution fusion | flops 15728640 | bytes 2359936 | tf_op jit(solution)/shard_map/hcd,dhpn->chpn/dot_general | solution.py:46
  54.9 1.7 %fusion.32 = f32[4,8,64,256]{3,2,1,0:T(8,128)S(1)} fusion(bf16[4,256,128,1]{2,1,3,0:T(8,128)(2,1)} %bitcast.214, bf16[4,8,64,128]{3,0,2,1:T(4,128)(2,1)} %slice.200), kind=kOutput, calls=%fused_computation.48 | convolution fusion | flops 134217728 | bytes 2883584 | tf_op jit(solution)/shard_map/chpn,ctn->cthp/dot_general | solution.py:85
  56.9 2.2 %fusion.18 = f32[4,256,8,64]{1,3,2,0:T(8,128)S(1)} fusion(f32[4,8,64,256]{3,2,1,0:T(8,128)S(1)} %fusion.32, f32[4,8,256]{2,1,0:T(8,128)S(1)} %copy.325, f32[4,256,256]{2,1,0:T(8,128)S(1)} %fusion.96, pred[256,256]{1,0:T(8,128)(4,1)S(1)} %copy-done.21, bf16[4,256,8,64]{1,0,3,2:T(4,128)(2,1)S(1)} %copy-done.5, f32[4,256,8]{1,2,0:T(8,128)S(1)} %copy-done.23), kind=kOutput, calls=%fused_computation.27 | convolution fusion | flops 277872640 | bytes 6422528 | tf_op jit(solution)/shard_map/chst,cshp->cthp/dot_general | solution.py:82
  59.2 1.4 copy.337
  60.5 1.8 %copy.408 = f32[64,8,4,256]{3,1,2,0:T(8,128)} copy(f32[64,8,4,256]{3,2,1,0:T(4,128)S(1)} %bitcast.205) | data formatting | bytes 4194304
  62.5 3.6 %and_and_fusion = pred[16,256,256]{2,1,0:T(8,128)(4,1)} fusion(s32[16,256]{1,0:T(8,128)S(1)} %eq.82, pred[16,256]{1,0:T(8,128)(4,1)S(1)} %and.129, pred[256,256]{1,0:T(8,128)(4,1)} %iota_compare_fusion.1), kind=kLoop, calls=%fused_computation.16 | loop fusion | flops 3145728 | bytes 1134592 | tf_op jit(solution)/shard_map/and | solution.py:75
  66.1 1.2 copy.412
  70.1 1.4 multiply_convert_fusion.4
  75.2 1.7 %pad_maximum_fusion.5 = f32[4,2,64,128]{3,2,1,0:T(8,128)} fusion(f32[1,2,64,128]{3,2,1,0:T(8,128)} %bitcast.34, f32[1,2,64,128]{3,2,1,0:T(8,128)} %bitcast.33, f32[1,2,64,128]{3,2,1,0:T(8,128)} %bitcast.32, f32[1,2,64,128]{3,2,1,0:T(8,128)} %bitcast.31), kind=kLoop, calls=%fused_computation.56 | loop fusion | flops 196608 | bytes 524288 | tf_op jit(solution)/shard_map/stack | solution.py:156
  76.9 1.5 %gather_fusion = f32[4,2,64,128]{3,2,1,0:T(8,128)S(1)} fusion(f32[4,2,64,128]{3,2,1,0:T(8,128)} %pad_maximum_fusion.5, s32[1024]{0:T(1024)S(1)} %pad_clamp_fusion), kind=kCustom, calls=%fused_computation | custom fusion | bytes 524304 | tf_op jit(solution)/shard_map/jit(_take)/gather | solution.py:158
  79.3 8.3 %collective-permute-done.1 = f32[8,65,128]{2,0,1:T(8,128)} collective-permute-done((f32[8,65,128]{2,0,1:T(8,128)}, f32[8,65,128]{2,0,1:T(8,128)}, u32[]{:S(2)}, u32[]{:S(2)}) %collective-permute-start.1) | collective-permute-done | bytes 266272 | tf_op jit(solution)/shard_map/ppermute | solution.py:169
  92.8 2.0 %fusion.19 = bf16[17,2,64,128]{3,0,2,1:T(8,128)(2,1)S(1)} fusion(f32[16,2,64,128]{3,2,1,0:T(8,128)S(1)} %fusion.24, f32[2,17,16]{1,2,0:T(8,128)S(1)} %select_reduce_fusion.1, f32[17]{0:T(128)S(1)} %pad_maximum_fusion.7, pred[17,16]{0,1:T(8,128)(4,1)S(1)} %iota_compare_fusion.3), kind=kOutput, calls=%fused_computation.32 | convolution fusion | flops 53756992 | bytes 1608148 | tf_op jit(solution)/shard_map/hcd,dhpn->chpn/dot_general | solution.py:46
  95.7 2.7 %fusion.97 = f32[16,256,256]{2,1,0:T(8,128)} fusion(bf16[16,256,128]{2,1,0:T(8,128)(2,1)S(1)} %bitcast.207, bf16[16,256,128]{2,1,0:T(8,128)(2,1)S(1)} %bitcast.202), kind=kOutput, calls=%fused_computation.193 | convolution fusion | flops 268435456 | bytes 6291456 | tf_op jit(solution)/shard_map/csn,ctn->cst/dot_general | solution.py:71
  98.4 11.5 %collective-permute-done.6 = f32[8,129,128]{2,0,1:T(8,128)S(1)} collective-permute-done((f32[8,129,128]{2,0,1:T(8,128)S(1)}, f32[8,129,128]{2,0,1:T(8,128)S(1)}, u32[]{:S(2)}, u32[]{:S(2)}) %collective-permute-start.6) | collective-permute-done | bytes 528416 | tf_op jit(solution)/shard_map/ppermute | solution.py:169
  112.1 1.4 copy_add_fusion.2
  114.0 5.1 %fusion.3 = f32[16,2,256,64]{2,3,1,0:T(8,128)} fusion(f32[16,2,256]{2,1,0:T(2,128)S(1)} %bitcast.234, f32[16,256,256]{2,1,0:T(8,128)S(1)} %copy-done.2, pred[16,256,256]{2,1,0:T(8,128)(4,1)} %and_and_fusion, bf16[16,256,2,64]{1,0,3,2:T(8,128)(2,1)S(1)} %bitcast.211), kind=kOutput, calls=%fused_computation.6 | convolution fusion | flops 276824064 | bytes 8421376 | tf_op jit(solution)/shard_map/chst,cshp->cthp/dot_general | solution.py:82
  119.2 8.7 %collective-permute-done.7 = f32[8,129,128]{2,0,1:T(8,128)S(1)} collective-permute-done((f32[8,129,128]{2,0,1:T(8,128)S(1)}, f32[8,129,128]{2,0,1:T(8,128)S(1)}, u32[]{:S(2)}, u32[]{:S(2)}) %collective-permute-start.7) | collective-permute-done | bytes 528416 | tf_op jit(solution)/shard_map/ppermute | solution.py:169
  130.1 1.5 fusion.16
  131.6 4.5 %copy.392 = bf16[16,256,2,64]{3,2,1,0:T(2,128)(2,1)S(1)} copy(bf16[16,256,2,64]{1,3,2,0:T(8,128)(2,1)} %fusion.16) | data formatting | bytes 2097152
  136.1 1.8 %reshape.406 = bf16[4096,128]{1,0:T(8,128)(2,1)} reshape(bf16[16,256,2,64]{3,2,1,0:T(2,128)(2,1)S(1)} %copy.392) | data formatting | bytes 2097152
  138.0 5.2 %collective-permute-done.8 = f32[8,129,128]{2,0,1:T(8,128)} collective-permute-done((f32[8,129,128]{2,0,1:T(8,128)}, f32[8,129,128]{2,0,1:T(8,128)}, u32[]{:S(2)}, u32[]{:S(2)}) %collective-permute-start.8) | collective-permute-done | bytes 528416 | tf_op jit(solution)/shard_map/ppermute | solution.py:169
  145.0 2.2 %bitcast_multiply_fusion.1 = f32[1024,8,64]{0,2,1:T(8,128)S(1)} fusion(f32[1024,8]{0,1:T(8,128)S(1)} %exponential_bitcast_fusion, bf16[1024,128]{1,0:T(8,128)(2,1)} %param.10, f32[8,64,128]{2,1,0:T(8,128)S(1)} %copy_add_fusion.1, f32[8,64,128]{2,0,1:T(8,128)S(1)} %get-tuple-element.32, f32[8,64,128]{2,0,1:T(8,128)S(1)} %get-tuple-element.31, ...), kind=kOutput, calls=%fused_computation.25 | convolution fusion | flops 135856128 | bytes 4227237 | tf_op jit(solution)/shard_map/hpn,tn->thp/dot_general | solution.py:183
  147.7 1.3 copy.375
  (188 shorter events, 41.1 us)
Async XLA Ops:
  0.6 95.1 %copy-start = (bf16[4096,128]{1,0:T(8,128)(2,1)S(1)}, bf16[4096,128]{1,0:T(8,128)(2,1)}, u32[]{:S(2)}) copy-start(bf16[4096,128]{1,0:T(8,128)(2,1)} %param.14) | copy-start | bytes 3145732
  0.6 3.3 %copy-start.18 = (s32[4096]{0:T(1024)S(1)}, s32[4096]{0:T(1024)}, u32[]{:S(2)}) copy-start(s32[4096]{0:T(1024)} %param.17) | copy-start | bytes 49156
  0.7 3.4 %copy-start.19 = (f32[2,4096]{1,0:T(2,128)S(1)}, f32[2,4096]{1,0:T(2,128)}, u32[]{:S(2)}) copy-start(f32[2,4096]{1,0:T(2,128)} %param.16) | copy-start | bytes 98308
  2.3 3.3 %copy-start.3 = (bf16[4096,128]{1,0:T(8,128)(2,1)S(1)}, bf16[4096,128]{1,0:T(8,128)(2,1)}, u32[]{:S(2)}) copy-start(bf16[4096,128]{1,0:T(8,128)(2,1)} %param.15) | copy-start | bytes 3145732
  4.6 23.1 %copy-start.22 = (f32[8,1024]{1,0:T(8,128)S(1)}, f32[8,1024]{1,0:T(8,128)}, u32[]{:S(2)}) copy-start(f32[8,1024]{1,0:T(8,128)} %param.12) | copy-start | bytes 98308
  5.5 28.3 %copy-start.27 = (f32[4]{0:T(128)S(1)}, f32[4]{0:T(128)}, u32[]{:S(2)}) copy-start(f32[4]{0:T(128)} %constant.37.clone.1) | copy-start | bytes 52
  5.6 29.2 %copy-start.25 = (f32[5]{0:T(128)S(1)}, f32[5]{0:T(128)}, u32[]{:S(2)}) copy-start(f32[5]{0:T(128)} %constant.63.clone.1) | copy-start | bytes 64
  6.7 68.5 %collective-permute-start.5 = (f32[2,64,128]{2,1,0:T(8,128)}, f32[2,64,128]{2,1,0:T(8,128)}, u32[]{:S(2)}, u32[]{:S(2)}) collective-permute-start(f32[2,64,128]{2,1,0:T(8,128)} %fusion.20), channel_id=1, source_target_pairs={{0,24},{1,56},{2,88},{3,120},{4,152},{5,184},{6,216},{7,248},{8,0}... | collective-permute-start | bytes 196616 | tf_op jit(solution)/shard_map/ppermute | solution.py:155
  11.7 63.5 %collective-permute-start.4 = (f32[2,64,128]{2,1,0:T(8,128)}, f32[2,64,128]{2,1,0:T(8,128)}, u32[]{:S(2)}, u32[]{:S(2)}) collective-permute-start(f32[2,64,128]{2,1,0:T(8,128)} %fusion.20), channel_id=1, source_target_pairs={{0,16},{1,48},{2,80},{3,112},{4,144},{5,176},{6,208},{7,240},{8,24... | collective-permute-start | bytes 196616 | tf_op jit(solution)/shard_map/ppermute | solution.py:155
  15.7 59.5 %collective-permute-start.3 = (f32[2,64,128]{2,1,0:T(8,128)}, f32[2,64,128]{2,1,0:T(8,128)}, u32[]{:S(2)}, u32[]{:S(2)}) collective-permute-start(f32[2,64,128]{2,1,0:T(8,128)} %fusion.20), channel_id=1, source_target_pairs={{0,8},{1,40},{2,72},{3,104},{4,136},{5,168},{6,200},{7,232},{8,16}... | collective-permute-start | bytes 196616 | tf_op jit(solution)/shard_map/ppermute | solution.py:155
  20.9 54.3 %collective-permute-start.2 = (f32[2,64,128]{2,1,0:T(8,128)}, f32[2,64,128]{2,1,0:T(8,128)}, u32[]{:S(2)}, u32[]{:S(2)}) collective-permute-start(f32[2,64,128]{2,1,0:T(8,128)} %fusion.20), channel_id=1, source_target_pairs={{0,0},{1,32},{2,64},{3,96},{4,128},{5,160},{6,192},{7,224},{8,8},{... | collective-permute-start | bytes 196616 | tf_op jit(solution)/shard_map/ppermute | solution.py:155
  37.2 6.6 %copy-start.15 = (bf16[1024,128]{1,0:T(8,128)(2,1)S(1)}, bf16[1024,128]{1,0:T(8,128)(2,1)}, u32[]{:S(2)}) copy-start(bf16[1024,128]{1,0:T(8,128)(2,1)} %param.11) | copy-start | bytes 786436
  47.9 24.4 %collective-permute-start = (f32[8,65,128]{2,0,1:T(8,128)}, f32[8,65,128]{2,0,1:T(8,128)}, u32[]{:S(2)}, u32[]{:S(2)}) collective-permute-start(f32[8,65,128]{2,0,1:T(8,128)} %pad_maximum_fusion.3), channel_id=1, source_target_pairs={{8,0},{16,8},{24,16},{32,24},{40,32},{48,40},{56,48},{64,56},{72,6... | collective-permute-start | bytes 798728 | tf_op jit(solution)/shard_map/ppermute | solution.py:169
  54.8 1.7 %copy-start.12 = (bf16[1024,128]{1,0:T(8,128)(2,1)S(1)}, bf16[1024,128]{1,0:T(8,128)(2,1)}, u32[]{:S(2)}) copy-start(bf16[1024,128]{1,0:T(8,128)(2,1)} %param.10) | copy-start | bytes 786436
  54.8 1.7 %copy-start.16 = (bf16[1024,128]{1,0:T(8,128)(2,1)S(1)}, bf16[1024,128]{1,0:T(8,128)(2,1)}, u32[]{:S(2)}) copy-start(bf16[1024,128]{1,0:T(8,128)(2,1)} %param.11) | copy-start | bytes 786436
  54.9 2.0 %copy-start.5 = (bf16[4,256,8,64]{1,0,3,2:T(4,128)(2,1)S(1)}, bf16[4,256,8,64]{1,0,3,2:T(4,128)(2,1)}, u32[]{:S(2)}) copy-start(bf16[4,256,8,64]{1,0,3,2:T(4,128)(2,1)} %reshape.377) | copy-start | bytes 3145732
  54.9 2.0 %copy-start.21 = (pred[256,256]{1,0:T(8,128)(4,1)S(1)}, pred[256,256]{1,0:T(8,128)(4,1)}, u32[]{:S(2)}) copy-start(pred[256,256]{1,0:T(8,128)(4,1)} %iota_compare_fusion.1) | copy-start | bytes 196612
  54.9 2.0 %copy-start.23 = (f32[4,256,8]{1,2,0:T(8,128)S(1)}, f32[4,256,8]{1,2,0:T(8,128)}, u32[]{:S(2)}) copy-start(f32[4,256,8]{1,2,0:T(8,128)} %get-tuple-element.39) | copy-start | bytes 98308
  60.5 1.8 %copy-start.26 = (s32[4]{0:T(128)S(1)}, s32[4]{0:T(128)}, u32[]{:S(2)}) copy-start(s32[4]{0:T(128)} %fusion.78) | copy-start | bytes 52
  60.5 1.8 %copy-start.28 = (pred[4]{0:T(512)(128)(4,1)S(1)}, pred[4]{0:T(512)(128)(4,1)}, u32[]{:S(2)}) copy-start(pred[4]{0:T(512)(128)(4,1)} %compare_and_fusion.1) | copy-start | bytes 16
  75.2 12.4 %collective-permute-start.1 = (f32[8,65,128]{2,0,1:T(8,128)}, f32[8,65,128]{2,0,1:T(8,128)}, u32[]{:S(2)}, u32[]{:S(2)}) collective-permute-start(f32[8,65,128]{2,0,1:T(8,128)} %pad_maximum_fusion.4), channel_id=1, source_target_pairs={{16,0},{24,8},{32,16},{40,24},{48,32},{56,40},{64,48},{72,56},{80,... | collective-permute-start | bytes 798728 | tf_op jit(solution)/shard_map/ppermute | solution.py:169
  89.3 2.0 %copy-start.9 = (f32[8,64,128]{2,0,1:T(8,128)}, f32[8,64,128]{2,0,1:T(8,128)S(1)}, u32[]{:S(2)}) copy-start(f32[8,64,128]{2,0,1:T(8,128)S(1)} %slice.151) | copy-start | bytes 786436
  92.4 17.5 %collective-permute-start.6 = (f32[8,129,128]{2,0,1:T(8,128)S(1)}, f32[8,129,128]{2,0,1:T(8,128)S(1)}, u32[]{:S(2)}, u32[]{:S(2)}) collective-permute-start(f32[8,129,128]{2,0,1:T(8,128)S(1)} %pad_maximum_fusion), channel_id=1, source_target_pairs={{32,0},{40,8},{48,16},{56,24},{64,32},{72,40},{80,48},{88,56},{96,... | collective-permute-start | bytes 1585160 | tf_op jit(solution)/shard_map/ppermute | solution.py:169
  95.7 18.3 %copy-start.4 = (bf16[16,8,16,256]{3,2,1,0:T(8,128)(2,1)S(1)}, bf16[16,8,16,256]{3,2,1,0:T(8,128)(2,1)}, u32[]{:S(2)}) copy-start(bf16[16,8,16,256]{3,2,1,0:T(8,128)(2,1)} %copy.412) | copy-start | bytes 3145732
  110.9 3.2 %copy-start.2 = (f32[16,256,256]{2,1,0:T(8,128)S(1)}, f32[16,256,256]{2,1,0:T(8,128)}, u32[]{:S(2)}) copy-start(f32[16,256,256]{2,1,0:T(8,128)} %fusion.97) | copy-start | bytes 12582916
  112.1 7.1 %copy-start.10 = (f32[8,64,128]{2,0,1:T(8,128)}, f32[8,64,128]{2,0,1:T(8,128)S(1)}, u32[]{:S(2)}) copy-start(f32[8,64,128]{2,0,1:T(8,128)S(1)} %get-tuple-element.35) | copy-start | bytes 786436
  112.1 1.9 %copy-start.24 = (f32[2,16,256]{2,0,1:T(2,128)S(1)}, f32[2,16,256]{2,0,1:T(2,128)}, u32[]{:S(2)}) copy-start(f32[2,16,256]{2,0,1:T(2,128)} %copy.487) | copy-start | bytes 98308
  113.9 14.0 %collective-permute-start.7 = (f32[8,129,128]{2,0,1:T(8,128)S(1)}, f32[8,129,128]{2,0,1:T(8,128)S(1)}, u32[]{:S(2)}, u32[]{:S(2)}) collective-permute-start(f32[8,129,128]{2,0,1:T(8,128)S(1)} %pad_maximum_fusion.1), channel_id=1, source_target_pairs={{64,0},{72,8},{80,16},{88,24},{96,32},{104,40},{112,48},{120,56},{... | collective-permute-start | bytes 1585160 | tf_op jit(solution)/shard_map/ppermute | solution.py:169
  128.3 1.8 %copy-start.13 = (f32[16,2,256,64]{2,3,1,0:T(8,128)S(1)}, f32[16,2,256,64]{2,3,1,0:T(8,128)}, u32[]{:S(2)}) copy-start(f32[16,2,256,64]{2,3,1,0:T(8,128)} %fusion.3) | copy-start | bytes 6291460
  129.5 13.7 %collective-permute-start.8 = (f32[8,129,128]{2,0,1:T(8,128)}, f32[8,129,128]{2,0,1:T(8,128)}, u32[]{:S(2)}, u32[]{:S(2)}) collective-permute-start(f32[8,129,128]{2,0,1:T(8,128)} %pad_maximum_fusion.2), channel_id=1, source_target_pairs={{128,0},{136,8},{144,16},{152,24},{160,32},{168,40},{176,48},{184,... | collective-permute-start | bytes 1585160 | tf_op jit(solution)/shard_map/ppermute | solution.py:169
  136.1 1.8 %copy-start.20 = (f32[1,8,8,128]{3,2,1,0:T(8,128)S(1)}, f32[1,8,8,128]{3,2,1,0:T(8,128)}, u32[]{:S(2)}) copy-start(f32[1,8,8,128]{3,2,1,0:T(8,128)} %fusion.108) | copy-start | bytes 98308
  145.0 2.2 %copy-start.1 = (f32[64,8,4,256]{3,1,2,0:T(8,128)S(1)}, f32[64,8,4,256]{3,1,2,0:T(8,128)}, u32[]{:S(2)}) copy-start(f32[64,8,4,256]{3,1,2,0:T(8,128)} %copy.408) | copy-start | bytes 6291460
  (6 other events, 6.7 us)

commit v4 on v3

--- a/solution.py
+++ b/solution.py
@@ -156,28 +156,36 @@
     pieces = jnp.stack(pieces)
     order = (seq_index % share - jnp.arange(share)) % share
     my_heads = jnp.take(pieces, order, axis=0).reshape((head_count,) + partial_state.shape[1:])
+    own_a = jnp.exp(shard_total)
     whole_b = start_grad
-    whole_a = jnp.exp(shard_total)
+    whole_a = own_a
     later_b = jnp.zeros_like(start_grad)
-    later_a = jnp.ones_like(whole_a)
-    shift = 1
-    while shift < seq_len:
-        pairs = [((k + shift) % seq_len, k) for k in range(seq_len)]
+    later_a = jnp.ones_like(own_a)
+    span = 1
+    while span < seq_len:
+        radix = min(4, seq_len // span)
         parts = [whole_b, jnp.broadcast_to(whole_a[:, None, None], (head_count, 1, N))]
-        if shift >= share:
+        if span >= share:
             parts.append(my_heads)
-        got = lax.ppermute(jnp.concatenate(parts, axis=1), "seq", pairs)
-        valid = seq_index + shift < seq_len
-        got_b = jnp.where(valid, got[:, :P_SIZE], 0.0)
-        got_a = jnp.where(valid, got[:, P_SIZE, 0], 1.0)
-        if shift >= share:
-            my_heads = my_heads + got[:, P_SIZE + 1 :]
-        later_b = later_b + later_a[:, None, None] * got_b
-        later_a = later_a * got_a
-        if shift * 2 < seq_len:
-            whole_b = whole_b + whole_a[:, None, None] * got_b
-            whole_a = whole_a * got_a
-        shift *= 2
+        message = jnp.concatenate(parts, axis=1)
+        gots = []
+        for step in range(1, radix):
+            shift = span * step
+            pairs = [((k + shift) % seq_len, k) for k in range(seq_len)]
+            gots.append((shift, lax.ppermute(message, "seq", pairs)))
+        summed_heads = my_heads
+        for shift, got in gots:
+            valid = seq_index + shift < seq_len
+            got_b = jnp.where(valid, got[:, :P_SIZE], 0.0)
+            got_a = jnp.where(valid, got[:, P_SIZE, 0], 1.0)
+            later_b = later_b + later_a[:, None, None] * got_b
+            later_a = later_a * got_a
+            if span >= share:
+                summed_heads = summed_heads + got[:, P_SIZE + 1 :]
+        my_heads = summed_heads
+        whole_b = start_grad + own_a[:, None, None] * later_b
+        whole_a = own_a * later_a
+        span *= radix
     incoming = later_b + later_a[:, None, None] * my_heads
     local_part = group_output(prompt_keys, prompt_queries, prompt_parts)
     carry_term = jnp.einsum(

time: 150 us -> 167 us (1.11)
  the two profiles are of different devices: /device:TPU:94 before, /device:TPU:95 now
where the time goes in v4:
time: 167 us; the launch traced here: 165 us
  waiting for transfers between devices  48.6 us (29%)
  local copies, waits for them, and re-layouts  44.3 us (27%)
  other arithmetic  26.1 us (16%)
  matrix products  23.1 us (14%)
  starting transfers between devices  22 us (13%)
    ppermute x7, waiting for transfers between devices, on_device(): gots.append((shift, lax.ppermute(message, 'seq', pairs)))  48.6 us
    ppermute x4, starting transfers between devices, on_device(): pieces.append(lax.ppermute(partial_state, ('seq', 'resp'), pairs))  18.9 us
    unnamed x72, local copies, waits for them, and re-layouts  17.6 us
    dot_general x2, matrix products, group_output(): jnp.einsum('chst,cshp->cthp', mixing, grad_group, preferred_element_type=...  7.41 us
    slice x7, local copies, waits for them, and re-layouts, on_device(): got_b = jnp.where(valid, got[:, :P_SIZE], 0.0)  6.65 us
    dot_general x2, matrix products, group_output(): jnp.einsum('chpn,ctn->cthp', end_grads.astype(jnp.bfloat16), key_group, p...  4.66 us
    dot_general x2, matrix products, group_parts(): jnp.einsum('hcd,dhpn->chpn', coef, states, precision=lax.Precision.HIGHEST)  4.5 us
    slice x7, local copies, waits for them, and re-layouts, on_device(): got_a = jnp.where(valid, got[:, P_SIZE, 0], 1.0)  4.17 us
  transfers between devices with their start and end apart: 11, of which 4 were waited for; matrix products, arithmetic and copies ran while one was open for 43% of the time, Pallas kernels for 0%

profile of v4, /device:TPU:95, one launch (start us, length us, event | category | flops | bytes accessed | tf_op | source)
XLA Modules:
  0.0 165.5 jit_solution(574925520434318575)
XLA Ops:
  2.3 1.6 copy.377
  6.7 6.7 %collective-permute-start.6 = (f32[2,64,128]{2,1,0:T(8,128)}, f32[2,64,128]{2,1,0:T(8,128)}, u32[]{:S(2)}, u32[]{:S(2)}) collective-permute-start(f32[2,64,128]{2,1,0:T(8,128)} %fusion.20), channel_id=1, source_target_pairs={{0,24},{1,56},{2,88},{3,120},{4,152},{5,184},{6,216},{7,248},{8,0}... | collective-permute-start | bytes 196616 | tf_op jit(solution)/shard_map/ppermute | solution.py:155
  13.4 3.1 %collective-permute-start.5 = (f32[2,64,128]{2,1,0:T(8,128)}, f32[2,64,128]{2,1,0:T(8,128)}, u32[]{:S(2)}, u32[]{:S(2)}) collective-permute-start(f32[2,64,128]{2,1,0:T(8,128)} %fusion.20), channel_id=1, source_target_pairs={{0,16},{1,48},{2,80},{3,112},{4,144},{5,176},{6,208},{7,240},{8,24... | collective-permute-start | bytes 196616 | tf_op jit(solution)/shard_map/ppermute | solution.py:155
  16.5 5.0 %collective-permute-start.4 = (f32[2,64,128]{2,1,0:T(8,128)}, f32[2,64,128]{2,1,0:T(8,128)}, u32[]{:S(2)}, u32[]{:S(2)}) collective-permute-start(f32[2,64,128]{2,1,0:T(8,128)} %fusion.20), channel_id=1, source_target_pairs={{0,8},{1,40},{2,72},{3,104},{4,136},{5,168},{6,200},{7,232},{8,16}... | collective-permute-start | bytes 196616 | tf_op jit(solution)/shard_map/ppermute | solution.py:155
  21.5 4.1 %collective-permute-start.3 = (f32[2,64,128]{2,1,0:T(8,128)}, f32[2,64,128]{2,1,0:T(8,128)}, u32[]{:S(2)}, u32[]{:S(2)}) collective-permute-start(f32[2,64,128]{2,1,0:T(8,128)} %fusion.20), channel_id=1, source_target_pairs={{0,0},{1,32},{2,64},{3,96},{4,128},{5,160},{6,192},{7,224},{8,8},{... | collective-permute-start | bytes 196616 | tf_op jit(solution)/shard_map/ppermute | solution.py:155
  25.6 2.3 %reduce-window.14 = f32[8,8,128]{2,1,0:T(8,128)S(1)} reduce-window(f32[8,8,128]{2,1,0:T(8,128)S(1)} %copy.354, f32[]{:T(128)} %constant.35.clone.1), window={size=1x1x128 pad=0_0x0_0x127_0}, to_apply=%region_0.0 | reduce-window | flops 1040384 | bytes 65540 | tf_op jit(solution)/shard_map/reduce-window
  32.8 2.3 %copy.358 = bf16[1024,512]{0,1:T(8,128)(2,1)} copy(bf16[1024,512]{1,0:T(8,128)(2,1)} %param.9) | data formatting | bytes 2097152 | tf_op args[0]
  35.1 2.7 %reshape.359 = bf16[4,256,8,64]{1,0,3,2:T(4,128)(2,1)} reshape(bf16[1024,512]{0,1:T(8,128)(2,1)} %copy.358) | data formatting | bytes 2097152 | tf_op jit(solution)/shard_map/reshape | solution.py:24
  40.0 1.6 multiply_convert_fusion.5
  42.1 2.5 %convolution_bitcast_fusion = f32[5,8,64,128]{3,0,2,1:T(8,128)S(1)} fusion(f32[8,5,4,1]{1,2,3,0:T(4,128)S(1)} %copy.411, f32[4,8,64,128]{3,2,1,0:T(8,128)S(1)} %fusion.28), kind=kOutput, calls=%fused_computation.30 | convolution fusion | flops 15728640 | bytes 2359936 | tf_op jit(solution)/shard_map/hcd,dhpn->chpn/dot_general | solution.py:46
  45.8 2.4 %collective-permute-start.2 = (f32[8,65,128]{2,0,1:T(8,128)}, f32[8,65,128]{2,0,1:T(8,128)}, u32[]{:S(2)}, u32[]{:S(2)}) collective-permute-start(f32[8,65,128]{2,0,1:T(8,128)} %pad_maximum_fusion.2), channel_id=1, source_target_pairs={{24,0},{32,8},{40,16},{48,24},{56,32},{64,40},{72,48},{80,56},{88,... | collective-permute-start | bytes 798728 | tf_op jit(solution)/shard_map/ppermute | solution.py:175
  55.1 1.7 fusion.32
  57.1 2.2 %fusion.18 = f32[4,256,8,64]{1,3,2,0:T(8,128)S(1)} fusion(f32[4,8,64,256]{3,2,1,0:T(8,128)S(1)} %fusion.32, f32[4,8,256]{2,1,0:T(8,128)S(1)} %copy.356, f32[4,256,256]{2,1,0:T(8,128)S(1)} %fusion.109, pred[256,256]{1,0:T(8,128)(4,1)S(1)} %copy-done.18, bf16[4,256,8,64]{1,0,3,2:T(4,128)(2,1)S(1)} %copy-done.5, f32[4,256,8]{1,2,0:T(8,128)S(1)} %copy-done.20), kind=kOutput, calls=%fused_computation.27 | convolution fusion | flops 277872640 | bytes 6422528 | tf_op jit(solution)/shard_map/chst,cshp->cthp/dot_general | solution.py:82
  59.4 1.4 copy.368
  60.7 1.8 %copy.446 = f32[64,8,4,256]{3,1,2,0:T(8,128)} copy(f32[64,8,4,256]{3,2,1,0:T(4,128)S(1)} %bitcast.199) | data formatting | bytes 4194304
  62.7 3.6 %and_and_fusion = pred[16,256,256]{2,1,0:T(8,128)(4,1)} fusion(s32[16,256]{1,0:T(8,128)S(1)} %eq.82, pred[16,256]{1,0:T(8,128)(4,1)S(1)} %and.129, pred[256,256]{1,0:T(8,128)(4,1)} %iota_compare_fusion.1), kind=kLoop, calls=%fused_computation.16 | loop fusion | flops 3145728 | bytes 1134592 | tf_op jit(solution)/shard_map/and | solution.py:75
  66.3 1.2 copy.450
  70.9 1.4 multiply_convert_fusion.4
  73.1 2.0 %fusion.19 = bf16[17,2,64,128]{3,0,2,1:T(8,128)(2,1)S(1)} fusion(f32[16,2,64,128]{3,2,1,0:T(8,128)S(1)} %fusion.24, f32[2,17,16]{1,2,0:T(8,128)S(1)} %select_reduce_fusion.1, f32[17]{0:T(128)S(1)} %pad_maximum_fusion.5, pred[17,16]{0,1:T(8,128)(4,1)S(1)} %iota_compare_fusion.3), kind=kOutput, calls=%fused_computation.32 | convolution fusion | flops 53756992 | bytes 1608148 | tf_op jit(solution)/shard_map/hcd,dhpn->chpn/dot_general | solution.py:46
  76.1 2.7 %fusion.110 = f32[16,256,256]{2,1,0:T(8,128)} fusion(bf16[16,256,128]{2,1,0:T(8,128)(2,1)S(1)} %bitcast.201, bf16[16,256,128]{2,1,0:T(8,128)(2,1)S(1)} %bitcast.196), kind=kOutput, calls=%fused_computation.199 | convolution fusion | flops 268435456 | bytes 6291456 | tf_op jit(solution)/shard_map/csn,ctn->cst/dot_general | solution.py:71
  82.3 8.4 %collective-permute-done.1 = f32[8,65,128]{2,0,1:T(8,128)} collective-permute-done((f32[8,65,128]{2,0,1:T(8,128)}, f32[8,65,128]{2,0,1:T(8,128)}, u32[]{:S(2)}, u32[]{:S(2)}) %collective-permute-start.1) | collective-permute-done | bytes 266272 | tf_op jit(solution)/shard_map/ppermute | solution.py:175
  91.4 2.4 %collective-permute-done = f32[8,65,128]{2,0,1:T(8,128)} collective-permute-done((f32[8,65,128]{2,0,1:T(8,128)}, f32[8,65,128]{2,0,1:T(8,128)}, u32[]{:S(2)}, u32[]{:S(2)}) %collective-permute-start) | collective-permute-done | bytes 266272 | tf_op jit(solution)/shard_map/ppermute | solution.py:175
  96.7 1.2 slice.169
  99.9 5.2 %fusion.3 = f32[16,2,256,64]{2,3,1,0:T(8,128)} fusion(f32[16,2,256]{2,1,0:T(2,128)S(1)} %bitcast.229, f32[16,256,256]{2,1,0:T(8,128)S(1)} %copy-done.2, pred[16,256,256]{2,1,0:T(8,128)(4,1)} %and_and_fusion, bf16[16,256,2,64]{1,0,3,2:T(8,128)(2,1)S(1)} %bitcast.205), kind=kOutput, calls=%fused_computation.6 | convolution fusion | flops 276824064 | bytes 8421376 | tf_op jit(solution)/shard_map/chst,cshp->cthp/dot_general | solution.py:82
  105.1 31.7 %collective-permute-done.8 = f32[8,129,128]{2,0,1:T(8,128)S(1)} collective-permute-done((f32[8,129,128]{2,0,1:T(8,128)}, f32[8,129,128]{2,0,1:T(8,128)S(1)}, u32[]{:S(2)}, u32[]{:S(2)}) %collective-permute-start.8) | collective-permute-done | bytes 528416 | tf_op jit(solution)/shard_map/ppermute | solution.py:175
  144.5 3.0 %fusion.16 = bf16[16,256,2,64]{1,3,2,0:T(8,128)(2,1)} fusion(f32[16,2,256,64]{2,3,1,0:T(8,128)} %fusion.3, bf16[16,256,128,1]{2,1,3,0:T(8,128)(2,1)S(1)} %bitcast.197, f32[16,256,2]{1,2,0:T(2,128)S(1)} %get-tuple-element.42, bf16[16,2,64,128]{3,0,2,1:T(8,128)(2,1)S(1)} %copy-done.9), kind=kOutput, calls=%fused_computation.22 | convolution fusion | flops 135790592 | bytes 4751360 | tf_op jit(solution)/shard_map/chpn,ctn->cthp/dot_general | solution.py:85
  147.5 4.5 %copy.425 = bf16[16,256,2,64]{3,2,1,0:T(2,128)(2,1)S(1)} copy(bf16[16,256,2,64]{1,3,2,0:T(8,128)(2,1)} %fusion.16) | data formatting | bytes 2097152
  152.1 1.8 %reshape.388 = bf16[4096,128]{1,0:T(8,128)(2,1)} reshape(bf16[16,256,2,64]{3,2,1,0:T(2,128)(2,1)S(1)} %copy.425) | data formatting | bytes 2097152
  153.9 6.2 %collective-permute-done.10 = f32[8,129,128]{2,0,1:T(8,128)} collective-permute-done((f32[8,129,128]{2,0,1:T(8,128)}, f32[8,129,128]{2,0,1:T(8,128)}, u32[]{:S(2)}, u32[]{:S(2)}) %collective-permute-start.10) | collective-permute-done | bytes 528416 | tf_op jit(solution)/shard_map/ppermute | solution.py:175
  160.9 1.2 fusion.104
  162.1 1.5 bitcast_multiply_fusion.1
  164.1 1.3 copy.408
  (181 shorter events, 43.7 us)
Async XLA Ops:
  0.6 75.5 %copy-start = (bf16[4096,128]{1,0:T(8,128)(2,1)S(1)}, bf16[4096,128]{1,0:T(8,128)(2,1)}, u32[]{:S(2)}) copy-start(bf16[4096,128]{1,0:T(8,128)(2,1)} %param.14) | copy-start | bytes 3145732
  0.6 3.3 %copy-start.15 = (s32[4096]{0:T(1024)S(1)}, s32[4096]{0:T(1024)}, u32[]{:S(2)}) copy-start(s32[4096]{0:T(1024)} %param.17) | copy-start | bytes 49156
  0.7 3.4 %copy-start.16 = (f32[2,4096]{1,0:T(2,128)S(1)}, f32[2,4096]{1,0:T(2,128)}, u32[]{:S(2)}) copy-start(f32[2,4096]{1,0:T(2,128)} %param.16) | copy-start | bytes 98308
  2.3 3.3 %copy-start.3 = (bf16[4096,128]{1,0:T(8,128)(2,1)S(1)}, bf16[4096,128]{1,0:T(8,128)(2,1)}, u32[]{:S(2)}) copy-start(bf16[4096,128]{1,0:T(8,128)(2,1)} %param.15) | copy-start | bytes 3145732
  4.6 21.0 %copy-start.19 = (f32[8,1024]{1,0:T(8,128)S(1)}, f32[8,1024]{1,0:T(8,128)}, u32[]{:S(2)}) copy-start(f32[8,1024]{1,0:T(8,128)} %param.12) | copy-start | bytes 98308
  5.5 26.2 %copy-start.25 = (f32[4]{0:T(128)S(1)}, f32[4]{0:T(128)}, u32[]{:S(2)}) copy-start(f32[4]{0:T(128)} %constant.37.clone.1) | copy-start | bytes 52
  5.6 27.1 %copy-start.24 = (f32[5]{0:T(128)S(1)}, f32[5]{0:T(128)}, u32[]{:S(2)}) copy-start(f32[5]{0:T(128)} %constant.39.clone.1) | copy-start | bytes 64
  6.7 72.1 %collective-permute-start.6 = (f32[2,64,128]{2,1,0:T(8,128)}, f32[2,64,128]{2,1,0:T(8,128)}, u32[]{:S(2)}, u32[]{:S(2)}) collective-permute-start(f32[2,64,128]{2,1,0:T(8,128)} %fusion.20), channel_id=1, source_target_pairs={{0,24},{1,56},{2,88},{3,120},{4,152},{5,184},{6,216},{7,248},{8,0}... | collective-permute-start | bytes 196616 | tf_op jit(solution)/shard_map/ppermute | solution.py:155
  13.4 65.5 %collective-permute-start.5 = (f32[2,64,128]{2,1,0:T(8,128)}, f32[2,64,128]{2,1,0:T(8,128)}, u32[]{:S(2)}, u32[]{:S(2)}) collective-permute-start(f32[2,64,128]{2,1,0:T(8,128)} %fusion.20), channel_id=1, source_target_pairs={{0,16},{1,48},{2,80},{3,112},{4,144},{5,176},{6,208},{7,240},{8,24... | collective-permute-start | bytes 196616 | tf_op jit(solution)/shard_map/ppermute | solution.py:155
  16.5 63.1 %collective-permute-start.4 = (f32[2,64,128]{2,1,0:T(8,128)}, f32[2,64,128]{2,1,0:T(8,128)}, u32[]{:S(2)}, u32[]{:S(2)}) collective-permute-start(f32[2,64,128]{2,1,0:T(8,128)} %fusion.20), channel_id=1, source_target_pairs={{0,8},{1,40},{2,72},{3,104},{4,136},{5,168},{6,200},{7,232},{8,16}... | collective-permute-start | bytes 196616 | tf_op jit(solution)/shard_map/ppermute | solution.py:155
  21.5 58.1 %collective-permute-start.3 = (f32[2,64,128]{2,1,0:T(8,128)}, f32[2,64,128]{2,1,0:T(8,128)}, u32[]{:S(2)}, u32[]{:S(2)}) collective-permute-start(f32[2,64,128]{2,1,0:T(8,128)} %fusion.20), channel_id=1, source_target_pairs={{0,0},{1,32},{2,64},{3,96},{4,128},{5,160},{6,192},{7,224},{8,8},{... | collective-permute-start | bytes 196616 | tf_op jit(solution)/shard_map/ppermute | solution.py:155
  35.1 6.6 %copy-start.10 = (bf16[1024,128]{1,0:T(8,128)(2,1)S(1)}, bf16[1024,128]{1,0:T(8,128)(2,1)}, u32[]{:S(2)}) copy-start(bf16[1024,128]{1,0:T(8,128)(2,1)} %param.11) | copy-start | bytes 786436
  45.8 35.6 %collective-permute-start.2 = (f32[8,65,128]{2,0,1:T(8,128)}, f32[8,65,128]{2,0,1:T(8,128)}, u32[]{:S(2)}, u32[]{:S(2)}) collective-permute-start(f32[8,65,128]{2,0,1:T(8,128)} %pad_maximum_fusion.2), channel_id=1, source_target_pairs={{24,0},{32,8},{40,16},{48,24},{56,32},{64,40},{72,48},{80,56},{88,... | collective-permute-start | bytes 798728 | tf_op jit(solution)/shard_map/ppermute | solution.py:175
  52.6 15.8 %copy-start.22 = (f32[15]{0:T(128)}, f32[15]{0:T(128)S(1)}, u32[]{:S(2)}) copy-start(f32[15]{0:T(128)S(1)} %convert_reduce_fusion) | copy-start | bytes 184
  55.1 2.0 %copy-start.5 = (bf16[4,256,8,64]{1,0,3,2:T(4,128)(2,1)S(1)}, bf16[4,256,8,64]{1,0,3,2:T(4,128)(2,1)}, u32[]{:S(2)}) copy-start(bf16[4,256,8,64]{1,0,3,2:T(4,128)(2,1)} %reshape.359) | copy-start | bytes 3145732
  55.1 2.0 %copy-start.18 = (pred[256,256]{1,0:T(8,128)(4,1)S(1)}, pred[256,256]{1,0:T(8,128)(4,1)}, u32[]{:S(2)}) copy-start(pred[256,256]{1,0:T(8,128)(4,1)} %iota_compare_fusion.1) | copy-start | bytes 196612
  55.1 2.0 %copy-start.20 = (f32[4,256,8]{1,2,0:T(8,128)S(1)}, f32[4,256,8]{1,2,0:T(8,128)}, u32[]{:S(2)}) copy-start(f32[4,256,8]{1,2,0:T(8,128)} %get-tuple-element.43) | copy-start | bytes 98308
  76.1 2.7 %copy-start.23 = (s32[4]{0:T(128)S(1)}, s32[4]{0:T(128)}, u32[]{:S(2)}) copy-start(s32[4]{0:T(128)} %fusion.86) | copy-start | bytes 52
  78.8 11.8 %collective-permute-start.1 = (f32[8,65,128]{2,0,1:T(8,128)}, f32[8,65,128]{2,0,1:T(8,128)}, u32[]{:S(2)}, u32[]{:S(2)}) collective-permute-start(f32[8,65,128]{2,0,1:T(8,128)} %pad_maximum_fusion.2), channel_id=1, source_target_pairs={{16,0},{24,8},{32,16},{40,24},{48,32},{56,40},{64,48},{72,56},{80,... | collective-permute-start | bytes 798728 | tf_op jit(solution)/shard_map/ppermute | solution.py:175
  78.9 14.9 %collective-permute-start = (f32[8,65,128]{2,0,1:T(8,128)}, f32[8,65,128]{2,0,1:T(8,128)}, u32[]{:S(2)}, u32[]{:S(2)}) collective-permute-start(f32[8,65,128]{2,0,1:T(8,128)} %pad_maximum_fusion.2), channel_id=1, source_target_pairs={{8,0},{16,8},{24,16},{32,24},{40,32},{48,40},{56,48},{64,56},{72,6... | collective-permute-start | bytes 798728 | tf_op jit(solution)/shard_map/ppermute | solution.py:175
  81.2 18.6 %copy-start.4 = (bf16[16,8,16,256]{3,2,1,0:T(8,128)(2,1)S(1)}, bf16[16,8,16,256]{3,2,1,0:T(8,128)(2,1)}, u32[]{:S(2)}) copy-start(bf16[16,8,16,256]{3,2,1,0:T(8,128)(2,1)} %copy.450) | copy-start | bytes 3145732
  94.6 5.3 %copy-start.21 = (f32[2,16,256]{2,0,1:T(2,128)S(1)}, f32[2,16,256]{2,0,1:T(2,128)}, u32[]{:S(2)}) copy-start(f32[2,16,256]{2,0,1:T(2,128)} %copy.546) | copy-start | bytes 98308
  95.5 4.3 %copy-start.2 = (f32[16,256,256]{2,1,0:T(8,128)S(1)}, f32[16,256,256]{2,1,0:T(8,128)}, u32[]{:S(2)}) copy-start(f32[16,256,256]{2,1,0:T(8,128)} %fusion.110) | copy-start | bytes 12582916
  99.9 36.9 %collective-permute-start.8 = (f32[8,129,128]{2,0,1:T(8,128)}, f32[8,129,128]{2,0,1:T(8,128)S(1)}, u32[]{:S(2)}, u32[]{:S(2)}) collective-permute-start(f32[8,129,128]{2,0,1:T(8,128)} %pad_maximum_fusion), channel_id=1, source_target_pairs={{64,0},{72,8},{80,16},{88,24},{96,32},{104,40},{112,48},{120,56},{... | collective-permute-start | bytes 1585160 | tf_op jit(solution)/shard_map/ppermute | solution.py:175
  99.9 37.7 %collective-permute-start.7 = (f32[8,129,128]{2,0,1:T(8,128)}, f32[8,129,128]{2,0,1:T(8,128)}, u32[]{:S(2)}, u32[]{:S(2)}) collective-permute-start(f32[8,129,128]{2,0,1:T(8,128)} %pad_maximum_fusion), channel_id=1, source_target_pairs={{32,0},{40,8},{48,16},{56,24},{64,32},{72,40},{80,48},{88,56},{96,... | collective-permute-start | bytes 1585160 | tf_op jit(solution)/shard_map/ppermute | solution.py:175
  105.1 36.3 %copy-start.12 = (f32[8,64,128]{2,1,0:T(8,128)S(1)}, f32[8,64,128]{2,1,0:T(8,128)}, u32[]{:S(2)}) copy-start(f32[8,64,128]{2,1,0:T(8,128)} %get-tuple-element.27) | copy-start | bytes 786436
  105.1 35.5 %collective-permute-start.9 = (f32[8,129,128]{2,0,1:T(8,128)}, f32[8,129,128]{2,0,1:T(8,128)S(1)}, u32[]{:S(2)}, u32[]{:S(2)}) collective-permute-start(f32[8,129,128]{2,0,1:T(8,128)} %pad_maximum_fusion), channel_id=1, source_target_pairs={{96,0},{104,8},{112,16},{120,24},{128,32},{136,40},{144,48},{152,5... | collective-permute-start | bytes 1585160 | tf_op jit(solution)/shard_map/ppermute | solution.py:175
  141.3 3.1 %copy-start.9 = (bf16[16,2,64,128]{3,0,2,1:T(8,128)(2,1)S(1)}, bf16[16,2,64,128]{3,0,2,1:T(8,128)(2,1)}, u32[]{:S(2)}) copy-start(bf16[16,2,64,128]{3,0,2,1:T(8,128)(2,1)} %slice.195) | copy-start | bytes 1572868
  142.5 2.0 %copy-start.6 = (f32[8,64,128]{2,1,0:T(8,128)}, f32[8,64,128]{2,1,0:T(8,128)S(1)}, u32[]{:S(2)}) copy-start(f32[8,64,128]{2,1,0:T(8,128)S(1)} %get-tuple-element.50) | copy-start | bytes 786436
  144.5 15.6 %collective-permute-start.10 = (f32[8,129,128]{2,0,1:T(8,128)}, f32[8,129,128]{2,0,1:T(8,128)}, u32[]{:S(2)}, u32[]{:S(2)}) collective-permute-start(f32[8,129,128]{2,0,1:T(8,128)} %pad_maximum_fusion.1), channel_id=1, source_target_pairs={{128,0},{136,8},{144,16},{152,24},{160,32},{168,40},{176,48},{184,... | collective-permute-start | bytes 1585160 | tf_op jit(solution)/shard_map/ppermute | solution.py:175
  152.0 10.1 %copy-start.7 = (f32[8,64,128]{2,1,0:T(8,128)S(1)}, f32[8,64,128]{2,1,0:T(8,128)}, u32[]{:S(2)}) copy-start(f32[8,64,128]{2,1,0:T(8,128)} %copy-done.6) | copy-start | bytes 786436
  160.9 2.8 %copy-start.1 = (f32[64,8,4,256]{3,1,2,0:T(8,128)S(1)}, f32[64,8,4,256]{3,1,2,0:T(8,128)}, u32[]{:S(2)}) copy-start(f32[64,8,4,256]{3,1,2,0:T(8,128)} %copy.446) | copy-start | bytes 6291460
  (6 other events, 8.7 us)

commit v5 on v3

--- a/solution.py
+++ b/solution.py
@@ -144,34 +144,40 @@
     seq_index = lax.axis_index("seq")
     seq_len = lax.axis_size("seq")
     share = head_count // partial_state.shape[0]
-    pieces = []
-    for turn in range(share):
-        pairs = []
-        for src_seq in range(seq_len):
-            for src_resp in range(resp_len):
-                dst_seq = share * src_resp + (src_seq % share + turn) % share
-                dst_resp = src_seq // share
-                pairs.append((src_seq * resp_len + src_resp, dst_seq * resp_len + dst_resp))
-        pieces.append(lax.ppermute(partial_state, ("seq", "resp"), pairs))
-    pieces = jnp.stack(pieces)
-    order = (seq_index % share - jnp.arange(share)) % share
-    my_heads = jnp.take(pieces, order, axis=0).reshape((head_count,) + partial_state.shape[1:])
+    pairs = []
+    for src_seq in range(seq_len):
+        for src_resp in range(resp_len):
+            dst_seq = share * src_resp + src_seq % share
+            dst_resp = src_seq // share
+            pairs.append((src_seq * resp_len + src_resp, dst_seq * resp_len + dst_resp))
+    pieces = lax.ppermute(partial_state, ("seq", "resp"), pairs)[None]
     whole_b = start_grad
     whole_a = jnp.exp(shard_total)
     later_b = jnp.zeros_like(start_grad)
     later_a = jnp.ones_like(whole_a)
+    my_heads = None
     shift = 1
     while shift < seq_len:
         pairs = [((k + shift) % seq_len, k) for k in range(seq_len)]
         parts = [whole_b, jnp.broadcast_to(whole_a[:, None, None], (head_count, 1, N))]
-        if shift >= share:
+        if my_heads is None:
+            parts.append(pieces.reshape(head_count, -1, N))
+        else:
             parts.append(my_heads)
         got = lax.ppermute(jnp.concatenate(parts, axis=1), "seq", pairs)
         valid = seq_index + shift < seq_len
         got_b = jnp.where(valid, got[:, :P_SIZE], 0.0)
         got_a = jnp.where(valid, got[:, P_SIZE, 0], 1.0)
-        if shift >= share:
-            my_heads = my_heads + got[:, P_SIZE + 1 :]
+        rest = got[:, P_SIZE + 1 :]
+        if my_heads is None:
+            pieces = jnp.concatenate([pieces, rest.reshape(pieces.shape)], axis=0)
+            if pieces.shape[0] == share:
+                order = (jnp.arange(share) - seq_index % share) % share
+                my_heads = jnp.take(pieces, order, axis=0).reshape(
+                    (head_count,) + partial_state.shape[1:]
+                )
+        else:
+            my_heads = my_heads + rest
         later_b = later_b + later_a[:, None, None] * got_b
         later_a = later_a * got_a
         if shift * 2 < seq_len:

time: 150 us -> 141 us (0.940)
  the two profiles are of different devices: /device:TPU:94 before, /device:TPU:14 now
where the time goes in v5:
time: 141 us; the launch traced here: 139 us
  local copies, waits for them, and re-layouts  42.8 us (30%)
  waiting for transfers between devices  33 us (23%)
  other arithmetic  27.4 us (19%)
  matrix products  24.7 us (18%)
  starting transfers between devices  9.43 us (7%)
  between operations  1.52 us (1%)
    ppermute x5, waiting for transfers between devices, on_device(): got = lax.ppermute(jnp.concatenate(parts, axis=1), 'seq', pairs)  33 us
    unnamed x110, local copies, waits for them, and re-layouts  19.7 us
    dot_general x2, matrix products, group_output(): jnp.einsum('chst,cshp->cthp', mixing, grad_group, preferred_element_type=...  8.78 us
    ppermute x1, starting transfers between devices, on_device(): pieces = lax.ppermute(partial_state, ('seq', 'resp'), pairs)[None]  7.25 us
    dot_general x2, matrix products, group_parts(): jnp.einsum('hcd,dhpn->chpn', coef, states, precision=lax.Precision.HIGHEST)  4.49 us
    another operation x6, other arithmetic  4.05 us
    slice x5, local copies, waits for them, and re-layouts, on_device(): got_b = jnp.where(valid, got[:, :P_SIZE], 0.0)  3.79 us
    dot_general x2, matrix products, group_output(): jnp.einsum('chpn,ctn->cthp', end_grads.astype(jnp.bfloat16), key_group, p...  3 us
  transfers between devices with their start and end apart: 6, of which 5 were waited for; matrix products, arithmetic and copies ran while one was open for 48% of the time, Pallas kernels for 0%

profile of v5, /device:TPU:14, one launch (start us, length us, event | category | flops | bytes accessed | tf_op | source)
XLA Modules:
  0.0 138.8 jit_solution(1154408143436430011)
XLA Ops:
  2.3 1.6 %copy.342 = bf16[4096,128]{0,1:T(8,128)(2,1)S(1)} copy(bf16[4096,128]{1,0:T(8,128)(2,1)} %param.13) | data formatting | bytes 2097152 | tf_op args[4]
  7.3 7.3 %collective-permute-start = (f32[2,64,128]{2,1,0:T(8,128)}, f32[2,64,128]{2,1,0:T(8,128)S(1)}, u32[]{:S(2)}, u32[]{:S(2)}) collective-permute-start(f32[2,64,128]{2,1,0:T(8,128)} %fusion.20), channel_id=1, source_target_pairs={{0,0},{1,32},{2,64},{3,96},{4,128},{5,160},{6,192},{7,224},{8,8},{... | collective-permute-start | bytes 196616 | tf_op jit(solution)/shard_map/ppermute | solution.py:153
  15.2 2.3 %reduce-window.14 = f32[8,8,128]{2,1,0:T(8,128)S(1)} reduce-window(f32[8,8,128]{2,1,0:T(8,128)S(1)} %copy.326, f32[]{:T(128)} %constant.35.clone.1), window={size=1x1x128 pad=0_0x0_0x127_0}, to_apply=%region_0.0 | reduce-window | flops 1040384 | bytes 65540 | tf_op jit(solution)/shard_map/reduce-window
  20.6 2.3 %copy.330 = bf16[1024,512]{0,1:T(8,128)(2,1)} copy(bf16[1024,512]{1,0:T(8,128)(2,1)} %param.9) | data formatting | bytes 2097152 | tf_op args[0]
  22.9 1.9 %reshape.386 = bf16[4,256,8,64]{1,0,3,2:T(4,128)(2,1)S(1)} reshape(bf16[1024,512]{0,1:T(8,128)(2,1)} %copy.330) | data formatting | bytes 2097152 | tf_op jit(solution)/shard_map/reshape | solution.py:24
  24.8 1.4 fusion.65
  27.0 2.5 %convolution_bitcast_fusion = f32[5,8,64,128]{3,0,2,1:T(8,128)S(1)} fusion(f32[8,5,4,1]{1,2,3,0:T(4,128)S(1)} %copy.385, f32[4,8,64,128]{3,2,1,0:T(8,128)S(1)} %fusion.28), kind=kOutput, calls=%fused_computation.30 | convolution fusion | flops 15728640 | bytes 2359936 | tf_op jit(solution)/shard_map/hcd,dhpn->chpn/dot_general | solution.py:46
  32.4 1.3 and.129
  41.0 1.1 copy.493
  43.1 1.2 multiply_bitcast_fusion.2
  45.3 1.5 %fusion.32 = f32[4,8,64,256]{3,2,1,0:T(8,128)S(1)} fusion(bf16[4,256,128,1]{2,1,3,0:T(8,128)(2,1)} %bitcast.215, bf16[4,8,64,128]{3,0,2,1:T(4,128)(2,1)} %slice.210), kind=kOutput, calls=%fused_computation.48 | convolution fusion | flops 134217728 | bytes 2883584 | tf_op jit(solution)/shard_map/chpn,ctn->cthp/dot_general | solution.py:85
  48.4 3.6 %fusion.18 = f32[4,256,8,64]{1,3,2,0:T(8,128)} fusion(f32[4,8,64,256]{3,2,1,0:T(8,128)S(1)} %fusion.32, f32[4,8,256]{2,1,0:T(8,128)S(1)} %copy-done.29, f32[4,256,256]{2,1,0:T(8,128)S(1)} %fusion.96, pred[256,256]{1,0:T(8,128)(4,1)S(1)} %copy-done.22, bf16[4,256,8,64]{1,0,3,2:T(4,128)(2,1)S(1)} %copy-done.8, f32[4,256,8]{1,2,0:T(8,128)S(1)} %copy-done.28), kind=kOutput, calls=%fused_computation.27 | convolution fusion | flops 277872640 | bytes 6422528 | tf_op jit(solution)/shard_map/chst,cshp->cthp/dot_general | solution.py:82
  54.0 1.7 %fusion.24 = f32[16,2,64,128]{3,2,1,0:T(8,128)S(1)} fusion(bf16[16,256,128,1]{2,1,3,0:T(8,128)(2,1)} %bitcast.207, bf16[16,256,2,64]{1,0,3,2:T(8,128)(2,1)S(1)} %multiply_convert_fusion.4), kind=kOutput, calls=%fused_computation.37 | convolution fusion | flops 134217728 | bytes 3145728 | tf_op jit(solution)/shard_map/clhp,cln->chpn/dot_general | solution.py:29
  55.7 2.7 %collective-permute-done.1 = f32[8,81,128]{2,0,1:T(8,128)} collective-permute-done((f32[8,81,128]{2,0,1:T(8,128)}, f32[8,81,128]{2,0,1:T(8,128)}, u32[]{:S(2)}, u32[]{:S(2)}) %collective-permute-start.1) | collective-permute-done | bytes 331808 | tf_op jit(solution)/shard_map/ppermute | solution.py:167
  60.2 1.2 bitcast_multiply_fusion.6
  62.0 1.7 %slice.158 = f32[8,64,128]{2,0,1:T(8,128)} slice(f32[8,81,128]{2,0,1:T(8,128)} %collective-permute-done.1), slice={[0:8], [0:64], [0:128]} | slice | bytes 524288 | tf_op jit(solution)/shard_map/slice | solution.py:169
  65.8 2.9 %copy.340 = f32[4,256,8,64]{1,0,3,2:T(4,128)S(1)} copy(f32[4,256,8,64]{1,3,2,0:T(8,128)} %fusion.18) | data formatting | bytes 4194304 | tf_op jit(solution)/shard_map/add | solution.py:96
  68.8 1.8 %copy.417 = f32[64,8,4,256]{3,1,2,0:T(8,128)} copy(f32[64,8,4,256]{3,2,1,0:T(4,128)S(1)} %bitcast.206) | data formatting | bytes 4194304
  70.8 2.5 %and_and_fusion = pred[16,256,256]{2,1,0:T(8,128)(4,1)} fusion(s32[16,256]{1,0:T(8,128)S(1)} %eq.82, pred[16,256]{1,0:T(8,128)(4,1)S(1)} %copy-done.26, pred[256,256]{1,0:T(8,128)(4,1)S(1)} %copy-done.23), kind=kLoop, calls=%fused_computation.16 | loop fusion | flops 3145728 | bytes 1134592 | tf_op jit(solution)/shard_map/and | solution.py:75
  73.3 4.2 %collective-permute-done.2 = f32[8,97,128]{2,0,1:T(8,128)S(1)} collective-permute-done((f32[8,97,128]{2,0,1:T(8,128)}, f32[8,97,128]{2,0,1:T(8,128)S(1)}, u32[]{:S(2)}, u32[]{:S(2)}) %collective-permute-start.2) | collective-permute-done | bytes 397344 | tf_op jit(solution)/shard_map/ppermute | solution.py:167
  82.1 2.0 %fusion.19 = bf16[17,2,64,128]{3,0,2,1:T(8,128)(2,1)S(1)} fusion(f32[16,2,64,128]{3,2,1,0:T(8,128)S(1)} %fusion.24, f32[2,17,16]{1,2,0:T(8,128)S(1)} %copy-done.25, f32[17]{0:T(128)S(1)} %pad_maximum_fusion.8, pred[17,16]{0,1:T(8,128)(4,1)S(1)} %copy-done.31), kind=kOutput, calls=%fused_computation.32 | convolution fusion | flops 53756992 | bytes 1608148 | tf_op jit(solution)/shard_map/hcd,dhpn->chpn/dot_general | solution.py:46
  85.2 2.7 %fusion.97 = f32[16,256,256]{2,1,0:T(8,128)} fusion(bf16[16,256,128]{2,1,0:T(8,128)(2,1)S(1)} %bitcast.208, bf16[16,256,128]{2,1,0:T(8,128)(2,1)S(1)} %bitcast.203), kind=kOutput, calls=%fused_computation.194 | convolution fusion | flops 268435456 | bytes 6291456 | tf_op jit(solution)/shard_map/csn,ctn->cst/dot_general | solution.py:71
  87.8 10.1 %collective-permute-done.3 = f32[8,129,128]{2,0,1:T(8,128)S(1)} collective-permute-done((f32[8,129,128]{2,0,1:T(8,128)S(1)}, f32[8,129,128]{2,0,1:T(8,128)S(1)}, u32[]{:S(2)}, u32[]{:S(2)}) %collective-permute-start.3) | collective-permute-done | bytes 528416 | tf_op jit(solution)/shard_map/ppermute | solution.py:167
  100.3 5.2 %fusion.3 = f32[16,2,256,64]{2,3,1,0:T(8,128)} fusion(f32[16,2,256]{2,1,0:T(2,128)S(1)} %bitcast.242, f32[16,256,256]{2,1,0:T(8,128)S(1)} %copy-done.2, pred[16,256,256]{2,1,0:T(8,128)(4,1)} %and_and_fusion, bf16[16,256,2,64]{1,0,3,2:T(8,128)(2,1)S(1)} %bitcast.210), kind=kOutput, calls=%fused_computation.6 | convolution fusion | flops 276824064 | bytes 8421376 | tf_op jit(solution)/shard_map/chst,cshp->cthp/dot_general | solution.py:82
  105.5 9.7 %collective-permute-done.4 = f32[8,129,128]{2,0,1:T(8,128)S(1)} collective-permute-done((f32[8,129,128]{2,0,1:T(8,128)S(1)}, f32[8,129,128]{2,0,1:T(8,128)S(1)}, u32[]{:S(2)}, u32[]{:S(2)}) %collective-permute-start.4) | collective-permute-done | bytes 528416 | tf_op jit(solution)/shard_map/ppermute | solution.py:167
  116.8 2.0 %collective-permute-start.5 = (f32[8,129,128]{2,0,1:T(8,128)}, f32[8,129,128]{2,0,1:T(8,128)}, u32[]{:S(2)}, u32[]{:S(2)}) collective-permute-start(f32[8,129,128]{2,0,1:T(8,128)} %pad_maximum_fusion.2), channel_id=1, source_target_pairs={{128,0},{136,8},{144,16},{152,24},{160,32},{168,40},{176,48},{184,... | collective-permute-start | bytes 1585160 | tf_op jit(solution)/shard_map/ppermute | solution.py:167
  118.8 1.5 %fusion.16 = bf16[16,256,2,64]{1,3,2,0:T(8,128)(2,1)} fusion(f32[16,2,256,64]{2,3,1,0:T(8,128)S(1)} %copy-done.13, bf16[16,256,128,1]{2,1,3,0:T(8,128)(2,1)S(1)} %bitcast.204, f32[16,256,2]{1,2,0:T(2,128)S(1)} %get-tuple-element.38, bf16[16,2,64,128]{3,0,2,1:T(8,128)(2,1)S(1)} %copy-done.14), kind=kOutput, calls=%fused_computation.22 | convolution fusion | flops 135790592 | bytes 4751360 | tf_op jit(solution)/shard_map/chpn,ctn->cthp/dot_general | solution.py:85
  120.2 4.5 %copy.399 = bf16[16,256,2,64]{3,2,1,0:T(2,128)(2,1)S(1)} copy(bf16[16,256,2,64]{1,3,2,0:T(8,128)(2,1)} %fusion.16) | data formatting | bytes 2097152
  124.8 1.8 %reshape.418 = bf16[4096,128]{1,0:T(8,128)(2,1)} reshape(bf16[16,256,2,64]{3,2,1,0:T(2,128)(2,1)S(1)} %copy.399) | data formatting | bytes 2097152
  126.6 6.3 %collective-permute-done.5 = f32[8,129,128]{2,0,1:T(8,128)} collective-permute-done((f32[8,129,128]{2,0,1:T(8,128)}, f32[8,129,128]{2,0,1:T(8,128)}, u32[]{:S(2)}, u32[]{:S(2)}) %collective-permute-start.5) | collective-permute-done | bytes 528416 | tf_op jit(solution)/shard_map/ppermute | solution.py:167
  134.8 2.2 %bitcast_multiply_fusion.1 = f32[1024,8,64]{0,2,1:T(8,128)S(1)} fusion(f32[1024,8]{0,1:T(8,128)S(1)} %exponential_bitcast_fusion, bf16[1024,128]{1,0:T(8,128)(2,1)} %param.10, f32[8,64,128]{2,1,0:T(8,128)S(1)} %copy_add_fusion.1, f32[8,64,128]{2,0,1:T(8,128)S(1)} %get-tuple-element.32, f32[8,64,128]{2,0,1:T(8,128)S(1)} %get-tuple-element.31, ...), kind=kOutput, calls=%fused_computation.25 | convolution fusion | flops 135856128 | bytes 4227237 | tf_op jit(solution)/shard_map/hpn,tn->thp/dot_general | solution.py:189
  137.4 1.3 copy.382
  (223 shorter events, 41.4 us)
Async XLA Ops:
  0.6 84.5 %copy-start = (bf16[4096,128]{1,0:T(8,128)(2,1)S(1)}, bf16[4096,128]{1,0:T(8,128)(2,1)}, u32[]{:S(2)}) copy-start(bf16[4096,128]{1,0:T(8,128)(2,1)} %param.14) | copy-start | bytes 3145732
  0.6 3.3 %copy-start.18 = (s32[4096]{0:T(1024)S(1)}, s32[4096]{0:T(1024)}, u32[]{:S(2)}) copy-start(s32[4096]{0:T(1024)} %param.17) | copy-start | bytes 49156
  0.7 3.4 %copy-start.20 = (f32[2,4096]{1,0:T(2,128)S(1)}, f32[2,4096]{1,0:T(2,128)}, u32[]{:S(2)}) copy-start(f32[2,4096]{1,0:T(2,128)} %param.16) | copy-start | bytes 98308
  2.3 3.8 %copy-start.27 = (pred[4096]{0:T(1024)(128)(4,1)}, pred[4096]{0:T(1024)(128)(4,1)S(1)}, u32[]{:S(2)}) copy-start(pred[4096]{0:T(1024)(128)(4,1)S(1)} %broadcast_compare_fusion.1) | copy-start | bytes 12292
  2.3 3.9 %copy-start.3 = (bf16[4096,128]{1,0:T(8,128)(2,1)S(1)}, bf16[4096,128]{1,0:T(8,128)(2,1)}, u32[]{:S(2)}) copy-start(bf16[4096,128]{1,0:T(8,128)(2,1)} %param.15) | copy-start | bytes 3145732
  5.7 9.5 %copy-start.24 = (f32[8,1024]{1,0:T(8,128)S(1)}, f32[8,1024]{1,0:T(8,128)}, u32[]{:S(2)}) copy-start(f32[8,1024]{1,0:T(8,128)} %param.12) | copy-start | bytes 98308
  6.1 13.5 %copy-start.44 = (f32[4]{0:T(128)S(1)}, f32[4]{0:T(128)}, u32[]{:S(2)}) copy-start(f32[4]{0:T(128)} %constant.37.clone.1) | copy-start | bytes 52
  6.1 14.3 %copy-start.41 = (f32[5]{0:T(128)S(1)}, f32[5]{0:T(128)}, u32[]{:S(2)}) copy-start(f32[5]{0:T(128)} %constant.63.clone.1) | copy-start | bytes 64
  7.3 45.3 %collective-permute-start = (f32[2,64,128]{2,1,0:T(8,128)}, f32[2,64,128]{2,1,0:T(8,128)S(1)}, u32[]{:S(2)}, u32[]{:S(2)}) collective-permute-start(f32[2,64,128]{2,1,0:T(8,128)} %fusion.20), channel_id=1, source_target_pairs={{0,0},{1,32},{2,64},{3,96},{4,128},{5,160},{6,192},{7,224},{8,8},{... | collective-permute-start | bytes 196616 | tf_op jit(solution)/shard_map/ppermute | solution.py:153
  22.9 3.7 %copy-start.15 = (bf16[1024,128]{1,0:T(8,128)(2,1)S(1)}, bf16[1024,128]{1,0:T(8,128)(2,1)}, u32[]{:S(2)}) copy-start(bf16[1024,128]{1,0:T(8,128)(2,1)} %param.11) | copy-start | bytes 786436
  40.9 6.4 %copy-start.5 = (bf16[16,8,16,256]{3,2,1,0:T(8,128)(2,1)}, bf16[16,8,16,256]{3,2,1,0:T(8,128)(2,1)S(1)}, u32[]{:S(2)}) copy-start(bf16[16,8,16,256]{3,2,1,0:T(8,128)(2,1)S(1)} %copy.421) | copy-start | bytes 3145732
  40.9 6.0 %copy-start.12 = (bf16[1024,128]{1,0:T(8,128)(2,1)S(1)}, bf16[1024,128]{1,0:T(8,128)(2,1)}, u32[]{:S(2)}) copy-start(bf16[1024,128]{1,0:T(8,128)(2,1)} %param.10) | copy-start | bytes 786436
  40.9 6.0 %copy-start.16 = (bf16[1024,128]{1,0:T(8,128)(2,1)S(1)}, bf16[1024,128]{1,0:T(8,128)(2,1)}, u32[]{:S(2)}) copy-start(bf16[1024,128]{1,0:T(8,128)(2,1)} %param.11) | copy-start | bytes 786436
  48.4 3.7 %copy-start.43 = (s32[4]{0:T(128)S(1)}, s32[4]{0:T(128)}, u32[]{:S(2)}) copy-start(s32[4]{0:T(128)} %fusion.78) | copy-start | bytes 52
  48.4 4.3 %copy-start.42 = (f32[8]{0:T(128)S(1)}, f32[8]{0:T(128)}, u32[]{:S(2)}) copy-start(f32[8]{0:T(128)} %exponential_bitcast_fusion.1) | copy-start | bytes 100
  48.4 4.3 %copy-start.17 = (f32[8,64,128]{2,0,1:T(8,128)S(1)}, f32[8,64,128]{2,0,1:T(8,128)}, u32[]{:S(2)}) copy-start(f32[8,64,128]{2,0,1:T(8,128)} %copy.343) | copy-start | bytes 786436
  53.5 5.0 %collective-permute-start.1 = (f32[8,81,128]{2,0,1:T(8,128)}, f32[8,81,128]{2,0,1:T(8,128)}, u32[]{:S(2)}, u32[]{:S(2)}) collective-permute-start(f32[8,81,128]{2,0,1:T(8,128)} %pad_maximum_fusion.4), channel_id=1, source_target_pairs={{8,0},{16,8},{24,16},{32,24},{40,32},{48,40},{56,48},{64,56},{72,6... | collective-permute-start | bytes 995336 | tf_op jit(solution)/shard_map/ppermute | solution.py:167
  55.7 10.0 %copy-start.40 = (f32[15]{0:T(128)S(1)}, f32[15]{0:T(128)}, u32[]{:S(2)}) copy-start(f32[15]{0:T(128)} %convert_reduce_fusion) | copy-start | bytes 184
  61.4 7.4 %copy-start.36 = (f32[8,1,1]{0,2,1:T(1,128)}, f32[8,1,1]{0,2,1:T(1,128)S(1)}, u32[]{:S(2)}) copy-start(f32[8,1,1]{0,2,1:T(1,128)S(1)} %get-tuple-element.28) | copy-start | bytes 100
  65.7 11.8 %collective-permute-start.2 = (f32[8,97,128]{2,0,1:T(8,128)}, f32[8,97,128]{2,0,1:T(8,128)S(1)}, u32[]{:S(2)}, u32[]{:S(2)}) collective-permute-start(f32[8,97,128]{2,0,1:T(8,128)} %pad_maximum_fusion.3), channel_id=1, source_target_pairs={{16,0},{24,8},{32,16},{40,24},{48,32},{56,40},{64,48},{72,56},{80,... | collective-permute-start | bytes 1191944 | tf_op jit(solution)/shard_map/ppermute | solution.py:167
  70.7 9.4 %copy-start.34 = (f32[8,1]{0,1:T(1,128)S(1)}, f32[8,1]{0,1:T(1,128)}, u32[]{:S(2)}) copy-start(f32[8,1]{0,1:T(1,128)} %copy-done.33) | copy-start | bytes 100
  70.7 9.4 %copy-start.37 = (f32[8,1,1]{0,2,1:T(1,128)S(1)}, f32[8,1,1]{0,2,1:T(1,128)}, u32[]{:S(2)}) copy-start(f32[8,1,1]{0,2,1:T(1,128)} %copy-done.36) | copy-start | bytes 100
  70.8 10.2 %copy-start.38 = (f32[8]{0:T(128)S(1)}, f32[8]{0:T(128)}, u32[]{:S(2)}) copy-start(f32[8]{0:T(128)} %get-tuple-element.27) | copy-start | bytes 100
  79.0 3.1 %copy-start.25 = (f32[2,17,16]{1,2,0:T(8,128)S(1)}, f32[2,17,16]{1,2,0:T(8,128)}, u32[]{:S(2)}) copy-start(f32[2,17,16]{1,2,0:T(8,128)} %select_reduce_fusion.1) | copy-start | bytes 6532
  81.9 3.2 %copy-start.4 = (bf16[4096,128]{1,0:T(8,128)(2,1)S(1)}, bf16[4096,128]{1,0:T(8,128)(2,1)}, u32[]{:S(2)}) copy-start(bf16[4096,128]{1,0:T(8,128)(2,1)} %param.15) | copy-start | bytes 3145732
  82.0 15.9 %collective-permute-start.3 = (f32[8,129,128]{2,0,1:T(8,128)S(1)}, f32[8,129,128]{2,0,1:T(8,128)S(1)}, u32[]{:S(2)}, u32[]{:S(2)}) collective-permute-start(f32[8,129,128]{2,0,1:T(8,128)S(1)} %pad_maximum_fusion), channel_id=1, source_target_pairs={{32,0},{40,8},{48,16},{56,24},{64,32},{72,40},{80,48},{88,56},{96,... | collective-permute-start | bytes 1585160 | tf_op jit(solution)/shard_map/ppermute | solution.py:167
  85.2 14.2 %copy-start.6 = (bf16[16,8,16,256]{3,2,1,0:T(8,128)(2,1)S(1)}, bf16[16,8,16,256]{3,2,1,0:T(8,128)(2,1)}, u32[]{:S(2)}) copy-start(bf16[16,8,16,256]{3,2,1,0:T(8,128)(2,1)} %copy-done.5) | copy-start | bytes 3145732
  99.2 16.0 %collective-permute-start.4 = (f32[8,129,128]{2,0,1:T(8,128)S(1)}, f32[8,129,128]{2,0,1:T(8,128)S(1)}, u32[]{:S(2)}, u32[]{:S(2)}) collective-permute-start(f32[8,129,128]{2,0,1:T(8,128)S(1)} %pad_maximum_fusion.1), channel_id=1, source_target_pairs={{64,0},{72,8},{80,16},{88,24},{96,32},{104,40},{112,48},{120,56},{... | collective-permute-start | bytes 1585160 | tf_op jit(solution)/shard_map/ppermute | solution.py:167
  115.2 3.5 %copy-start.11 = (f32[8,64,128]{2,0,1:T(8,128)}, f32[8,64,128]{2,0,1:T(8,128)S(1)}, u32[]{:S(2)}) copy-start(f32[8,64,128]{2,0,1:T(8,128)S(1)} %get-tuple-element.33) | copy-start | bytes 786436
  115.3 3.5 %copy-start.14 = (bf16[16,2,64,128]{3,0,2,1:T(8,128)(2,1)S(1)}, bf16[16,2,64,128]{3,0,2,1:T(8,128)(2,1)}, u32[]{:S(2)}) copy-start(bf16[16,2,64,128]{3,0,2,1:T(8,128)(2,1)} %slice.180) | copy-start | bytes 1572868
  115.6 3.2 %copy-start.13 = (f32[16,2,256,64]{2,3,1,0:T(8,128)S(1)}, f32[16,2,256,64]{2,3,1,0:T(8,128)}, u32[]{:S(2)}) copy-start(f32[16,2,256,64]{2,3,1,0:T(8,128)} %fusion.3) | copy-start | bytes 6291460
  116.8 16.1 %collective-permute-start.5 = (f32[8,129,128]{2,0,1:T(8,128)}, f32[8,129,128]{2,0,1:T(8,128)}, u32[]{:S(2)}, u32[]{:S(2)}) collective-permute-start(f32[8,129,128]{2,0,1:T(8,128)} %pad_maximum_fusion.2), channel_id=1, source_target_pairs={{128,0},{136,8},{144,16},{152,24},{160,32},{168,40},{176,48},{184,... | collective-permute-start | bytes 1585160 | tf_op jit(solution)/shard_map/ppermute | solution.py:167
  (20 other events, 30.3 us)

commit v6 on v5

--- a/solution.py
+++ b/solution.py
@@ -150,6 +150,7 @@
             dst_seq = share * src_resp + src_seq % share
             dst_resp = src_seq // share
             pairs.append((src_seq * resp_len + src_resp, dst_seq * resp_len + dst_resp))
+    partial_state, cum_sums = lax.optimization_barrier((partial_state, cum_sums))
     pieces = lax.ppermute(partial_state, ("seq", "resp"), pairs)[None]
     whole_b = start_grad
     whole_a = jnp.exp(shard_total)

time: 141 us -> 142 us (level)
    unnamed x110 -> x112, local copies, waits for them, and re-layouts: 19.7 us -> 19.5 us
  transfers between devices with their start and end apart: 6 -> 6, of which waited for: 5 -> 5; matrix products, arithmetic and copies ran while one was open for 48% -> 45% of each run, Pallas kernels for 0% -> 0%
where the time goes in v6:
time: 142 us; the launch traced here: 139 us
  local copies, waits for them, and re-layouts  43.9 us (31%)
  waiting for transfers between devices  32.9 us (23%)
  other arithmetic  26.9 us (19%)
  matrix products  24.7 us (17%)
  starting transfers between devices  9.44 us (7%)
  between operations  1.55 us (1%)
    ppermute x5, waiting for transfers between devices, on_device(): got = lax.ppermute(jnp.concatenate(parts, axis=1), 'seq', pairs)  32.9 us
    unnamed x112, local copies, waits for them, and re-layouts  19.5 us
    dot_general x2, matrix products, group_output(): jnp.einsum('chst,cshp->cthp', mixing, grad_group, preferred_element_type=...  8.77 us
    ppermute x1, starting transfers between devices, on_device(): pieces = lax.ppermute(partial_state, ('seq', 'resp'), pairs)[None]  7.25 us
    dot_general x2, matrix products, group_parts(): jnp.einsum('hcd,dhpn->chpn', coef, states, precision=lax.Precision.HIGHEST)  4.5 us
    another operation x6, other arithmetic  4.03 us
    slice x5, local copies, waits for them, and re-layouts, on_device(): got_b = jnp.where(valid, got[:, :P_SIZE], 0.0)  3.78 us
    dot_general x2, matrix products, group_output(): jnp.einsum('chpn,ctn->cthp', end_grads.astype(jnp.bfloat16), key_group, p...  2.99 us
  transfers between devices with their start and end apart: 6, of which 5 were waited for; matrix products, arithmetic and copies ran while one was open for 45% of the time, Pallas kernels for 0%

profile of v6, /device:TPU:14, one launch (start us, length us, event | category | flops | bytes accessed | tf_op | source)
XLA Modules:
  0.0 139.3 jit_solution(12435417407404799448)
XLA Ops:
  3.1 2.3 %reduce-window.14 = f32[8,8,128]{2,1,0:T(8,128)S(1)} reduce-window(f32[8,8,128]{2,1,0:T(8,128)S(1)} %copy.326, f32[]{:T(128)} %constant.35.clone.1), window={size=1x1x128 pad=0_0x0_0x127_0}, to_apply=%region_0.0 | reduce-window | flops 1040384 | bytes 65540 | tf_op jit(solution)/shard_map/reduce-window
  5.6 1.6 %copy.342 = bf16[4096,128]{0,1:T(8,128)(2,1)S(1)} copy(bf16[4096,128]{1,0:T(8,128)(2,1)} %param.13) | data formatting | bytes 2097152 | tf_op args[4]
  10.6 7.3 %collective-permute-start = (f32[2,64,128]{2,1,0:T(8,128)}, f32[2,64,128]{2,1,0:T(8,128)S(1)}, u32[]{:S(2)}, u32[]{:S(2)}) collective-permute-start(f32[2,64,128]{2,1,0:T(8,128)} %fusion.20), channel_id=1, source_target_pairs={{0,0},{1,32},{2,64},{3,96},{4,128},{5,160},{6,192},{7,224},{8,8},{... | collective-permute-start | bytes 196616 | tf_op jit(solution)/shard_map/ppermute | solution.py:154
  21.3 2.3 %copy.330 = bf16[1024,512]{0,1:T(8,128)(2,1)} copy(bf16[1024,512]{1,0:T(8,128)(2,1)} %param.9) | data formatting | bytes 2097152 | tf_op args[0]
  23.6 1.9 %reshape.386 = bf16[4,256,8,64]{1,0,3,2:T(4,128)(2,1)S(1)} reshape(bf16[1024,512]{0,1:T(8,128)(2,1)} %copy.330) | data formatting | bytes 2097152 | tf_op jit(solution)/shard_map/reshape | solution.py:24
  25.5 1.4 fusion.65
  27.7 2.5 %convolution_bitcast_fusion = f32[5,8,64,128]{3,0,2,1:T(8,128)S(1)} fusion(f32[8,5,4,1]{1,2,3,0:T(4,128)S(1)} %copy.385, f32[4,8,64,128]{3,2,1,0:T(8,128)S(1)} %fusion.28), kind=kOutput, calls=%fused_computation.30 | convolution fusion | flops 15728640 | bytes 2359936 | tf_op jit(solution)/shard_map/hcd,dhpn->chpn/dot_general | solution.py:46
  33.0 1.3 and.129
  41.5 1.1 copy.491
  43.5 1.3 multiply_bitcast_fusion.2
  45.8 1.5 %fusion.32 = f32[4,8,64,256]{3,2,1,0:T(8,128)S(1)} fusion(bf16[4,256,128,1]{2,1,3,0:T(8,128)(2,1)} %bitcast.213, bf16[4,8,64,128]{3,0,2,1:T(4,128)(2,1)} %slice.210), kind=kOutput, calls=%fused_computation.48 | convolution fusion | flops 134217728 | bytes 2883584 | tf_op jit(solution)/shard_map/chpn,ctn->cthp/dot_general | solution.py:85
  48.9 3.6 %fusion.18 = f32[4,256,8,64]{1,3,2,0:T(8,128)} fusion(f32[4,8,64,256]{3,2,1,0:T(8,128)S(1)} %fusion.32, f32[4,8,256]{2,1,0:T(8,128)S(1)} %copy-done.30, f32[4,256,256]{2,1,0:T(8,128)S(1)} %fusion.96, pred[256,256]{1,0:T(8,128)(4,1)S(1)} %copy-done.21, bf16[4,256,8,64]{1,0,3,2:T(4,128)(2,1)S(1)} %copy-done.8, f32[4,256,8]{1,2,0:T(8,128)S(1)} %copy-done.29), kind=kOutput, calls=%fused_computation.27 | convolution fusion | flops 277872640 | bytes 6422528 | tf_op jit(solution)/shard_map/chst,cshp->cthp/dot_general | solution.py:82
  54.6 1.7 %fusion.24 = f32[16,2,64,128]{3,2,1,0:T(8,128)S(1)} fusion(bf16[16,256,128,1]{2,1,3,0:T(8,128)(2,1)} %bitcast.205, bf16[16,256,2,64]{1,0,3,2:T(8,128)(2,1)S(1)} %multiply_convert_fusion.4), kind=kOutput, calls=%fused_computation.37 | convolution fusion | flops 134217728 | bytes 3145728 | tf_op jit(solution)/shard_map/clhp,cln->chpn/dot_general | solution.py:29
  56.3 2.6 %collective-permute-done.1 = f32[8,81,128]{2,0,1:T(8,128)} collective-permute-done((f32[8,81,128]{2,0,1:T(8,128)}, f32[8,81,128]{2,0,1:T(8,128)}, u32[]{:S(2)}, u32[]{:S(2)}) %collective-permute-start.1) | collective-permute-done | bytes 331808 | tf_op jit(solution)/shard_map/ppermute | solution.py:168
  60.7 1.2 bitcast_multiply_fusion.6
  62.5 1.7 %slice.158 = f32[8,64,128]{2,0,1:T(8,128)} slice(f32[8,81,128]{2,0,1:T(8,128)} %collective-permute-done.1), slice={[0:8], [0:64], [0:128]} | slice | bytes 524288 | tf_op jit(solution)/shard_map/slice | solution.py:170
  66.4 2.9 %copy.340 = f32[4,256,8,64]{1,0,3,2:T(4,128)S(1)} copy(f32[4,256,8,64]{1,3,2,0:T(8,128)} %fusion.18) | data formatting | bytes 4194304 | tf_op jit(solution)/shard_map/add | solution.py:96
  69.4 1.8 %copy.417 = f32[64,8,4,256]{3,1,2,0:T(8,128)} copy(f32[64,8,4,256]{3,2,1,0:T(4,128)S(1)} %bitcast.204) | data formatting | bytes 4194304
  71.4 2.5 %and_and_fusion = pred[16,256,256]{2,1,0:T(8,128)(4,1)} fusion(s32[16,256]{1,0:T(8,128)S(1)} %eq.82, pred[16,256]{1,0:T(8,128)(4,1)S(1)} %copy-done.27, pred[256,256]{1,0:T(8,128)(4,1)S(1)} %copy-done.22), kind=kLoop, calls=%fused_computation.16 | loop fusion | flops 3145728 | bytes 1134592 | tf_op jit(solution)/shard_map/and | solution.py:75
  73.8 4.2 %collective-permute-done.2 = f32[8,97,128]{2,0,1:T(8,128)S(1)} collective-permute-done((f32[8,97,128]{2,0,1:T(8,128)}, f32[8,97,128]{2,0,1:T(8,128)S(1)}, u32[]{:S(2)}, u32[]{:S(2)}) %collective-permute-start.2) | collective-permute-done | bytes 397344 | tf_op jit(solution)/shard_map/ppermute | solution.py:168
  82.7 2.0 %fusion.19 = bf16[17,2,64,128]{3,0,2,1:T(8,128)(2,1)S(1)} fusion(f32[16,2,64,128]{3,2,1,0:T(8,128)S(1)} %fusion.24, f32[2,17,16]{1,2,0:T(8,128)S(1)} %copy-done.26, f32[17]{0:T(128)S(1)} %pad_maximum_fusion.8, pred[17,16]{0,1:T(8,128)(4,1)S(1)} %copy-done.32), kind=kOutput, calls=%fused_computation.32 | convolution fusion | flops 53756992 | bytes 1608148 | tf_op jit(solution)/shard_map/hcd,dhpn->chpn/dot_general | solution.py:46
  85.7 2.7 %fusion.97 = f32[16,256,256]{2,1,0:T(8,128)} fusion(bf16[16,256,128]{2,1,0:T(8,128)(2,1)S(1)} %bitcast.206, bf16[16,256,128]{2,1,0:T(8,128)(2,1)S(1)} %bitcast.201), kind=kOutput, calls=%fused_computation.194 | convolution fusion | flops 268435456 | bytes 6291456 | tf_op jit(solution)/shard_map/csn,ctn->cst/dot_general | solution.py:71
  88.4 10.1 %collective-permute-done.3 = f32[8,129,128]{2,0,1:T(8,128)S(1)} collective-permute-done((f32[8,129,128]{2,0,1:T(8,128)S(1)}, f32[8,129,128]{2,0,1:T(8,128)S(1)}, u32[]{:S(2)}, u32[]{:S(2)}) %collective-permute-start.3) | collective-permute-done | bytes 528416 | tf_op jit(solution)/shard_map/ppermute | solution.py:168
  100.9 5.1 %fusion.3 = f32[16,2,256,64]{2,3,1,0:T(8,128)} fusion(f32[16,2,256]{2,1,0:T(2,128)S(1)} %bitcast.241, f32[16,256,256]{2,1,0:T(8,128)S(1)} %copy-done.2, pred[16,256,256]{2,1,0:T(8,128)(4,1)} %and_and_fusion, bf16[16,256,2,64]{1,0,3,2:T(8,128)(2,1)S(1)} %bitcast.208), kind=kOutput, calls=%fused_computation.6 | convolution fusion | flops 276824064 | bytes 8421376 | tf_op jit(solution)/shard_map/chst,cshp->cthp/dot_general | solution.py:82
  106.1 9.7 %collective-permute-done.4 = f32[8,129,128]{2,0,1:T(8,128)S(1)} collective-permute-done((f32[8,129,128]{2,0,1:T(8,128)S(1)}, f32[8,129,128]{2,0,1:T(8,128)S(1)}, u32[]{:S(2)}, u32[]{:S(2)}) %collective-permute-start.4) | collective-permute-done | bytes 528416 | tf_op jit(solution)/shard_map/ppermute | solution.py:168
  117.3 2.0 %collective-permute-start.5 = (f32[8,129,128]{2,0,1:T(8,128)}, f32[8,129,128]{2,0,1:T(8,128)}, u32[]{:S(2)}, u32[]{:S(2)}) collective-permute-start(f32[8,129,128]{2,0,1:T(8,128)} %pad_maximum_fusion.2), channel_id=1, source_target_pairs={{128,0},{136,8},{144,16},{152,24},{160,32},{168,40},{176,48},{184,... | collective-permute-start | bytes 1585160 | tf_op jit(solution)/shard_map/ppermute | solution.py:168
  119.3 1.5 %fusion.16 = bf16[16,256,2,64]{1,3,2,0:T(8,128)(2,1)} fusion(f32[16,2,256,64]{2,3,1,0:T(8,128)S(1)} %copy-done.13, bf16[16,256,128,1]{2,1,3,0:T(8,128)(2,1)S(1)} %bitcast.202, f32[16,256,2]{1,2,0:T(2,128)S(1)} %get-tuple-element.42, bf16[16,2,64,128]{3,0,2,1:T(8,128)(2,1)S(1)} %copy-done.14), kind=kOutput, calls=%fused_computation.22 | convolution fusion | flops 135790592 | bytes 4751360 | tf_op jit(solution)/shard_map/chpn,ctn->cthp/dot_general | solution.py:85
  120.8 4.5 %copy.399 = bf16[16,256,2,64]{3,2,1,0:T(2,128)(2,1)S(1)} copy(bf16[16,256,2,64]{1,3,2,0:T(8,128)(2,1)} %fusion.16) | data formatting | bytes 2097152
  125.3 1.8 %reshape.418 = bf16[4096,128]{1,0:T(8,128)(2,1)} reshape(bf16[16,256,2,64]{3,2,1,0:T(2,128)(2,1)S(1)} %copy.399) | data formatting | bytes 2097152
  127.2 6.3 %collective-permute-done.5 = f32[8,129,128]{2,0,1:T(8,128)} collective-permute-done((f32[8,129,128]{2,0,1:T(8,128)}, f32[8,129,128]{2,0,1:T(8,128)}, u32[]{:S(2)}, u32[]{:S(2)}) %collective-permute-start.5) | collective-permute-done | bytes 528416 | tf_op jit(solution)/shard_map/ppermute | solution.py:168
  135.3 2.2 %bitcast_multiply_fusion.1 = f32[1024,8,64]{0,2,1:T(8,128)S(1)} fusion(f32[1024,8]{0,1:T(8,128)S(1)} %exponential_bitcast_fusion, bf16[1024,128]{1,0:T(8,128)(2,1)} %param.10, f32[8,64,128]{2,1,0:T(8,128)S(1)} %copy_add_fusion.1, f32[8,64,128]{2,0,1:T(8,128)S(1)} %get-tuple-element.36, f32[8,64,128]{2,0,1:T(8,128)S(1)} %get-tuple-element.35, ...), kind=kOutput, calls=%fused_computation.25 | convolution fusion | flops 135856128 | bytes 4227237 | tf_op jit(solution)/shard_map/hpn,tn->thp/dot_general | solution.py:190
  138.0 1.3 copy.382
  (225 shorter events, 42.0 us)
Async XLA Ops:
  0.6 85.1 %copy-start = (bf16[4096,128]{1,0:T(8,128)(2,1)S(1)}, bf16[4096,128]{1,0:T(8,128)(2,1)}, u32[]{:S(2)}) copy-start(bf16[4096,128]{1,0:T(8,128)(2,1)} %param.14) | copy-start | bytes 3145732
  0.6 6.7 %copy-start.18 = (s32[4096]{0:T(1024)S(1)}, s32[4096]{0:T(1024)}, u32[]{:S(2)}) copy-start(s32[4096]{0:T(1024)} %param.17) | copy-start | bytes 49156
  0.7 6.7 %copy-start.20 = (f32[2,4096]{1,0:T(2,128)S(1)}, f32[2,4096]{1,0:T(2,128)}, u32[]{:S(2)}) copy-start(f32[2,4096]{1,0:T(2,128)} %param.16) | copy-start | bytes 98308
  2.3 7.2 %copy-start.28 = (pred[4096]{0:T(1024)(128)(4,1)}, pred[4096]{0:T(1024)(128)(4,1)S(1)}, u32[]{:S(2)}) copy-start(pred[4096]{0:T(1024)(128)(4,1)S(1)} %broadcast_compare_fusion.1) | copy-start | bytes 12292
  5.6 3.9 %copy-start.3 = (bf16[4096,128]{1,0:T(8,128)(2,1)S(1)}, bf16[4096,128]{1,0:T(8,128)(2,1)}, u32[]{:S(2)}) copy-start(bf16[4096,128]{1,0:T(8,128)(2,1)} %param.15) | copy-start | bytes 3145732
  9.0 10.3 %copy-start.23 = (f32[1,8,8,128]{3,1,2,0:T(8,128)}, f32[1,8,8,128]{3,1,2,0:T(8,128)S(1)}, u32[]{:S(2)}) copy-start(f32[1,8,8,128]{3,1,2,0:T(8,128)S(1)} %copy.493) | copy-start | bytes 98308
  9.0 10.6 %copy-start.25 = (f32[8,1024]{1,0:T(8,128)S(1)}, f32[8,1024]{1,0:T(8,128)}, u32[]{:S(2)}) copy-start(f32[8,1024]{1,0:T(8,128)} %param.12) | copy-start | bytes 98308
  9.5 10.9 %copy-start.45 = (f32[4]{0:T(128)S(1)}, f32[4]{0:T(128)}, u32[]{:S(2)}) copy-start(f32[4]{0:T(128)} %constant.37.clone.1) | copy-start | bytes 52
  9.5 11.6 %copy-start.42 = (f32[5]{0:T(128)S(1)}, f32[5]{0:T(128)}, u32[]{:S(2)}) copy-start(f32[5]{0:T(128)} %constant.63.clone.1) | copy-start | bytes 64
  10.6 42.5 %collective-permute-start = (f32[2,64,128]{2,1,0:T(8,128)}, f32[2,64,128]{2,1,0:T(8,128)S(1)}, u32[]{:S(2)}, u32[]{:S(2)}) collective-permute-start(f32[2,64,128]{2,1,0:T(8,128)} %fusion.20), channel_id=1, source_target_pairs={{0,0},{1,32},{2,64},{3,96},{4,128},{5,160},{6,192},{7,224},{8,8},{... | collective-permute-start | bytes 196616 | tf_op jit(solution)/shard_map/ppermute | solution.py:154
  23.6 3.7 %copy-start.15 = (bf16[1024,128]{1,0:T(8,128)(2,1)S(1)}, bf16[1024,128]{1,0:T(8,128)(2,1)}, u32[]{:S(2)}) copy-start(bf16[1024,128]{1,0:T(8,128)(2,1)} %param.11) | copy-start | bytes 786436
  41.3 6.4 %copy-start.5 = (bf16[16,8,16,256]{3,2,1,0:T(8,128)(2,1)}, bf16[16,8,16,256]{3,2,1,0:T(8,128)(2,1)S(1)}, u32[]{:S(2)}) copy-start(bf16[16,8,16,256]{3,2,1,0:T(8,128)(2,1)S(1)} %copy.421) | copy-start | bytes 3145732
  41.3 6.1 %copy-start.12 = (bf16[1024,128]{1,0:T(8,128)(2,1)S(1)}, bf16[1024,128]{1,0:T(8,128)(2,1)}, u32[]{:S(2)}) copy-start(bf16[1024,128]{1,0:T(8,128)(2,1)} %param.10) | copy-start | bytes 786436
  41.3 6.1 %copy-start.16 = (bf16[1024,128]{1,0:T(8,128)(2,1)S(1)}, bf16[1024,128]{1,0:T(8,128)(2,1)}, u32[]{:S(2)}) copy-start(bf16[1024,128]{1,0:T(8,128)(2,1)} %param.11) | copy-start | bytes 786436
  48.9 3.7 %copy-start.44 = (s32[4]{0:T(128)S(1)}, s32[4]{0:T(128)}, u32[]{:S(2)}) copy-start(s32[4]{0:T(128)} %fusion.78) | copy-start | bytes 52
  48.9 4.3 %copy-start.43 = (f32[8]{0:T(128)S(1)}, f32[8]{0:T(128)}, u32[]{:S(2)}) copy-start(f32[8]{0:T(128)} %exponential_bitcast_fusion.1) | copy-start | bytes 100
  48.9 4.3 %copy-start.17 = (f32[8,64,128]{2,0,1:T(8,128)S(1)}, f32[8,64,128]{2,0,1:T(8,128)}, u32[]{:S(2)}) copy-start(f32[8,64,128]{2,0,1:T(8,128)} %copy.343) | copy-start | bytes 786436
  54.0 5.0 %collective-permute-start.1 = (f32[8,81,128]{2,0,1:T(8,128)}, f32[8,81,128]{2,0,1:T(8,128)}, u32[]{:S(2)}, u32[]{:S(2)}) collective-permute-start(f32[8,81,128]{2,0,1:T(8,128)} %pad_maximum_fusion.4), channel_id=1, source_target_pairs={{8,0},{16,8},{24,16},{32,24},{40,32},{48,40},{56,48},{64,56},{72,6... | collective-permute-start | bytes 995336 | tf_op jit(solution)/shard_map/ppermute | solution.py:168
  56.3 9.9 %copy-start.41 = (f32[15]{0:T(128)S(1)}, f32[15]{0:T(128)}, u32[]{:S(2)}) copy-start(f32[15]{0:T(128)} %convert_reduce_fusion) | copy-start | bytes 184
  61.9 7.5 %copy-start.37 = (f32[8,1,1]{0,2,1:T(1,128)}, f32[8,1,1]{0,2,1:T(1,128)S(1)}, u32[]{:S(2)}) copy-start(f32[8,1,1]{0,2,1:T(1,128)S(1)} %get-tuple-element.32) | copy-start | bytes 100
  66.3 11.8 %collective-permute-start.2 = (f32[8,97,128]{2,0,1:T(8,128)}, f32[8,97,128]{2,0,1:T(8,128)S(1)}, u32[]{:S(2)}, u32[]{:S(2)}) collective-permute-start(f32[8,97,128]{2,0,1:T(8,128)} %pad_maximum_fusion.3), channel_id=1, source_target_pairs={{16,0},{24,8},{32,16},{40,24},{48,32},{56,40},{64,48},{72,56},{80,... | collective-permute-start | bytes 1191944 | tf_op jit(solution)/shard_map/ppermute | solution.py:168
  71.2 9.4 %copy-start.35 = (f32[8,1]{0,1:T(1,128)S(1)}, f32[8,1]{0,1:T(1,128)}, u32[]{:S(2)}) copy-start(f32[8,1]{0,1:T(1,128)} %copy-done.34) | copy-start | bytes 100
  71.2 9.4 %copy-start.38 = (f32[8,1,1]{0,2,1:T(1,128)S(1)}, f32[8,1,1]{0,2,1:T(1,128)}, u32[]{:S(2)}) copy-start(f32[8,1,1]{0,2,1:T(1,128)} %copy-done.37) | copy-start | bytes 100
  71.4 10.3 %copy-start.39 = (f32[8]{0:T(128)S(1)}, f32[8]{0:T(128)}, u32[]{:S(2)}) copy-start(f32[8]{0:T(128)} %get-tuple-element.31) | copy-start | bytes 100
  82.5 3.2 %copy-start.4 = (bf16[4096,128]{1,0:T(8,128)(2,1)S(1)}, bf16[4096,128]{1,0:T(8,128)(2,1)}, u32[]{:S(2)}) copy-start(bf16[4096,128]{1,0:T(8,128)(2,1)} %param.15) | copy-start | bytes 3145732
  82.6 15.9 %collective-permute-start.3 = (f32[8,129,128]{2,0,1:T(8,128)S(1)}, f32[8,129,128]{2,0,1:T(8,128)S(1)}, u32[]{:S(2)}, u32[]{:S(2)}) collective-permute-start(f32[8,129,128]{2,0,1:T(8,128)S(1)} %pad_maximum_fusion), channel_id=1, source_target_pairs={{32,0},{40,8},{48,16},{56,24},{64,32},{72,40},{80,48},{88,56},{96,... | collective-permute-start | bytes 1585160 | tf_op jit(solution)/shard_map/ppermute | solution.py:168
  85.7 14.2 %copy-start.6 = (bf16[16,8,16,256]{3,2,1,0:T(8,128)(2,1)S(1)}, bf16[16,8,16,256]{3,2,1,0:T(8,128)(2,1)}, u32[]{:S(2)}) copy-start(bf16[16,8,16,256]{3,2,1,0:T(8,128)(2,1)} %copy-done.5) | copy-start | bytes 3145732
  99.8 15.9 %collective-permute-start.4 = (f32[8,129,128]{2,0,1:T(8,128)S(1)}, f32[8,129,128]{2,0,1:T(8,128)S(1)}, u32[]{:S(2)}, u32[]{:S(2)}) collective-permute-start(f32[8,129,128]{2,0,1:T(8,128)S(1)} %pad_maximum_fusion.1), channel_id=1, source_target_pairs={{64,0},{72,8},{80,16},{88,24},{96,32},{104,40},{112,48},{120,56},{... | collective-permute-start | bytes 1585160 | tf_op jit(solution)/shard_map/ppermute | solution.py:168
  115.8 3.5 %copy-start.11 = (f32[8,64,128]{2,0,1:T(8,128)}, f32[8,64,128]{2,0,1:T(8,128)S(1)}, u32[]{:S(2)}) copy-start(f32[8,64,128]{2,0,1:T(8,128)S(1)} %get-tuple-element.37) | copy-start | bytes 786436
  115.8 3.5 %copy-start.14 = (bf16[16,2,64,128]{3,0,2,1:T(8,128)(2,1)S(1)}, bf16[16,2,64,128]{3,0,2,1:T(8,128)(2,1)}, u32[]{:S(2)}) copy-start(bf16[16,2,64,128]{3,0,2,1:T(8,128)(2,1)} %slice.180) | copy-start | bytes 1572868
  116.1 3.2 %copy-start.13 = (f32[16,2,256,64]{2,3,1,0:T(8,128)S(1)}, f32[16,2,256,64]{2,3,1,0:T(8,128)}, u32[]{:S(2)}) copy-start(f32[16,2,256,64]{2,3,1,0:T(8,128)} %fusion.3) | copy-start | bytes 6291460
  117.3 16.1 %collective-permute-start.5 = (f32[8,129,128]{2,0,1:T(8,128)}, f32[8,129,128]{2,0,1:T(8,128)}, u32[]{:S(2)}, u32[]{:S(2)}) collective-permute-start(f32[8,129,128]{2,0,1:T(8,128)} %pad_maximum_fusion.2), channel_id=1, source_target_pairs={{128,0},{136,8},{144,16},{152,24},{160,32},{168,40},{176,48},{184,... | collective-permute-start | bytes 1585160 | tf_op jit(solution)/shard_map/ppermute | solution.py:168
  (21 other events, 33.4 us)

commit v7 on v5

--- a/solution.py
+++ b/solution.py
@@ -127,10 +127,8 @@
     resp_segment,
 ):
     resp_alive = resp_segment < RESP_DEV
-    resp_parts = group_parts(resp_grad, resp_queries, resp_decay, resp_segment, resp_alive)
-    resp_dx = group_output(resp_keys, resp_queries, resp_parts).astype(jnp.bfloat16)
     partial_state = initial_state(
-        resp_grad, resp_queries, resp_decay, resp_segment, resp_alive, resp_parts[0]
+        resp_grad, resp_queries, resp_decay, resp_segment, resp_alive, jnp.cumsum(resp_decay, axis=1)
     )
     resp_len = lax.axis_size("resp")
     head_count = prompt_decay.shape[0]
@@ -164,7 +162,12 @@
             parts.append(pieces.reshape(head_count, -1, N))
         else:
             parts.append(my_heads)
-        got = lax.ppermute(jnp.concatenate(parts, axis=1), "seq", pairs)
+        message = jnp.concatenate(parts, axis=1)
+        if shift == 1:
+            message, resp_grad, resp_keys, prompt_keys, prompt_parts = lax.optimization_barrier(
+                (message, resp_grad, resp_keys, prompt_keys, prompt_parts)
+            )
+        got = lax.ppermute(message, "seq", pairs)
         valid = seq_index + shift < seq_len
         got_b = jnp.where(valid, got[:, :P_SIZE], 0.0)
         got_a = jnp.where(valid, got[:, P_SIZE, 0], 1.0)
@@ -185,7 +188,10 @@
             whole_a = whole_a * got_a
         shift *= 2
     incoming = later_b + later_a[:, None, None] * my_heads
+    resp_parts = group_parts(resp_grad, resp_queries, resp_decay, resp_segment, resp_alive)
+    resp_dx = group_output(resp_keys, resp_queries, resp_parts).astype(jnp.bfloat16)
     local_part = group_output(prompt_keys, prompt_queries, prompt_parts)
+    cum_sums = prompt_parts[0]
     carry_term = jnp.einsum(
         "hpn,tn->thp",
         incoming.astype(jnp.bfloat16),

time: 141 us -> 159 us (1.13)
  local copies, waits for them, and re-layouts: 42.8 us -> 61.1 us
  waiting for transfers between devices: 33 us -> 21.4 us
  matrix products: 24.7 us -> 28.9 us
  other arithmetic: 27.4 us -> 30.9 us
  starting transfers between devices: 9.43 us -> 12.4 us
    ppermute x5, waiting for transfers between devices: 33 us -> 21.4 us  [on_device(): got = lax.ppermute(message, 'seq', pairs)]
    dot_general x0 -> x2, local copies, waits for them, and re-layouts: none -> 8 us  [group_output(): jnp.einsum('csn,ctn->cst', query_group, key_group, preferred_element_type...]
    ppermute x5, starting transfers between devices: 2.18 us -> 5.18 us  [on_device(): got = lax.ppermute(message, 'seq', pairs)]
    broadcast_in_dim x2, local copies, waits for them, and re-layouts: 0.16 us -> 2.44 us  [on_device(): jnp.take(pieces, order, axis=0)]
    optimization_barrier x0 -> x3, local copies, waits for them, and re-layouts: none -> 2.18 us  [on_device(): lax.optimization_barrier((message, resp_grad, resp_keys, prompt_keys, pro...]
    and x1 -> x2, other arithmetic: 2.46 us -> 4.53 us  [group_output(): (row_index >= col_index)[None]]
    squeeze x3 -> x2, local copies, waits for them, and re-layouts: 0.67 us -> 2.59 us  [group_parts(): group_gains = jnp.exp(cum_group[:, :, -1] - before)]
    transpose x0 -> x1, other arithmetic: none -> 1.9 us  [group_output(): reach_weight.transpose(0, 2, 1)[:, :, :, None]]
  transfers between devices with their start and end apart: 6 -> 6, of which waited for: 5 -> 2; matrix products, arithmetic and copies ran while one was open for 48% -> 58% of each run, Pallas kernels for 0% -> 0%
where the time goes in v7:
time: 159 us; the launch traced here: 156 us
  local copies, waits for them, and re-layouts  61.1 us (38%)
  other arithmetic  30.9 us (19%)
  matrix products  28.9 us (18%)
  waiting for transfers between devices  21.4 us (13%)
  starting transfers between devices  12.4 us (8%)
    ppermute x5, waiting for transfers between devices, on_device(): got = lax.ppermute(message, 'seq', pairs)  21.4 us
    unnamed x108, local copies, waits for them, and re-layouts  18.7 us
    dot_general x2, matrix products, group_output(): jnp.einsum('chst,cshp->cthp', mixing, grad_group, preferred_element_type=...  9.36 us
    dot_general x2, local copies, waits for them, and re-layouts, group_output(): jnp.einsum('csn,ctn->cst', query_group, key_group, preferred_element_type...  8 us
    ppermute x1, starting transfers between devices, on_device(): pieces = lax.ppermute(partial_state, ('seq', 'resp'), pairs)[None]  7.25 us
    dot_general x2, matrix products, group_parts(): jnp.einsum('hcd,dhpn->chpn', coef, states, precision=lax.Precision.HIGHEST)  5.39 us
    ppermute x5, starting transfers between devices, on_device(): got = lax.ppermute(message, 'seq', pairs)  5.18 us
    dot_general x2, matrix products, group_output(): jnp.einsum('chpn,ctn->cthp', end_grads.astype(jnp.bfloat16), key_group, p...  4.63 us
  transfers between devices with their start and end apart: 6, of which 2 were waited for; matrix products, arithmetic and copies ran while one was open for 58% of the time, Pallas kernels for 0%

profile of v7, /device:TPU:14, one launch (start us, length us, event | category | flops | bytes accessed | tf_op | source)
XLA Modules:
  0.0 156.2 jit_solution(117702559888059824)
XLA Ops:
  2.3 2.4 %copy.359 = bf16[4096,128]{0,1:T(8,128)(2,1)} copy(bf16[4096,128]{1,0:T(8,128)(2,1)} %param.13) | data formatting | bytes 2097152 | tf_op args[4]
  6.4 2.4 %fusion.18 = f32[2,64,128]{2,1,0:T(8,128)} fusion(bf16[4096,2,64]{0,2,1:T(8,128)(2,1)} %bitcast.213, bf16[4096,128]{1,0:T(8,128)(2,1)S(1)} %copy-done.4, f32[4096,2]{0,1:T(2,128)S(1)} %fusion.58), kind=kOutput, calls=%fused_computation.33 | convolution fusion | flops 135790592 | bytes 2195456 | tf_op jit(solution)/shard_map/thp,tn->hpn/dot_general | solution.py:115
  8.8 7.3 %collective-permute-start = (f32[2,64,128]{2,1,0:T(8,128)}, f32[2,64,128]{2,1,0:T(8,128)S(1)}, u32[]{:S(2)}, u32[]{:S(2)}) collective-permute-start(f32[2,64,128]{2,1,0:T(8,128)} %fusion.18), channel_id=1, source_target_pairs={{0,0},{1,32},{2,64},{3,96},{4,128},{5,160},{6,192},{7,224},{8,8},{... | collective-permute-start | bytes 196616 | tf_op jit(solution)/shard_map/ppermute | solution.py:151
  16.1 2.3 %reduce-window.14 = f32[8,8,128]{2,1,0:T(8,128)S(1)} reduce-window(f32[8,8,128]{2,1,0:T(8,128)S(1)} %copy.350, f32[]{:T(128)} %constant.36.clone.1), window={size=1x1x128 pad=0_0x0_0x127_0}, to_apply=%region_0.0 | reduce-window | flops 1040384 | bytes 65540 | tf_op jit(solution)/shard_map/reduce-window
  21.1 1.9 %reshape.401 = bf16[4,256,8,64]{1,0,3,2:T(4,128)(2,1)S(1)} reshape(bf16[1024,512]{0,1:T(8,128)(2,1)} %copy.354) | data formatting | bytes 2097152 | tf_op jit(solution)/shard_map/reshape | solution.py:24
  24.0 2.5 %convolution_bitcast_fusion.1 = f32[5,8,64,128]{3,0,2,1:T(8,128)S(1)} fusion(f32[8,5,4,1]{1,2,3,0:T(4,128)S(1)} %copy.412, f32[4,8,64,128]{3,2,1,0:T(8,128)S(1)} %fusion.27), kind=kOutput, calls=%fused_computation.28 | convolution fusion | flops 15728640 | bytes 2359936 | tf_op jit(solution)/shard_map/hcd,dhpn->chpn/dot_general | solution.py:46
  40.3 1.3 copy.407
  41.7 1.4 copy.511
  43.0 1.6 %copy.401 = f32[2,16,256]{1,0,2:T(2,128)} copy(f32[2,16,256]{2,1,0:T(8,128)} %bitcast.234) | data formatting | bytes 65536 | tf_op jit(solution)/shard_map/reshape | solution.py:18
  46.7 1.4 copy.402
  48.8 1.5 fusion.62
  50.9 3.4 %and_and_fusion = pred[16,256,256]{2,1,0:T(8,128)(4,1)} fusion(s32[16,256]{1,0:T(8,128)S(1)} %eq.112, pred[16,256]{1,0:T(8,128)(4,1)} %and.154, pred[256,256]{1,0:T(8,128)(4,1)S(1)} %iota_compare_fusion), kind=kLoop, calls=%fused_computation.16 | loop fusion | flops 3145728 | bytes 1134592 | tf_op jit(solution)/shard_map/and | solution.py:75
  61.0 1.5 copy.443
  65.4 2.9 %fusion.17 = bf16[17,2,64,128]{3,0,2,1:T(8,128)(2,1)} fusion(f32[16,2,64,128]{3,2,1,0:T(8,128)S(1)} %fusion.22, f32[2,17,16]{1,2,0:T(8,128)S(1)} %copy-done.33, f32[17]{0:T(128)S(1)} %copy-done.42, pred[17,16]{0,1:T(8,128)(4,1)S(1)} %copy-done.37), kind=kOutput, calls=%fused_computation.32 | convolution fusion | flops 53756992 | bytes 1608148 | tf_op jit(solution)/shard_map/hcd,dhpn->chpn/dot_general | solution.py:46
  68.2 2.7 %convolution_bitcast_fusion = f32[16,256,256]{1,2,0:T(8,128)} fusion(bf16[16,256,128]{2,1,0:T(8,128)(2,1)S(1)} %bitcast.196, bf16[16,256,128]{2,1,0:T(8,128)(2,1)S(1)} %bitcast.205), kind=kOutput, calls=%fused_computation.18 | convolution fusion | flops 268435456 | bytes 6291456 | tf_op jit(solution)/shard_map/csn,ctn->cst/dot_general | solution.py:71
  75.3 1.7 %pad_maximum_fusion.3 = f32[8,97,128]{2,0,1:T(8,128)} fusion(f32[8,32,128]{2,0,1:T(8,128)} %copy.375, f32[8,1,128]{2,0,1:T(8,128)S(1)} %broadcast_in_dim.324, f32[8,64,128]{2,0,1:T(8,128)S(1)} %copy.374), kind=kLoop, calls=%fused_computation.53 | loop fusion | flops 198656 | bytes 794624 | tf_op jit(solution)/shard_map/concatenate | solution.py:165
  77.0 1.9 %select_bitcast_fusion = f32[4,256,8]{2,0,1:T(4,128)} fusion(f32[4,8,256]{1,0,2:T(4,128)S(1)} %bitcast.202, f32[4,8]{1,0:T(4,128)S(1)} %copy-done.38, pred[4,256]{0,1:T(8,128)(4,1)} %broadcast_compare_fusion), kind=kLoop, calls=%fused_computation.52 | loop fusion | flops 16384 | bytes 66688 | tf_op jit(solution)/shard_map/transpose | solution.py:96
  79.7 2.6 %copy.362 = f32[4,256,256]{2,1,0:T(8,128)} copy(f32[4,256,256]{1,2,0:T(8,128)} %convolution_bitcast_fusion.2) | data formatting | bytes 2097152 | tf_op jit(solution)/shard_map/csn,ctn->cst/dot_general | solution.py:71
  82.5 2.2 %slice.182 = bf16[16,2,64,128]{3,0,2,1:T(8,128)(2,1)} slice(bf16[17,2,64,128]{3,0,2,1:T(8,128)(2,1)} %fusion.17), slice={[1:17], [0:2], [0:64], [0:128]} | slice | bytes 1048576 | tf_op jit(solution)/shard_map/slice | solution.py:50
  84.7 5.4 %copy.395 = f32[16,256,256]{2,1,0:T(8,128)} copy(f32[16,256,256]{1,2,0:T(8,128)} %convolution_bitcast_fusion) | data formatting | bytes 8388608 | tf_op jit(solution)/shard_map/csn,ctn->cst/dot_general | solution.py:71
  90.1 1.8 %fusion.32 = f32[4,256,8,64]{1,3,2,0:T(8,128)} fusion(bf16[4,256,128,1]{2,1,3,0:T(8,128)(2,1)S(1)} %bitcast.212, bf16[4,8,64,128]{3,0,2,1:T(4,128)(2,1)S(1)} %copy-done.15), kind=kOutput, calls=%fused_computation.50 | convolution fusion | flops 134217728 | bytes 2883584 | tf_op jit(solution)/shard_map/chpn,ctn->cthp/dot_general | solution.py:85
  98.3 2.8 %fusion.30 = f32[16,256,2,64]{1,3,2,0:T(8,128)} fusion(bf16[16,256,128,1]{2,1,3,0:T(8,128)(2,1)S(1)} %bitcast.195, bf16[16,2,64,128]{3,0,2,1:T(8,128)(2,1)} %slice.182), kind=kOutput, calls=%fused_computation.48 | convolution fusion | flops 134217728 | bytes 3670016 | tf_op jit(solution)/shard_map/chpn,ctn->cthp/dot_general | solution.py:85
  101.2 11.9 %collective-permute-done.3 = f32[8,129,128]{2,0,1:T(8,128)S(1)} collective-permute-done((f32[8,129,128]{2,0,1:T(8,128)S(1)}, f32[8,129,128]{2,0,1:T(8,128)S(1)}, u32[]{:S(2)}, u32[]{:S(2)}) %collective-permute-start.3) | collective-permute-done | bytes 528416 | tf_op jit(solution)/shard_map/ppermute | solution.py:170
  116.4 5.4 %fusion.15 = bf16[16,256,2,64]{1,3,2,0:T(8,128)(2,1)} fusion(f32[16,256,2,64]{1,3,2,0:T(8,128)} %fusion.30, f32[16,2,256]{2,1,0:T(2,128)S(1)} %bitcast.238, f32[16,256,256]{2,1,0:T(8,128)S(1)} %copy-done.2, pred[16,256,256]{2,1,0:T(8,128)(4,1)} %and_and_fusion, bf16[16,256,2,64]{1,0,3,2:T(8,128)(2,1)S(1)} %bitcast.207, f32[16,256,2]{1,2,0:T(2,128)S(1)} %copy-done.36), kind=kOutput, calls=%fused_computation.22 | convolution fusion | flops 278396928 | bytes 9502720 | tf_op jit(solution)/shard_map/chst,cshp->cthp/dot_general | solution.py:82
  121.8 9.5 %collective-permute-done.4 = f32[8,129,128]{2,0,1:T(8,128)S(1)} collective-permute-done((f32[8,129,128]{2,0,1:T(8,128)S(1)}, f32[8,129,128]{2,0,1:T(8,128)S(1)}, u32[]{:S(2)}, u32[]{:S(2)}) %collective-permute-start.4) | collective-permute-done | bytes 528416 | tf_op jit(solution)/shard_map/ppermute | solution.py:170
  132.9 3.9 %collective-permute-start.5 = (f32[8,129,128]{2,0,1:T(8,128)}, f32[8,129,128]{2,0,1:T(8,128)}, u32[]{:S(2)}, u32[]{:S(2)}) collective-permute-start(f32[8,129,128]{2,0,1:T(8,128)} %pad_maximum_fusion.2), channel_id=1, source_target_pairs={{128,0},{136,8},{144,16},{152,24},{160,32},{168,40},{176,48},{184,... | collective-permute-start | bytes 1585160 | tf_op jit(solution)/shard_map/ppermute | solution.py:170
  136.8 4.0 %bitcast_add_fusion.2 = f32[4,256,8,64]{1,3,2,0:T(8,128)S(1)} fusion(f32[4,256,8,64]{1,3,2,0:T(8,128)S(1)} %copy-done.13, f32[4,8,256]{2,1,0:T(8,128)S(1)} %copy-done.34, f32[4,256,256]{2,1,0:T(8,128)} %copy.362, pred[4,256,256]{2,1,0:T(8,128)(4,1)} %and_and_fusion.1, bf16[4,256,8,64]{1,0,3,2:T(4,128)(2,1)S(1)} %copy-done.7, f32[4,256,8]{1,2,0:T(8,128)S(1)} %copy.369), kind=kOutput, calls=%fused_computation.25 | convolution fusion | flops 277872640 | bytes 6619136 | tf_op jit(solution)/shard_map/chst,cshp->cthp/dot_general | solution.py:82
  140.8 1.4 copy.370
  142.1 1.8 %copy.442 = f32[64,8,4,256]{3,1,2,0:T(8,128)} copy(f32[64,8,4,256]{3,2,1,0:T(4,128)S(1)} %bitcast.198) | data formatting | bytes 4194304
  143.9 4.5 %copy.421 = bf16[16,256,2,64]{3,2,1,0:T(2,128)(2,1)S(1)} copy(bf16[16,256,2,64]{1,3,2,0:T(8,128)(2,1)} %fusion.15) | data formatting | bytes 2097152
  148.5 1.8 %reshape.436 = bf16[4096,128]{1,0:T(8,128)(2,1)} reshape(bf16[16,256,2,64]{3,2,1,0:T(2,128)(2,1)S(1)} %copy.421) | data formatting | bytes 2097152
  152.2 2.2 %convolution_multiply_fusion = f32[1024,8,64]{0,2,1:T(8,128)S(1)} fusion(f32[1024,8]{0,1:T(8,128)S(1)} %exponential_bitcast_fusion, bf16[1024,128]{1,0:T(8,128)(2,1)} %param.10, f32[8,64,128]{2,1,0:T(8,128)S(1)} %copy_add_fusion.1, f32[8,64,128]{2,0,1:T(8,128)S(1)} %get-tuple-element.52, f32[8,64,128]{2,0,1:T(8,128)S(1)} %get-tuple-element.51, ...), kind=kOutput, calls=%fused_computation.29 | convolution fusion | flops 135856128 | bytes 4227237 | tf_op jit(solution)/shard_map/hpn,tn->thp/dot_general | solution.py:195
  (233 shorter events, 53.8 us)
Async XLA Ops:
  0.6 67.6 %copy-start = (bf16[4096,128]{1,0:T(8,128)(2,1)S(1)}, bf16[4096,128]{1,0:T(8,128)(2,1)}, u32[]{:S(2)}) copy-start(bf16[4096,128]{1,0:T(8,128)(2,1)} %param.14) | copy-start | bytes 3145732
  0.6 4.1 %copy-start.27 = (s32[4096]{0:T(1024)S(1)}, s32[4096]{0:T(1024)}, u32[]{:S(2)}) copy-start(s32[4096]{0:T(1024)} %param.17) | copy-start | bytes 49156
  0.7 4.1 %copy-start.28 = (f32[2,4096]{1,0:T(2,128)S(1)}, f32[2,4096]{1,0:T(2,128)}, u32[]{:S(2)}) copy-start(f32[2,4096]{1,0:T(2,128)} %param.16) | copy-start | bytes 98308
  2.3 4.1 %copy-start.4 = (bf16[4096,128]{1,0:T(8,128)(2,1)S(1)}, bf16[4096,128]{1,0:T(8,128)(2,1)}, u32[]{:S(2)}) copy-start(bf16[4096,128]{1,0:T(8,128)(2,1)} %param.15) | copy-start | bytes 3145732
  5.4 10.6 %copy-start.32 = (f32[8,1024]{1,0:T(8,128)S(1)}, f32[8,1024]{1,0:T(8,128)}, u32[]{:S(2)}) copy-start(f32[8,1024]{1,0:T(8,128)} %param.12) | copy-start | bytes 98308
  6.3 13.0 %copy-start.44 = (f32[4]{0:T(128)S(1)}, f32[4]{0:T(128)}, u32[]{:S(2)}) copy-start(f32[4]{0:T(128)} %constant.37.clone.1) | copy-start | bytes 52
  6.3 13.2 %copy-start.43 = (f32[5]{0:T(128)S(1)}, f32[5]{0:T(128)}, u32[]{:S(2)}) copy-start(f32[5]{0:T(128)} %constant.39.clone.1) | copy-start | bytes 64
  6.3 13.4 %copy-start.16 = (bf16[1024,512]{1,0:T(8,128)(2,1)S(1)}, bf16[1024,512]{1,0:T(8,128)(2,1)}, u32[]{:S(2)}) copy-start(bf16[1024,512]{1,0:T(8,128)(2,1)} %param.9) | copy-start | bytes 3145732
  8.8 48.8 %collective-permute-start = (f32[2,64,128]{2,1,0:T(8,128)}, f32[2,64,128]{2,1,0:T(8,128)S(1)}, u32[]{:S(2)}, u32[]{:S(2)}) collective-permute-start(f32[2,64,128]{2,1,0:T(8,128)} %fusion.18), channel_id=1, source_target_pairs={{0,0},{1,32},{2,64},{3,96},{4,128},{5,160},{6,192},{7,224},{8,8},{... | collective-permute-start | bytes 196616 | tf_op jit(solution)/shard_map/ppermute | solution.py:151
  27.9 31.8 %copy-start.3 = (bf16[4096,128]{1,0:T(8,128)(2,1)S(1)}, bf16[4096,128]{1,0:T(8,128)(2,1)}, u32[]{:S(2)}) copy-start(bf16[4096,128]{1,0:T(8,128)(2,1)} %param.13) | copy-start | bytes 3145732
  27.9 33.1 %copy-start.18 = (pred[256,256]{1,0:T(8,128)(4,1)}, pred[256,256]{1,0:T(8,128)(4,1)S(1)}, u32[]{:S(2)}) copy-start(pred[256,256]{1,0:T(8,128)(4,1)S(1)} %iota_compare_fusion) | copy-start | bytes 196612
  57.6 4.9 %copy-start.20 = (f32[2,64,128]{2,1,0:T(8,128)}, f32[2,64,128]{2,1,0:T(8,128)S(1)}, u32[]{:S(2)}) copy-start(f32[2,64,128]{2,1,0:T(8,128)S(1)} %collective-permute-done) | copy-start | bytes 196612
  59.7 2.8 %copy-start.12 = (bf16[1024,128]{1,0:T(8,128)(2,1)S(1)}, bf16[1024,128]{1,0:T(8,128)(2,1)}, u32[]{:S(2)}) copy-start(bf16[1024,128]{1,0:T(8,128)(2,1)} %param.10) | copy-start | bytes 786436
  59.7 11.3 %collective-permute-start.1 = (f32[8,81,128]{2,0,1:T(8,128)}, f32[8,81,128]{2,0,1:T(8,128)}, u32[]{:S(2)}, u32[]{:S(2)}) collective-permute-start(f32[8,81,128]{2,0,1:T(8,128)} %pad_maximum_fusion.4), channel_id=1, source_target_pairs={{8,0},{16,8},{24,16},{32,24},{40,32},{48,40},{56,48},{64,56},{72,6... | collective-permute-start | bytes 995336 | tf_op jit(solution)/shard_map/ppermute | solution.py:170
  61.0 3.4 %copy-start.31 = (f32[16,256,2]{1,0,2:T(8,128)S(1)}, f32[16,256,2]{1,0,2:T(8,128)}, u32[]{:S(2)}) copy-start(f32[16,256,2]{1,0,2:T(8,128)} %copy.403) | copy-start | bytes 98308
  68.2 3.6 %copy-start.21 = (f32[2,64,128]{2,1,0:T(8,128)S(1)}, f32[2,64,128]{2,1,0:T(8,128)}, u32[]{:S(2)}) copy-start(f32[2,64,128]{2,1,0:T(8,128)} %copy-done.20) | copy-start | bytes 196612
  68.2 5.1 %copy-start.40 = (f32[8,1]{0,1:T(1,128)S(1)}, f32[8,1]{0,1:T(1,128)}, u32[]{:S(2)}) copy-start(f32[8,1]{0,1:T(1,128)} %copy-done.39) | copy-start | bytes 100
  71.0 6.0 %copy-start.38 = (f32[4,8]{1,0:T(4,128)S(1)}, f32[4,8]{1,0:T(4,128)}, u32[]{:S(2)}) copy-start(f32[4,8]{1,0:T(4,128)} %slice_bitcast_fusion) | copy-start | bytes 388
  77.0 14.9 %collective-permute-start.2 = (f32[8,97,128]{2,0,1:T(8,128)}, f32[8,97,128]{2,0,1:T(8,128)}, u32[]{:S(2)}, u32[]{:S(2)}) collective-permute-start(f32[8,97,128]{2,0,1:T(8,128)} %pad_maximum_fusion.3), channel_id=1, source_target_pairs={{16,0},{24,8},{32,16},{40,24},{48,32},{56,40},{64,48},{72,56},{80,... | collective-permute-start | bytes 1191944 | tf_op jit(solution)/shard_map/ppermute | solution.py:170
  84.7 5.4 %copy-start.15 = (bf16[4,8,64,128]{3,0,2,1:T(4,128)(2,1)S(1)}, bf16[4,8,64,128]{3,0,2,1:T(4,128)(2,1)}, u32[]{:S(2)}) copy-start(bf16[4,8,64,128]{3,0,2,1:T(4,128)(2,1)} %slice.159) | copy-start | bytes 1572868
  90.1 2.8 %copy-start.22 = (f32[2,64,128]{2,1,0:T(8,128)S(1)}, f32[2,64,128]{2,1,0:T(8,128)}, u32[]{:S(2)}) copy-start(f32[2,64,128]{2,1,0:T(8,128)} %copy-done.20) | copy-start | bytes 196612
  90.1 2.8 %copy-start.24 = (f32[8,16,128]{2,1,0:T(8,128)S(1)}, f32[8,16,128]{2,1,0:T(8,128)}, u32[]{:S(2)}) copy-start(f32[8,16,128]{2,1,0:T(8,128)} %copy-done.23) | copy-start | bytes 196612
  90.1 3.5 %copy-start.41 = (pred[8]{0:T(512)(128)(4,1)S(1)}, pred[8]{0:T(512)(128)(4,1)}, u32[]{:S(2)}) copy-start(pred[8]{0:T(512)(128)(4,1)} %broadcast_in_dim.329) | copy-start | bytes 28
  93.6 3.6 %copy-start.19 = (pred[256,256]{1,0:T(8,128)(4,1)S(1)}, pred[256,256]{1,0:T(8,128)(4,1)}, u32[]{:S(2)}) copy-start(pred[256,256]{1,0:T(8,128)(4,1)} %copy-done.18) | copy-start | bytes 196612
  95.6 5.6 %copy-start.9 = (f32[8,64,128]{2,0,1:T(8,128)}, f32[8,64,128]{2,0,1:T(8,128)S(1)}, u32[]{:S(2)}) copy-start(f32[8,64,128]{2,0,1:T(8,128)S(1)} %slice.163) | copy-start | bytes 786436
  96.0 17.0 %collective-permute-start.3 = (f32[8,129,128]{2,0,1:T(8,128)S(1)}, f32[8,129,128]{2,0,1:T(8,128)S(1)}, u32[]{:S(2)}, u32[]{:S(2)}) collective-permute-start(f32[8,129,128]{2,0,1:T(8,128)S(1)} %pad_maximum_fusion), channel_id=1, source_target_pairs={{32,0},{40,8},{48,16},{56,24},{64,32},{72,40},{80,48},{88,56},{96,... | collective-permute-start | bytes 1585160 | tf_op jit(solution)/shard_map/ppermute | solution.py:170
  116.3 15.0 %collective-permute-start.4 = (f32[8,129,128]{2,0,1:T(8,128)S(1)}, f32[8,129,128]{2,0,1:T(8,128)S(1)}, u32[]{:S(2)}, u32[]{:S(2)}) collective-permute-start(f32[8,129,128]{2,0,1:T(8,128)S(1)} %pad_maximum_fusion.1), channel_id=1, source_target_pairs={{64,0},{72,8},{80,16},{88,24},{96,32},{104,40},{112,48},{120,56},{... | collective-permute-start | bytes 1585160 | tf_op jit(solution)/shard_map/ppermute | solution.py:170
  131.4 9.4 %copy-start.11 = (f32[8,64,128]{2,0,1:T(8,128)}, f32[8,64,128]{2,0,1:T(8,128)S(1)}, u32[]{:S(2)}) copy-start(f32[8,64,128]{2,0,1:T(8,128)S(1)} %get-tuple-element.53) | copy-start | bytes 786436
  131.4 5.4 %copy-start.7 = (bf16[4,256,8,64]{1,0,3,2:T(4,128)(2,1)S(1)}, bf16[4,256,8,64]{1,0,3,2:T(4,128)(2,1)}, u32[]{:S(2)}) copy-start(bf16[4,256,8,64]{1,0,3,2:T(4,128)(2,1)} %copy-done.6) | copy-start | bytes 3145732
  131.4 5.4 %copy-start.34 = (f32[4,8,256]{2,1,0:T(8,128)S(1)}, f32[4,8,256]{2,1,0:T(8,128)}, u32[]{:S(2)}) copy-start(f32[4,8,256]{2,1,0:T(8,128)} %copy.365) | copy-start | bytes 98308
  131.7 5.0 %copy-start.13 = (f32[4,256,8,64]{1,3,2,0:T(8,128)S(1)}, f32[4,256,8,64]{1,3,2,0:T(8,128)}, u32[]{:S(2)}) copy-start(f32[4,256,8,64]{1,3,2,0:T(8,128)} %fusion.32) | copy-start | bytes 6291460
  132.9 17.5 %collective-permute-start.5 = (f32[8,129,128]{2,0,1:T(8,128)}, f32[8,129,128]{2,0,1:T(8,128)}, u32[]{:S(2)}, u32[]{:S(2)}) collective-permute-start(f32[8,129,128]{2,0,1:T(8,128)} %pad_maximum_fusion.2), channel_id=1, source_target_pairs={{128,0},{136,8},{144,16},{152,24},{160,32},{168,40},{176,48},{184,... | collective-permute-start | bytes 1585160 | tf_op jit(solution)/shard_map/ppermute | solution.py:170
  (19 other events, 27.8 us)

commit v8 on v5

--- a/solution.py
+++ b/solution.py
@@ -1,7 +1,10 @@
 import jax
 import jax.numpy as jnp
 from jax import lax
+from jax.experimental import pallas as pl
 from jax.sharding import PartitionSpec as P
+
+_INTERPRET = False
 
 P_SIZE = 64
 N = 128
@@ -115,6 +118,21 @@
     return jnp.einsum("thp,tn->hpn", weighted, queries, preferred_element_type=jnp.float32)
 
 
+def _scan_round(flag_ref, got_ref, msg_ref, later_ref, msg_out, later_out):
+    heads = got_ref.shape[0]
+    lanes = got_ref.shape[2]
+    valid = flag_ref[...]
+    got_b = got_ref[:, 0:P_SIZE, :] * valid
+    got_a = got_ref[:, P_SIZE : P_SIZE + 1, :] * valid + (1.0 - valid)
+    later_a = later_ref[:, P_SIZE : P_SIZE + 1, :]
+    later_out[:, 0:P_SIZE, :] = later_ref[:, 0:P_SIZE, :] + later_a * got_b
+    later_out[:, P_SIZE : P_SIZE + 8, :] = jnp.broadcast_to(later_a * got_a, (heads, 8, lanes))
+    whole_a = msg_ref[:, P_SIZE : P_SIZE + 1, :]
+    msg_out[:, 0:P_SIZE, :] = msg_ref[:, 0:P_SIZE, :] + whole_a * got_b
+    msg_out[:, P_SIZE : P_SIZE + 8, :] = jnp.broadcast_to(whole_a * got_a, (heads, 8, lanes))
+    msg_out[:, P_SIZE + 8 :, :] = msg_ref[:, P_SIZE + 8 :, :] + got_ref[:, P_SIZE + 8 :, :]
+
+
 def on_device(
     prompt_grad,
     prompt_keys,
@@ -150,41 +168,38 @@
             dst_seq = share * src_resp + src_seq % share
             dst_resp = src_seq // share
             pairs.append((src_seq * resp_len + src_resp, dst_seq * resp_len + dst_resp))
-    pieces = lax.ppermute(partial_state, ("seq", "resp"), pairs)[None]
-    whole_b = start_grad
-    whole_a = jnp.exp(shard_total)
-    later_b = jnp.zeros_like(start_grad)
-    later_a = jnp.ones_like(whole_a)
-    my_heads = None
+    piece = lax.ppermute(partial_state, ("seq", "resp"), pairs)
+    own_a = jnp.exp(shard_total)
+    slotted = lax.dynamic_update_slice_in_dim(
+        jnp.zeros((head_count,) + partial_state.shape[1:], jnp.float32),
+        piece,
+        (seq_index % share) * partial_state.shape[0],
+        0,
+    )
+    message = jnp.concatenate(
+        [start_grad, jnp.broadcast_to(own_a[:, None, None], (head_count, 8, N)), slotted], axis=1
+    )
+    later = jnp.concatenate(
+        [jnp.zeros_like(start_grad), jnp.ones((head_count, 8, N), jnp.float32)], axis=1
+    )
+    step = pl.pallas_call(
+        _scan_round,
+        out_shape=(
+            jax.ShapeDtypeStruct(message.shape, jnp.float32),
+            jax.ShapeDtypeStruct(later.shape, jnp.float32),
+        ),
+        interpret=_INTERPRET,
+    )
     shift = 1
     while shift < seq_len:
         pairs = [((k + shift) % seq_len, k) for k in range(seq_len)]
-        parts = [whole_b, jnp.broadcast_to(whole_a[:, None, None], (head_count, 1, N))]
-        if my_heads is None:
-            parts.append(pieces.reshape(head_count, -1, N))
-        else:
-            parts.append(my_heads)
-        got = lax.ppermute(jnp.concatenate(parts, axis=1), "seq", pairs)
-        valid = seq_index + shift < seq_len
-        got_b = jnp.where(valid, got[:, :P_SIZE], 0.0)
-        got_a = jnp.where(valid, got[:, P_SIZE, 0], 1.0)
-        rest = got[:, P_SIZE + 1 :]
-        if my_heads is None:
-            pieces = jnp.concatenate([pieces, rest.reshape(pieces.shape)], axis=0)
-            if pieces.shape[0] == share:
-                order = (jnp.arange(share) - seq_index % share) % share
-                my_heads = jnp.take(pieces, order, axis=0).reshape(
-                    (head_count,) + partial_state.shape[1:]
-                )
-        else:
-            my_heads = my_heads + rest
-        later_b = later_b + later_a[:, None, None] * got_b
-        later_a = later_a * got_a
-        if shift * 2 < seq_len:
-            whole_b = whole_b + whole_a[:, None, None] * got_b
-            whole_a = whole_a * got_a
+        got = lax.ppermute(message, "seq", pairs)
+        flag = jnp.broadcast_to(
+            (seq_index + shift < seq_len).astype(jnp.float32), (1, 1, N)
+        )
+        message, later = step(flag, got, message, later)
         shift *= 2
-    incoming = later_b + later_a[:, None, None] * my_heads
+    incoming = later[:, :P_SIZE] + later[:, P_SIZE : P_SIZE + 1] * message[:, P_SIZE + 8 :]
     local_part = group_output(prompt_keys, prompt_queries, prompt_parts)
     carry_term = jnp.einsum(
         "hpn,tn->thp",

time: 141 us -> 165 us (1.17)
  Pallas kernels: 0 us -> 11.4 us
  waiting for transfers between devices: 33 us -> 41.9 us
  matrix products: 24.7 us -> 28.2 us
    pallas_call x0 -> x5, Pallas kernels: none -> 11.4 us  [on_device(): message, later = step(flag, got, message, later)]
    ppermute x6, waiting for transfers between devices: 33 us -> 41.9 us  [the longest x5 41.9 us: on_device(): got = lax.ppermute(message, 'seq', pairs)]
    slice x14 -> x2, local copies, waits for them, and re-layouts: 7.02 us -> 0.91 us  [the longest x1 0.76 us: on_device(): later[:, P_SIZE:P_SIZE + 1] * message[:, P_SIZE + 8:]]
    broadcast_in_dim x8 -> x6, local copies, waits for them, and re-layouts: 1.05 us -> 3.44 us  [the longest x5 2.73 us: on_device(): jnp.broadcast_to((seq_index + shift < seq_len).astype(jnp.float32), (1, 1...]
    unnamed x110 -> x51, local copies, waits for them, and re-layouts: 19.7 us -> 17.6 us
    dot_general x2, matrix products: 8.78 us -> 10.8 us  [group_output(): jnp.einsum('chst,cshp->cthp', mixing, grad_group, preferred_element_type=...]
    squeeze x3, local copies, waits for them, and re-layouts: 0.67 us -> 2.6 us  [group_parts(): group_gains = jnp.exp(cum_group[:, :, -1] - before)]
    dot_general x2, matrix products: 3 us -> 4.8 us  [group_output(): jnp.einsum('chpn,ctn->cthp', end_grads.astype(jnp.bfloat16), key_group, p...]
  transfers between devices with their start and end apart: 6 -> 6, of which waited for: 5 -> 5; matrix products, arithmetic and copies ran while one was open for 48% -> 50% of each run, Pallas kernels for 0% -> 0%
where the time goes in v8:
time: 165 us; the launch traced here: 162 us
  local copies, waits for them, and re-layouts  42.8 us (26%)
  waiting for transfers between devices  41.9 us (25%)
  matrix products  28.2 us (17%)
  other arithmetic  27.5 us (17%)
  Pallas kernels  11.4 us (7%)
  starting transfers between devices  9.54 us (6%)
    ppermute x5, waiting for transfers between devices, on_device(): got = lax.ppermute(message, 'seq', pairs)  41.9 us
    unnamed x51, local copies, waits for them, and re-layouts  17.6 us
    pallas_call x5, Pallas kernels, on_device(): message, later = step(flag, got, message, later)  11.4 us
    dot_general x2, matrix products, group_output(): jnp.einsum('chst,cshp->cthp', mixing, grad_group, preferred_element_type=...  10.8 us
    ppermute x1, starting transfers between devices, on_device(): piece = lax.ppermute(partial_state, ('seq', 'resp'), pairs)  7.25 us
    dot_general x2, matrix products, group_parts(): jnp.einsum('hcd,dhpn->chpn', coef, states, precision=lax.Precision.HIGHEST)  5.21 us
    dot_general x2, matrix products, group_output(): jnp.einsum('chpn,ctn->cthp', end_grads.astype(jnp.bfloat16), key_group, p...  4.8 us
    dot_general x2, matrix products, group_output(): jnp.einsum('csn,ctn->cst', query_group, key_group, preferred_element_type...  3.88 us
  transfers between devices with their start and end apart: 6, of which 5 were waited for; matrix products, arithmetic and copies ran while one was open for 50% of the time, Pallas kernels for 0%

profile of v8, /device:TPU:14, one launch (start us, length us, event | category | flops | bytes accessed | tf_op | source)
XLA Modules:
  0.0 162.5 jit_solution(16359154478311429476)
XLA Ops:
  2.3 1.6 copy.116
  6.7 7.2 %collective-permute-start = (f32[2,64,128]{2,1,0:T(8,128)}, f32[2,64,128]{2,1,0:T(8,128)}, u32[]{:S(2)}, u32[]{:S(2)}) collective-permute-start(f32[2,64,128]{2,1,0:T(8,128)} %fusion.20), channel_id=1, source_target_pairs={{0,0},{1,32},{2,64},{3,96},{4,128},{5,160},{6,192},{7,224},{8,8},{... | collective-permute-start | bytes 196616 | tf_op jit(solution)/shard_map/ppermute | solution.py:171
  14.6 2.3 %reduce-window.14 = f32[8,8,128]{2,1,0:T(8,128)S(1)} reduce-window(f32[8,8,128]{2,1,0:T(8,128)S(1)} %copy.101, f32[]{:T(128)} %constant.18.clone.1), window={size=1x1x128 pad=0_0x0_0x127_0}, to_apply=%region_0.0 | reduce-window | flops 1040384 | bytes 65540 | tf_op jit(solution)/shard_map/reduce-window
  26.9 2.3 %copy.105 = bf16[1024,512]{0,1:T(8,128)(2,1)} copy(bf16[1024,512]{1,0:T(8,128)(2,1)} %param.9) | data formatting | bytes 2097152 | tf_op args[0]
  29.2 2.7 %reshape.288 = bf16[4,256,8,64]{1,0,3,2:T(4,128)(2,1)} reshape(bf16[1024,512]{0,1:T(8,128)(2,1)} %copy.105) | data formatting | bytes 2097152 | tf_op jit(solution)/shard_map/reshape | solution.py:27
  33.3 1.6 %multiply_convert_fusion.5 = bf16[4,256,8,64]{1,0,3,2:T(4,128)(2,1)S(1)} fusion(bf16[4,256,8,64]{1,0,3,2:T(4,128)(2,1)} %reshape.288, f32[4,256,8]{1,0,2:T(4,128)S(1)} %copy.109), kind=kLoop, calls=%fused_computation.28 | loop fusion | flops 1572864 | bytes 2129920 | tf_op jit(solution)/shard_map/convert_element_type | solution.py:31
  35.4 2.5 %fusion.27 = f32[8,64,128,5]{2,3,1,0:T(8,128)S(1)} fusion(f32[8,5,4,1]{1,2,3,0:T(4,128)S(1)} %copy-done.14, f32[4,8,64,128]{3,2,1,0:T(8,128)S(1)} %fusion.29), kind=kOutput, calls=%fused_computation.38 | convolution fusion | flops 15728640 | bytes 2359936 | tf_op jit(solution)/shard_map/hcd,dhpn->chpn/dot_general | solution.py:49
  38.9 1.8 %fusion.33 = f32[4,8,64,256]{3,2,1,0:T(8,128)} fusion(bf16[4,256,128,1]{2,1,3,0:T(8,128)(2,1)S(1)} %bitcast.178, f32[5,8,64,128]{3,2,1,0:T(8,128)S(1)} %bitcast.169), kind=kOutput, calls=%fused_computation.44 | convolution fusion | flops 134545408 | bytes 3670016 | tf_op jit(solution)/shard_map/chpn,ctn->cthp/dot_general | solution.py:88
  53.2 4.9 %fusion.18 = f32[4,256,8,64]{1,3,2,0:T(8,128)} fusion(f32[4,8,64,256]{3,2,1,0:T(8,128)} %fusion.33, f32[4,8,256]{2,1,0:T(8,128)} %copy.103, f32[4,256,256]{2,1,0:T(8,128)S(1)} %fusion.66, pred[256,256]{1,0:T(8,128)(4,1)} %iota_compare_fusion.1, bf16[4,256,8,64]{1,0,3,2:T(4,128)(2,1)} %reshape.288, f32[4,256,8]{1,2,0:T(8,128)} %get-tuple-element.36), kind=kOutput, calls=%fused_computation.26 | convolution fusion | flops 277872640 | bytes 6422528 | tf_op jit(solution)/shard_map/chst,cshp->cthp/dot_general | solution.py:85
  59.3 2.9 %copy.114 = f32[4,256,8,64]{1,0,3,2:T(4,128)S(1)} copy(f32[4,256,8,64]{1,3,2,0:T(8,128)} %fusion.18) | data formatting | bytes 4194304 | tf_op jit(solution)/shard_map/add | solution.py:99
  62.2 1.8 %copy.148 = f32[64,8,4,256]{3,1,2,0:T(8,128)} copy(f32[64,8,4,256]{3,2,1,0:T(4,128)S(1)} %bitcast.171) | data formatting | bytes 4194304
  69.7 6.2 %collective-permute-done.1.got_ref = f32[8,136,128]{2,1,0:T(8,128)S(1)} collective-permute-done((f32[8,136,128]{2,1,0:T(8,128)S(1)}, f32[8,136,128]{2,1,0:T(8,128)S(1)}, u32[]{:S(2)}, u32[]{:S(2)}) %collective-permute-start.1) | collective-permute-done | bytes 557088 | tf_op jit(solution)/shard_map/ppermute | solution.py:196
  77.3 2.2 %shard_map.104 = (f32[8,136,128]{2,1,0:T(8,128)}, f32[8,72,128]{2,1,0:T(8,128)}) custom-call(f32[1,1,128]{2,1,0:T(1,128)} %broadcast_in_dim.244.flag_ref, f32[8,136,128]{2,1,0:T(8,128)} %copy-done.9, f32[8,136,128]{2,1,0:T(8,128)} %copy-done.6, f32[8,72,128]{2,1,0:T(8,128)} %concatenate.17.later_ref), custom_call_target="tpu_custom_call" | custom-call | tf_op jit(solution)/shard_map/pallas_call | solution.py:200
  80.9 1.5 select_reduce_fusion.1
  82.4 3.4 %and_and_fusion = pred[16,256,256]{2,1,0:T(8,128)(4,1)} fusion(s32[16,256]{1,0:T(8,128)S(1)} %eq.80, pred[16,256]{1,0:T(8,128)(4,1)} %and.96, pred[256,256]{1,0:T(8,128)(4,1)S(1)} %copy-done.12), kind=kLoop, calls=%fused_computation.15 | loop fusion | flops 3145728 | bytes 1134592 | tf_op jit(solution)/shard_map/and | solution.py:78
  85.7 9.1 %collective-permute-done.2.got_ref = f32[8,136,128]{2,1,0:T(8,128)} collective-permute-done((f32[8,136,128]{2,1,0:T(8,128)}, f32[8,136,128]{2,1,0:T(8,128)}, u32[]{:S(2)}, u32[]{:S(2)}) %collective-permute-start.2) | collective-permute-done | bytes 557088 | tf_op jit(solution)/shard_map/ppermute | solution.py:196
  95.4 2.2 %shard_map.105 = (f32[8,136,128]{2,1,0:T(8,128)}, f32[8,72,128]{2,1,0:T(8,128)}) custom-call(f32[1,1,128]{2,1,0:T(1,128)} %broadcast_in_dim.243.flag_ref, f32[8,136,128]{2,1,0:T(8,128)} %collective-permute-done.2.got_ref, f32[8,136,128]{2,1,0:T(8,128)} %get-tuple-element.12.msg_ref, f32[8,72,128]{2,1,0:T(8,128)} %get-tuple-element.13.later_ref), custom_call_target="tpu_custom_call" | custom-call | tf_op jit(solution)/shard_map/pallas_call | solution.py:200
  97.7 2.7 %fusion.19 = bf16[17,2,64,128]{3,0,2,1:T(8,128)(2,1)S(1)} fusion(f32[16,2,64,128]{3,2,1,0:T(8,128)S(1)} %fusion.24, f32[2,17,16]{1,2,0:T(8,128)} %select_reduce_fusion.1, f32[17]{0:T(128)} %pad_maximum_fusion.2, pred[17,16]{0,1:T(8,128)(4,1)} %iota_compare_fusion.3), kind=kOutput, calls=%fused_computation.31 | convolution fusion | flops 53756992 | bytes 1608148 | tf_op jit(solution)/shard_map/hcd,dhpn->chpn/dot_general | solution.py:49
  101.4 2.6 %fusion.67 = f32[16,256,256]{2,1,0:T(8,128)} fusion(bf16[16,256,128]{2,1,0:T(8,128)(2,1)S(1)} %bitcast.173, bf16[16,256,128]{2,1,0:T(8,128)(2,1)S(1)} %bitcast.166), kind=kOutput, calls=%fused_computation.127 | convolution fusion | flops 268435456 | bytes 6291456 | tf_op jit(solution)/shard_map/csn,ctn->cst/dot_general | solution.py:74
  104.0 10.4 %collective-permute-done.3.got_ref = f32[8,136,128]{2,1,0:T(8,128)} collective-permute-done((f32[8,136,128]{2,1,0:T(8,128)}, f32[8,136,128]{2,1,0:T(8,128)}, u32[]{:S(2)}, u32[]{:S(2)}) %collective-permute-start.3) | collective-permute-done | bytes 557088 | tf_op jit(solution)/shard_map/ppermute | solution.py:196
  115.0 2.3 %shard_map.106 = (f32[8,136,128]{2,1,0:T(8,128)}, f32[8,72,128]{2,1,0:T(8,128)}) custom-call(f32[1,1,128]{2,1,0:T(1,128)} %broadcast_in_dim.242.flag_ref, f32[8,136,128]{2,1,0:T(8,128)} %collective-permute-done.3.got_ref, f32[8,136,128]{2,1,0:T(8,128)} %get-tuple-element.14.msg_ref, f32[8,72,128]{2,1,0:T(8,128)} %get-tuple-element.15.later_ref), custom_call_target="tpu_custom_call" | custom-call | tf_op jit(solution)/shard_map/pallas_call | solution.py:200
  117.3 5.9 %fusion.3 = f32[16,2,256,64]{2,3,1,0:T(8,128)} fusion(f32[16,2,256]{2,1,0:T(2,128)S(1)} %bitcast.198, f32[16,256,256]{2,1,0:T(8,128)} %fusion.67, pred[16,256,256]{2,1,0:T(8,128)(4,1)} %and_and_fusion, bf16[16,256,2,64]{1,0,3,2:T(8,128)(2,1)S(1)} %bitcast.177), kind=kOutput, calls=%fused_computation.5 | convolution fusion | flops 276824064 | bytes 8421376 | tf_op jit(solution)/shard_map/chst,cshp->cthp/dot_general | solution.py:85
  123.2 10.8 %collective-permute-done.4.got_ref = f32[8,136,128]{2,1,0:T(8,128)} collective-permute-done((f32[8,136,128]{2,1,0:T(8,128)}, f32[8,136,128]{2,1,0:T(8,128)}, u32[]{:S(2)}, u32[]{:S(2)}) %collective-permute-start.4) | collective-permute-done | bytes 557088 | tf_op jit(solution)/shard_map/ppermute | solution.py:196
  134.6 2.3 %shard_map.107 = (f32[8,136,128]{2,1,0:T(8,128)}, f32[8,72,128]{2,1,0:T(8,128)}) custom-call(f32[1,1,128]{2,1,0:T(1,128)} %broadcast_in_dim.241.flag_ref, f32[8,136,128]{2,1,0:T(8,128)} %collective-permute-done.4.got_ref, f32[8,136,128]{2,1,0:T(8,128)} %get-tuple-element.16.msg_ref, f32[8,72,128]{2,1,0:T(8,128)} %get-tuple-element.17.later_ref), custom_call_target="tpu_custom_call" | custom-call | tf_op jit(solution)/shard_map/pallas_call | solution.py:200
  136.8 2.0 %collective-permute-start.5 = (f32[8,136,128]{2,1,0:T(8,128)}, f32[8,136,128]{2,1,0:T(8,128)}, u32[]{:S(2)}, u32[]{:S(2)}) collective-permute-start(f32[8,136,128]{2,1,0:T(8,128)} %get-tuple-element.18.msg_ref), channel_id=1, source_target_pairs={{128,0},{136,8},{144,16},{152,24},{160,32},{168,40},{176,48},{184,... | collective-permute-start | bytes 1671176 | tf_op jit(solution)/shard_map/ppermute | solution.py:196
  138.9 3.0 %fusion.16 = bf16[16,256,2,64]{1,3,2,0:T(8,128)(2,1)} fusion(f32[16,2,256,64]{2,3,1,0:T(8,128)} %fusion.3, bf16[16,256,128,1]{2,1,3,0:T(8,128)(2,1)S(1)} %bitcast.167, f32[16,256,2]{1,2,0:T(2,128)S(1)} %get-tuple-element.35, bf16[16,2,64,128]{3,0,2,1:T(8,128)(2,1)S(1)} %copy-done.7), kind=kOutput, calls=%fused_computation.21 | convolution fusion | flops 135790592 | bytes 4751360 | tf_op jit(solution)/shard_map/chpn,ctn->cthp/dot_general | solution.py:88
  141.9 4.5 %copy.145 = bf16[16,256,2,64]{3,2,1,0:T(2,128)(2,1)S(1)} copy(bf16[16,256,2,64]{1,3,2,0:T(8,128)(2,1)} %fusion.16) | data formatting | bytes 2097152
  146.4 1.8 %reshape.309 = bf16[4096,128]{1,0:T(8,128)(2,1)} reshape(bf16[16,256,2,64]{3,2,1,0:T(2,128)(2,1)S(1)} %copy.145) | data formatting | bytes 2097152
  148.3 5.3 %collective-permute-done.5.got_ref = f32[8,136,128]{2,1,0:T(8,128)} collective-permute-done((f32[8,136,128]{2,1,0:T(8,128)}, f32[8,136,128]{2,1,0:T(8,128)}, u32[]{:S(2)}, u32[]{:S(2)}) %collective-permute-start.5) | collective-permute-done | bytes 557088 | tf_op jit(solution)/shard_map/ppermute | solution.py:196
  154.1 2.4 %shard_map.108 = (f32[8,136,128]{2,1,0:T(8,128)}, f32[8,72,128]{2,1,0:T(8,128)}) custom-call(f32[1,1,128]{2,1,0:T(1,128)} %broadcast_in_dim.240.flag_ref, f32[8,136,128]{2,1,0:T(8,128)} %collective-permute-done.5.got_ref, f32[8,136,128]{2,1,0:T(8,128)} %get-tuple-element.18.msg_ref, f32[8,72,128]{2,1,0:T(8,128)} %get-tuple-element.19.later_ref), custom_call_target="tpu_custom_call" | custom-call | tf_op jit(solution)/shard_map/pallas_call | solution.py:200
  157.3 1.5 bitcast_multiply_fusion.1
  160.2 2.3 %copy.131 = bf16[1024,512]{1,0:T(8,128)(2,1)} copy(bf16[1024,512]{0,1:T(8,128)(2,1)} %fusion.17) | data formatting | bytes 2097152
  (127 shorter events, 45.3 us)
Async XLA Ops:
  0.6 100.8 %copy-start = (bf16[4096,128]{1,0:T(8,128)(2,1)S(1)}, bf16[4096,128]{1,0:T(8,128)(2,1)}, u32[]{:S(2)}) copy-start(bf16[4096,128]{1,0:T(8,128)(2,1)} %param.14) | copy-start | bytes 3145732
  0.6 3.3 %copy-start.10 = (s32[4096]{0:T(1024)S(1)}, s32[4096]{0:T(1024)}, u32[]{:S(2)}) copy-start(s32[4096]{0:T(1024)} %param.17) | copy-start | bytes 49156
  0.7 3.4 %copy-start.11 = (f32[2,4096]{1,0:T(2,128)S(1)}, f32[2,4096]{1,0:T(2,128)}, u32[]{:S(2)}) copy-start(f32[2,4096]{1,0:T(2,128)} %param.16) | copy-start | bytes 98308
  2.3 3.3 %copy-start.2 = (bf16[4096,128]{1,0:T(8,128)(2,1)S(1)}, bf16[4096,128]{1,0:T(8,128)(2,1)}, u32[]{:S(2)}) copy-start(bf16[4096,128]{1,0:T(8,128)(2,1)} %param.15) | copy-start | bytes 3145732
  5.1 9.5 %copy-start.13 = (f32[8,1024]{1,0:T(8,128)S(1)}, f32[8,1024]{1,0:T(8,128)}, u32[]{:S(2)}) copy-start(f32[8,1024]{1,0:T(8,128)} %param.12) | copy-start | bytes 98308
  5.5 19.2 %copy-start.19 = (f32[4]{0:T(128)S(1)}, f32[4]{0:T(128)}, u32[]{:S(2)}) copy-start(f32[4]{0:T(128)} %constant.20.clone.1) | copy-start | bytes 52
  5.6 20.6 %copy-start.18 = (f32[5]{0:T(128)S(1)}, f32[5]{0:T(128)}, u32[]{:S(2)}) copy-start(f32[5]{0:T(128)} %constant.15.clone.1) | copy-start | bytes 64
  6.7 59.3 %collective-permute-start = (f32[2,64,128]{2,1,0:T(8,128)}, f32[2,64,128]{2,1,0:T(8,128)}, u32[]{:S(2)}, u32[]{:S(2)}) collective-permute-start(f32[2,64,128]{2,1,0:T(8,128)} %fusion.20), channel_id=1, source_target_pairs={{0,0},{1,32},{2,64},{3,96},{4,128},{5,160},{6,192},{7,224},{8,8},{... | collective-permute-start | bytes 196616 | tf_op jit(solution)/shard_map/ppermute | solution.py:171
  29.2 5.7 %copy-start.8 = (bf16[1024,128]{1,0:T(8,128)(2,1)S(1)}, bf16[1024,128]{1,0:T(8,128)(2,1)}, u32[]{:S(2)}) copy-start(bf16[1024,128]{1,0:T(8,128)(2,1)} %param.11) | copy-start | bytes 786436
  33.3 2.1 %copy-start.14 = (f32[8,5,4,1]{1,2,3,0:T(4,128)S(1)}, f32[8,5,4,1]{1,2,3,0:T(4,128)}, u32[]{:S(2)}) copy-start(f32[8,5,4,1]{1,2,3,0:T(4,128)} %copy.134) | copy-start | bytes 1924
  37.9 1.0 copy-start.5
  53.2 4.9 %copy-start.16 = (f32[8,1]{0,1:T(1,128)S(1)}, f32[8,1]{0,1:T(1,128)}, u32[]{:S(2)}) copy-start(f32[8,1]{0,1:T(1,128)} %copy.147) | copy-start | bytes 100
  65.2 3.6 %copy-start.3 = (bf16[16,8,16,256]{3,2,1,0:T(8,128)(2,1)S(1)}, bf16[16,8,16,256]{3,2,1,0:T(8,128)(2,1)}, u32[]{:S(2)}) copy-start(bf16[16,8,16,256]{3,2,1,0:T(8,128)(2,1)} %copy.152) | copy-start | bytes 3145732
  68.6 1.1 copy-start.6
  68.6 7.3 %collective-permute-start.1 = (f32[8,136,128]{2,1,0:T(8,128)S(1)}, f32[8,136,128]{2,1,0:T(8,128)S(1)}, u32[]{:S(2)}, u32[]{:S(2)}) collective-permute-start(f32[8,136,128]{2,1,0:T(8,128)S(1)} %pad_maximum_fusion.msg_ref), channel_id=1, source_target_pairs={{8,0},{16,8},{24,16},{32,24},{40,32},{48,40},{56,48},{64,56},{72,6... | collective-permute-start | bytes 1671176 | tf_op jit(solution)/shard_map/ppermute | solution.py:196
  69.1 13.3 %copy-start.12 = (pred[256,256]{1,0:T(8,128)(4,1)S(1)}, pred[256,256]{1,0:T(8,128)(4,1)}, u32[]{:S(2)}) copy-start(pred[256,256]{1,0:T(8,128)(4,1)} %iota_compare_fusion.1) | copy-start | bytes 196612
  75.9 0.8 copy-start.9
  79.5 15.3 %collective-permute-start.2 = (f32[8,136,128]{2,1,0:T(8,128)}, f32[8,136,128]{2,1,0:T(8,128)}, u32[]{:S(2)}, u32[]{:S(2)}) collective-permute-start(f32[8,136,128]{2,1,0:T(8,128)} %get-tuple-element.12.msg_ref), channel_id=1, source_target_pairs={{16,0},{24,8},{32,16},{40,24},{48,32},{56,40},{64,48},{72,56},{80,... | collective-permute-start | bytes 1671176 | tf_op jit(solution)/shard_map/ppermute | solution.py:196
  97.7 16.8 %collective-permute-start.3 = (f32[8,136,128]{2,1,0:T(8,128)}, f32[8,136,128]{2,1,0:T(8,128)}, u32[]{:S(2)}, u32[]{:S(2)}) collective-permute-start(f32[8,136,128]{2,1,0:T(8,128)} %get-tuple-element.14.msg_ref), channel_id=1, source_target_pairs={{32,0},{40,8},{48,16},{56,24},{64,32},{72,40},{80,48},{88,56},{96,... | collective-permute-start | bytes 1671176 | tf_op jit(solution)/shard_map/ppermute | solution.py:196
  101.4 15.9 %copy-start.4 = (bf16[16,8,16,256]{3,2,1,0:T(8,128)(2,1)S(1)}, bf16[16,8,16,256]{3,2,1,0:T(8,128)(2,1)}, u32[]{:S(2)}) copy-start(bf16[16,8,16,256]{3,2,1,0:T(8,128)(2,1)} %copy.152) | copy-start | bytes 3145732
  101.4 15.9 %copy-start.15 = (f32[2,16,256]{2,0,1:T(2,128)S(1)}, f32[2,16,256]{2,0,1:T(2,128)}, u32[]{:S(2)}) copy-start(f32[2,16,256]{2,0,1:T(2,128)} %copy.185) | copy-start | bytes 98308
  117.3 16.8 %collective-permute-start.4 = (f32[8,136,128]{2,1,0:T(8,128)}, f32[8,136,128]{2,1,0:T(8,128)}, u32[]{:S(2)}, u32[]{:S(2)}) collective-permute-start(f32[8,136,128]{2,1,0:T(8,128)} %get-tuple-element.16.msg_ref), channel_id=1, source_target_pairs={{64,0},{72,8},{80,16},{88,24},{96,32},{104,40},{112,48},{120,56},{... | collective-permute-start | bytes 1671176 | tf_op jit(solution)/shard_map/ppermute | solution.py:196
  117.3 21.6 %copy-start.7 = (bf16[16,2,64,128]{3,0,2,1:T(8,128)(2,1)S(1)}, bf16[16,2,64,128]{3,0,2,1:T(8,128)(2,1)}, u32[]{:S(2)}) copy-start(bf16[16,2,64,128]{3,0,2,1:T(8,128)(2,1)} %slice.114) | copy-start | bytes 1572868
  136.8 16.8 %collective-permute-start.5 = (f32[8,136,128]{2,1,0:T(8,128)}, f32[8,136,128]{2,1,0:T(8,128)}, u32[]{:S(2)}, u32[]{:S(2)}) collective-permute-start(f32[8,136,128]{2,1,0:T(8,128)} %get-tuple-element.18.msg_ref), channel_id=1, source_target_pairs={{128,0},{136,8},{144,16},{152,24},{160,32},{168,40},{176,48},{184,... | collective-permute-start | bytes 1671176 | tf_op jit(solution)/shard_map/ppermute | solution.py:196
  146.4 1.8 %copy-start.17 = (f32[8,1]{0,1:T(1,128)S(1)}, f32[8,1]{0,1:T(1,128)}, u32[]{:S(2)}) copy-start(f32[8,1]{0,1:T(1,128)} %copy.147) | copy-start | bytes 100
  154.1 4.6 %copy-start.1 = (f32[64,8,4,256]{3,1,2,0:T(8,128)S(1)}, f32[64,8,4,256]{3,1,2,0:T(8,128)}, u32[]{:S(2)}) copy-start(f32[64,8,4,256]{3,1,2,0:T(8,128)} %copy.148) | copy-start | bytes 6291460

commit v9 on v5

--- a/solution.py
+++ b/solution.py
@@ -151,6 +151,8 @@
             dst_resp = src_seq // share
             pairs.append((src_seq * resp_len + src_resp, dst_seq * resp_len + dst_resp))
     pieces = lax.ppermute(partial_state, ("seq", "resp"), pairs)[None]
+    local_part = group_output(prompt_keys, prompt_queries, prompt_parts)
+    start_grad, resp_dx, local_part = lax.optimization_barrier((start_grad, resp_dx, local_part))
     whole_b = start_grad
     whole_a = jnp.exp(shard_total)
     later_b = jnp.zeros_like(start_grad)
@@ -185,7 +187,6 @@
             whole_a = whole_a * got_a
         shift *= 2
     incoming = later_b + later_a[:, None, None] * my_heads
-    local_part = group_output(prompt_keys, prompt_queries, prompt_parts)
     carry_term = jnp.einsum(
         "hpn,tn->thp",
         incoming.astype(jnp.bfloat16),

time: 141 us -> 161 us (1.14)
  waiting for transfers between devices: 33 us -> 60.2 us
  matrix products: 24.7 us -> 16.6 us
    ppermute x5, waiting for transfers between devices: 33 us -> 60.1 us  [on_device(): got = lax.ppermute(jnp.concatenate(parts, axis=1), 'seq', pairs)]
    concatenate x5, other arithmetic: 2.44 us -> 5.97 us  [on_device(): got = lax.ppermute(jnp.concatenate(parts, axis=1), 'seq', pairs)]
    dot_general x2, matrix products: 8.78 us -> 6.11 us  [group_output(): jnp.einsum('chst,cshp->cthp', mixing, grad_group, preferred_element_type=...]
    unnamed x110 -> x108, local copies, waits for them, and re-layouts: 19.7 us -> 17.4 us
    dot_general x2, matrix products: 3 us -> 0.88 us  [group_output(): jnp.einsum('chpn,ctn->cthp', end_grads.astype(jnp.bfloat16), key_group, p...]
    slice x5, local copies, waits for them, and re-layouts: 3.79 us -> 5.83 us  [on_device(): got_b = jnp.where(valid, got[:, :P_SIZE], 0.0)]
    add x2, other arithmetic: 0.21 us -> 2.21 us  [on_device(): my_heads = my_heads + rest]
    dot_general x2, matrix products: 2.95 us -> 1 us  [group_output(): jnp.einsum('csn,ctn->cst', query_group, key_group, preferred_element_type...]
  transfers between devices with their start and end apart: 6 -> 6, of which waited for: 5 -> 5; matrix products, arithmetic and copies ran while one was open for 48% -> 24% of each run, Pallas kernels for 0% -> 0%
where the time goes in v9:
time: 161 us; the launch traced here: 158 us
  waiting for transfers between devices  60.2 us (37%)
  local copies, waits for them, and re-layouts  43.8 us (27%)
  other arithmetic  26.8 us (17%)
  matrix products  16.6 us (10%)
  starting transfers between devices  9.29 us (6%)
    ppermute x5, waiting for transfers between devices, on_device(): got = lax.ppermute(jnp.concatenate(parts, axis=1), 'seq', pairs)  60.1 us
    unnamed x108, local copies, waits for them, and re-layouts  17.4 us
    ppermute x1, starting transfers between devices, on_device(): pieces = lax.ppermute(partial_state, ('seq', 'resp'), pairs)[None]  7.25 us
    dot_general x2, matrix products, group_output(): jnp.einsum('chst,cshp->cthp', mixing, grad_group, preferred_element_type=...  6.11 us
    concatenate x5, other arithmetic, on_device(): got = lax.ppermute(jnp.concatenate(parts, axis=1), 'seq', pairs)  5.97 us
    slice x5, local copies, waits for them, and re-layouts, on_device(): got_b = jnp.where(valid, got[:, :P_SIZE], 0.0)  5.83 us
    dot_general x2, matrix products, group_parts(): jnp.einsum('hcd,dhpn->chpn', coef, states, precision=lax.Precision.HIGHEST)  4.5 us
    slice x5, local copies, waits for them, and re-layouts, on_device(): got_a = jnp.where(valid, got[:, P_SIZE, 0], 1.0)  3.41 us
  transfers between devices with their start and end apart: 6, of which 5 were waited for; matrix products, arithmetic and copies ran while one was open for 24% of the time, Pallas kernels for 0%

profile of v9, /device:TPU:14, one launch (start us, length us, event | category | flops | bytes accessed | tf_op | source)
XLA Modules:
  0.0 158.1 jit_solution(16961081204648928846)
XLA Ops:
  4.1 1.6 copy.338
  6.4 1.1 fusion.20
  7.5 7.3 %collective-permute-start = (f32[2,64,128]{2,1,0:T(8,128)}, f32[2,64,128]{2,1,0:T(8,128)S(1)}, u32[]{:S(2)}, u32[]{:S(2)}) collective-permute-start(f32[2,64,128]{2,1,0:T(8,128)} %fusion.20), channel_id=1, source_target_pairs={{0,0},{1,32},{2,64},{3,96},{4,128},{5,160},{6,192},{7,224},{8,8},{... | collective-permute-start | bytes 196616 | tf_op jit(solution)/shard_map/ppermute | solution.py:153
  16.8 2.3 %reduce-window.14 = f32[8,8,128]{2,1,0:T(8,128)S(1)} reduce-window(f32[8,8,128]{2,1,0:T(8,128)S(1)} %copy.326, f32[]{:T(128)} %constant.35.clone.1), window={size=1x1x128 pad=0_0x0_0x127_0}, to_apply=%region_0.0 | reduce-window | flops 1040384 | bytes 65540 | tf_op jit(solution)/shard_map/reduce-window
  22.9 2.0 %fusion.19 = bf16[17,2,64,128]{3,0,2,1:T(8,128)(2,1)S(1)} fusion(f32[16,2,64,128]{3,2,1,0:T(8,128)S(1)} %fusion.25, f32[2,17,16]{1,2,0:T(8,128)S(1)} %select_reduce_fusion.1, f32[17]{0:T(128)S(1)} %pad_maximum_fusion.8, pred[17,16]{0,1:T(8,128)(4,1)S(1)} %iota_compare_fusion.3), kind=kOutput, calls=%fused_computation.32 | convolution fusion | flops 53756992 | bytes 1608148 | tf_op jit(solution)/shard_map/hcd,dhpn->chpn/dot_general | solution.py:46
  25.9 2.4 %and_and_fusion = pred[16,256,256]{2,1,0:T(8,128)(4,1)} fusion(s32[16,256]{1,0:T(8,128)S(1)} %eq.79, pred[16,256]{1,0:T(8,128)(4,1)S(1)} %and.123, pred[256,256]{1,0:T(8,128)(4,1)S(1)} %iota_compare_fusion.1), kind=kLoop, calls=%fused_computation.17 | loop fusion | flops 3145728 | bytes 1134592 | tf_op jit(solution)/shard_map/and | solution.py:75
  32.0 1.2 multiply_convert_fusion.5
  33.6 2.5 %convolution_bitcast_fusion = f32[5,8,64,128]{3,0,2,1:T(8,128)S(1)} fusion(f32[8,5,4,1]{1,2,3,0:T(4,128)S(1)} %copy.385, f32[4,8,64,128]{3,2,1,0:T(8,128)S(1)} %fusion.29), kind=kOutput, calls=%fused_computation.30 | convolution fusion | flops 15728640 | bytes 2359936 | tf_op jit(solution)/shard_map/hcd,dhpn->chpn/dot_general | solution.py:46
  36.2 1.3 copy-done.8
  41.1 3.9 %fusion.2 = f32[16,2,256,64]{2,3,1,0:T(8,128)S(1)} fusion(f32[16,2,256]{2,1,0:T(2,128)S(1)} %bitcast.249, f32[16,256,256]{2,1,0:T(8,128)S(1)} %fusion.96, pred[16,256,256]{2,1,0:T(8,128)(4,1)S(1)} %copy-done.23, bf16[16,256,2,64]{1,0,3,2:T(8,128)(2,1)S(1)} %bitcast.218), kind=kOutput, calls=%fused_computation.5 | convolution fusion | flops 276824064 | bytes 8421376 | tf_op jit(solution)/shard_map/chst,cshp->cthp/dot_general | solution.py:82
  46.3 2.2 %fusion.16 = f32[4,256,8,64]{1,3,2,0:T(8,128)S(1)} fusion(f32[4,8,64,256]{3,2,1,0:T(8,128)S(1)} %fusion.32, f32[4,8,256]{2,1,0:T(8,128)S(1)} %copy-done.35, f32[4,256,256]{2,1,0:T(8,128)S(1)} %fusion.97, pred[256,256]{1,0:T(8,128)(4,1)S(1)} %copy-done.30, bf16[4,256,8,64]{1,0,3,2:T(4,128)(2,1)S(1)} %copy-done.7, f32[4,256,8]{1,2,0:T(8,128)S(1)} %copy-done.33), kind=kOutput, calls=%fused_computation.24 | convolution fusion | flops 277872640 | bytes 6422528 | tf_op jit(solution)/shard_map/chst,cshp->cthp/dot_general | solution.py:82
  48.5 1.8 %slice.154 = f32[1,8,64,128]{3,0,2,1:T(1,128)S(1)} slice(f32[5,8,64,128]{3,0,2,1:T(8,128)} %copy-done.8), slice={[0:1], [0:8], [0:64], [0:128]} | slice | bytes 524288 | tf_op jit(solution)/shard_map/slice | solution.py:49
  50.9 1.4 copy.418
  52.3 1.4 copy.354
  55.1 5.0 %collective-permute-done.1 = f32[8,81,128]{2,0,1:T(8,128)} collective-permute-done((f32[8,81,128]{2,0,1:T(8,128)}, f32[8,81,128]{2,0,1:T(8,128)}, u32[]{:S(2)}, u32[]{:S(2)}) %collective-permute-start.1) | collective-permute-done | bytes 331808 | tf_op jit(solution)/shard_map/ppermute | solution.py:169
  66.4 11.1 %collective-permute-done.2 = f32[8,97,128]{2,0,1:T(8,128)} collective-permute-done((f32[8,97,128]{2,0,1:T(8,128)}, f32[8,97,128]{2,0,1:T(8,128)}, u32[]{:S(2)}, u32[]{:S(2)}) %collective-permute-start.2) | collective-permute-done | bytes 397344 | tf_op jit(solution)/shard_map/ppermute | solution.py:169
  83.2 1.5 gather_fusion
  86.4 1.8 %pad_maximum_fusion = f32[8,129,128]{2,0,1:T(8,128)} fusion(f32[8,64,128]{2,0,1:T(8,128)S(1)} %copy.368, f32[8,1,128]{2,0,1:T(8,128)S(1)} %broadcast_in_dim.325, f32[8,64,128]{2,0,1:T(8,128)} %copy.367), kind=kLoop, calls=%fused_computation.45 | loop fusion | flops 264192 | bytes 1056768 | tf_op jit(solution)/shard_map/concatenate | solution.py:169
  88.2 16.2 %collective-permute-done.3 = f32[8,129,128]{2,0,1:T(8,128)} collective-permute-done((f32[8,129,128]{2,0,1:T(8,128)}, f32[8,129,128]{2,0,1:T(8,128)}, u32[]{:S(2)}, u32[]{:S(2)}) %collective-permute-start.3) | collective-permute-done | bytes 528416 | tf_op jit(solution)/shard_map/ppermute | solution.py:169
  105.1 1.1 fusion.94
  106.2 1.2 copy_add_fusion.2
  109.2 16.1 %collective-permute-done.4 = f32[8,129,128]{2,0,1:T(8,128)} collective-permute-done((f32[8,129,128]{2,0,1:T(8,128)}, f32[8,129,128]{2,0,1:T(8,128)}, u32[]{:S(2)}, u32[]{:S(2)}) %collective-permute-start.4) | collective-permute-done | bytes 528416 | tf_op jit(solution)/shard_map/ppermute | solution.py:169
  125.3 1.8 %fusion.93 = (f32[8,64,128]{2,0,1:T(8,128)S(1)}, f32[8,64,128]{2,0,1:T(8,128)}) fusion(f32[8,129,128]{2,0,1:T(8,128)} %collective-permute-done.4), kind=kLoop, calls=%fused_computation.190 | loop fusion | bytes 1048576 | tf_op jit(solution)/shard_map/slice | solution.py:171
  127.8 1.0 multiply_add_fusion
  132.5 1.8 %pad_maximum_fusion.2 = f32[8,129,128]{2,0,1:T(8,128)} fusion(f32[8,64,128]{2,0,1:T(8,128)S(1)} %copy.378, f32[8,1,128]{2,0,1:T(8,128)S(1)} %broadcast_in_dim.333, f32[8,64,128]{2,0,1:T(8,128)} %copy.377), kind=kLoop, calls=%fused_computation.47 | loop fusion | flops 264192 | bytes 1056768 | tf_op jit(solution)/shard_map/concatenate | solution.py:169
  134.3 2.0 %collective-permute-start.5 = (f32[8,129,128]{2,0,1:T(8,128)}, f32[8,129,128]{2,0,1:T(8,128)}, u32[]{:S(2)}, u32[]{:S(2)}) collective-permute-start(f32[8,129,128]{2,0,1:T(8,128)} %pad_maximum_fusion.2), channel_id=1, source_target_pairs={{128,0},{136,8},{144,16},{152,24},{160,32},{168,40},{176,48},{184,... | collective-permute-start | bytes 1585160 | tf_op jit(solution)/shard_map/ppermute | solution.py:169
  136.3 2.3 %copy.383 = bf16[4096,128]{1,0:T(8,128)(2,1)} copy(bf16[4096,128]{0,1:T(8,128)(2,1)} %bitcast.214) | data formatting | bytes 2097152
  138.7 11.8 %collective-permute-done.5 = f32[8,129,128]{2,0,1:T(8,128)} collective-permute-done((f32[8,129,128]{2,0,1:T(8,128)}, f32[8,129,128]{2,0,1:T(8,128)}, u32[]{:S(2)}, u32[]{:S(2)}) %collective-permute-start.5) | collective-permute-done | bytes 528416 | tf_op jit(solution)/shard_map/ppermute | solution.py:169
  151.2 1.1 fusion.92
  152.3 2.1 %bitcast_multiply_fusion = f32[1024,8,64]{0,2,1:T(8,128)S(1)} fusion(f32[1024,8]{0,1:T(8,128)S(1)} %exponential_bitcast_fusion, bf16[1024,128]{1,0:T(8,128)(2,1)} %param.10, f32[8,64,128]{2,1,0:T(8,128)S(1)} %copy-done.15, f32[8,64,128]{2,0,1:T(8,128)S(1)} %get-tuple-element.38, f32[8,64,128]{2,0,1:T(8,128)S(1)} %get-tuple-element.37, ...), kind=kOutput, calls=%fused_computation.22 | convolution fusion | flops 135856128 | bytes 4227237 | tf_op jit(solution)/shard_map/hpn,tn->thp/dot_general | solution.py:190
  154.3 1.4 fusion.15
  155.8 2.3 %copy.382 = bf16[1024,512]{1,0:T(8,128)(2,1)} copy(bf16[1024,512]{0,1:T(8,128)(2,1)} %fusion.15) | data formatting | bytes 2097152
  (222 shorter events, 42.9 us)
Async XLA Ops:
  0.6 38.0 %copy-start = (bf16[4096,128]{1,0:T(8,128)(2,1)S(1)}, bf16[4096,128]{1,0:T(8,128)(2,1)}, u32[]{:S(2)}) copy-start(bf16[4096,128]{1,0:T(8,128)(2,1)} %param.14) | copy-start | bytes 3145732
  0.6 5.2 %copy-start.25 = (s32[4096]{0:T(1024)S(1)}, s32[4096]{0:T(1024)}, u32[]{:S(2)}) copy-start(s32[4096]{0:T(1024)} %param.17) | copy-start | bytes 49156
  0.7 5.1 %copy-start.26 = (f32[2,4096]{1,0:T(2,128)S(1)}, f32[2,4096]{1,0:T(2,128)}, u32[]{:S(2)}) copy-start(f32[2,4096]{1,0:T(2,128)} %param.16) | copy-start | bytes 98308
  4.1 2.3 %copy-start.1 = (bf16[4096,128]{1,0:T(8,128)(2,1)S(1)}, bf16[4096,128]{1,0:T(8,128)(2,1)}, u32[]{:S(2)}) copy-start(bf16[4096,128]{1,0:T(8,128)(2,1)} %param.15) | copy-start | bytes 3145732
  5.9 10.9 %copy-start.32 = (f32[8,1024]{1,0:T(8,128)S(1)}, f32[8,1024]{1,0:T(8,128)}, u32[]{:S(2)}) copy-start(f32[8,1024]{1,0:T(8,128)} %param.12) | copy-start | bytes 98308
  7.5 46.8 %collective-permute-start = (f32[2,64,128]{2,1,0:T(8,128)}, f32[2,64,128]{2,1,0:T(8,128)S(1)}, u32[]{:S(2)}, u32[]{:S(2)}) collective-permute-start(f32[2,64,128]{2,1,0:T(8,128)} %fusion.20), channel_id=1, source_target_pairs={{0,0},{1,32},{2,64},{3,96},{4,128},{5,160},{6,192},{7,224},{8,8},{... | collective-permute-start | bytes 196616 | tf_op jit(solution)/shard_map/ppermute | solution.py:153
  15.0 4.8 %copy-start.40 = (f32[15]{0:T(128)}, f32[15]{0:T(128)S(1)}, u32[]{:S(2)}) copy-start(f32[15]{0:T(128)S(1)} %convert_reduce_fusion) | copy-start | bytes 184
  15.5 10.4 %copy-start.29 = (pred[256,256]{1,0:T(8,128)(4,1)}, pred[256,256]{1,0:T(8,128)(4,1)S(1)}, u32[]{:S(2)}) copy-start(pred[256,256]{1,0:T(8,128)(4,1)S(1)} %iota_compare_fusion.1) | copy-start | bytes 196612
  19.6 18.9 %copy-start.27 = (f32[1,8,8,128]{3,2,1,0:T(8,128)}, f32[1,8,8,128]{3,2,1,0:T(8,128)S(1)}, u32[]{:S(2)}) copy-start(f32[1,8,8,128]{3,2,1,0:T(8,128)S(1)} %fusion.108) | copy-start | bytes 98308
  21.1 1.6 copy-start.4
  24.8 4.0 %copy-start.44 = (f32[4]{0:T(128)S(1)}, f32[4]{0:T(128)}, u32[]{:S(2)}) copy-start(f32[4]{0:T(128)} %constant.36.clone.1) | copy-start | bytes 52
  24.9 5.4 %copy-start.22 = (bf16[1024,512]{1,0:T(8,128)(2,1)S(1)}, bf16[1024,512]{1,0:T(8,128)(2,1)}, u32[]{:S(2)}) copy-start(bf16[1024,512]{1,0:T(8,128)(2,1)} %param.9) | copy-start | bytes 3145732
  30.8 2.4 %copy-start.24 = (bf16[1024,128]{1,0:T(8,128)(2,1)S(1)}, bf16[1024,128]{1,0:T(8,128)(2,1)}, u32[]{:S(2)}) copy-start(bf16[1024,128]{1,0:T(8,128)(2,1)} %param.11) | copy-start | bytes 786436
  31.6 1.5 copy-start.6
  33.6 5.0 %copy-start.3 = (bf16[4096,128]{1,0:T(8,128)(2,1)S(1)}, bf16[4096,128]{1,0:T(8,128)(2,1)}, u32[]{:S(2)}) copy-start(bf16[4096,128]{1,0:T(8,128)(2,1)} %param.15) | copy-start | bytes 3145732
  41.1 4.0 %copy-start.21 = (bf16[16,2,64,128]{3,0,2,1:T(8,128)(2,1)S(1)}, bf16[16,2,64,128]{3,0,2,1:T(8,128)(2,1)}, u32[]{:S(2)}) copy-start(bf16[16,2,64,128]{3,0,2,1:T(8,128)(2,1)} %slice.163) | copy-start | bytes 1572868
  41.1 4.0 %copy-start.31 = (f32[16,256,2]{1,2,0:T(2,128)S(1)}, f32[16,256,2]{1,2,0:T(2,128)}, u32[]{:S(2)}) copy-start(f32[16,256,2]{1,2,0:T(2,128)} %get-tuple-element.46) | copy-start | bytes 98308
  50.3 3.8 %copy-start.13 = (f32[1,8,64,128]{3,0,2,1:T(1,128)}, f32[1,8,64,128]{3,0,2,1:T(1,128)S(1)}, u32[]{:S(2)}) copy-start(f32[1,8,64,128]{3,0,2,1:T(1,128)S(1)} %slice.154) | copy-start | bytes 786436
  55.1 5.0 %collective-permute-start.1 = (f32[8,81,128]{2,0,1:T(8,128)}, f32[8,81,128]{2,0,1:T(8,128)}, u32[]{:S(2)}, u32[]{:S(2)}) collective-permute-start(f32[8,81,128]{2,0,1:T(8,128)} %pad_maximum_fusion.4), channel_id=1, source_target_pairs={{8,0},{16,8},{24,16},{32,24},{40,32},{48,40},{56,48},{64,56},{72,6... | collective-permute-start | bytes 995336 | tf_op jit(solution)/shard_map/ppermute | solution.py:169
  60.9 17.7 %copy-start.36 = (f32[8]{0:T(128)}, f32[8]{0:T(128)S(1)}, u32[]{:S(2)}) copy-start(f32[8]{0:T(128)S(1)} %get-tuple-element.31) | copy-start | bytes 100
  65.6 11.9 %collective-permute-start.2 = (f32[8,97,128]{2,0,1:T(8,128)}, f32[8,97,128]{2,0,1:T(8,128)}, u32[]{:S(2)}, u32[]{:S(2)}) collective-permute-start(f32[8,97,128]{2,0,1:T(8,128)} %pad_maximum_fusion.3), channel_id=1, source_target_pairs={{16,0},{24,8},{32,16},{40,24},{48,32},{56,40},{64,48},{72,56},{80,... | collective-permute-start | bytes 1191944 | tf_op jit(solution)/shard_map/ppermute | solution.py:169
  78.5 1.7 %copy-start.17 = (f32[8,64,128]{2,0,1:T(8,128)}, f32[8,64,128]{2,0,1:T(8,128)S(1)}, u32[]{:S(2)}) copy-start(f32[8,64,128]{2,0,1:T(8,128)S(1)} %slice.169) | copy-start | bytes 786436
  83.2 21.9 %copy-start.39 = (f32[8,1,1]{0,2,1:T(1,128)S(1)}, f32[8,1,1]{0,2,1:T(1,128)}, u32[]{:S(2)}) copy-start(f32[8,1,1]{0,2,1:T(1,128)} %fusion.85) | copy-start | bytes 100
  83.2 21.9 %copy-start.37 = (f32[8]{0:T(128)S(1)}, f32[8]{0:T(128)}, u32[]{:S(2)}) copy-start(f32[8]{0:T(128)} %copy-done.36) | copy-start | bytes 100
  83.2 23.0 %copy-start.38 = (pred[8]{0:T(512)(128)(4,1)S(1)}, pred[8]{0:T(512)(128)(4,1)}, u32[]{:S(2)}) copy-start(pred[8]{0:T(512)(128)(4,1)} %broadcast_in_dim.327) | copy-start | bytes 28
  88.2 16.2 %collective-permute-start.3 = (f32[8,129,128]{2,0,1:T(8,128)}, f32[8,129,128]{2,0,1:T(8,128)}, u32[]{:S(2)}, u32[]{:S(2)}) collective-permute-start(f32[8,129,128]{2,0,1:T(8,128)} %pad_maximum_fusion), channel_id=1, source_target_pairs={{32,0},{40,8},{48,16},{56,24},{64,32},{72,40},{80,48},{88,56},{96,... | collective-permute-start | bytes 1585160 | tf_op jit(solution)/shard_map/ppermute | solution.py:169
  106.2 2.1 %copy-start.18 = (f32[8,64,128]{2,0,1:T(8,128)}, f32[8,64,128]{2,0,1:T(8,128)S(1)}, u32[]{:S(2)}) copy-start(f32[8,64,128]{2,0,1:T(8,128)S(1)} %get-tuple-element.41) | copy-start | bytes 786436
  108.3 22.2 %copy-start.10 = (f32[8,64,128]{2,1,0:T(8,128)S(1)}, f32[8,64,128]{2,1,0:T(8,128)}, u32[]{:S(2)}) copy-start(f32[8,64,128]{2,1,0:T(8,128)} %copy-done.9) | copy-start | bytes 786436
  109.2 16.1 %collective-permute-start.4 = (f32[8,129,128]{2,0,1:T(8,128)}, f32[8,129,128]{2,0,1:T(8,128)}, u32[]{:S(2)}, u32[]{:S(2)}) collective-permute-start(f32[8,129,128]{2,0,1:T(8,128)} %pad_maximum_fusion.1), channel_id=1, source_target_pairs={{64,0},{72,8},{80,16},{88,24},{96,32},{104,40},{112,48},{120,56},{... | collective-permute-start | bytes 1585160 | tf_op jit(solution)/shard_map/ppermute | solution.py:169
  130.5 8.1 %copy-start.28 = (f32[1,8,8,128]{3,2,1,0:T(8,128)S(1)}, f32[1,8,8,128]{3,2,1,0:T(8,128)}, u32[]{:S(2)}) copy-start(f32[1,8,8,128]{3,2,1,0:T(8,128)} %copy-done.27) | copy-start | bytes 98308
  132.5 19.8 %copy-start.15 = (f32[8,64,128]{2,1,0:T(8,128)S(1)}, f32[8,64,128]{2,1,0:T(8,128)}, u32[]{:S(2)}) copy-start(f32[8,64,128]{2,1,0:T(8,128)} %copy-done.14) | copy-start | bytes 786436
  134.3 16.1 %collective-permute-start.5 = (f32[8,129,128]{2,0,1:T(8,128)}, f32[8,129,128]{2,0,1:T(8,128)}, u32[]{:S(2)}, u32[]{:S(2)}) collective-permute-start(f32[8,129,128]{2,0,1:T(8,128)} %pad_maximum_fusion.2), channel_id=1, source_target_pairs={{128,0},{136,8},{144,16},{152,24},{160,32},{168,40},{176,48},{184,... | collective-permute-start | bytes 1585160 | tf_op jit(solution)/shard_map/ppermute | solution.py:169
  (19 other events, 21.2 us)

commit v10 on v5

--- a/solution.py
+++ b/solution.py
@@ -150,6 +150,12 @@
             dst_seq = share * src_resp + src_seq % share
             dst_resp = src_seq // share
             pairs.append((src_seq * resp_len + src_resp, dst_seq * resp_len + dst_resp))
+    shift = 1
+    while shift < resp_len:
+        partial_state = partial_state + lax.ppermute(
+            partial_state, "resp", [(k, k ^ shift) for k in range(resp_len)]
+        )
+        shift *= 2
     pieces = lax.ppermute(partial_state, ("seq", "resp"), pairs)[None]
     whole_b = start_grad
     whole_a = jnp.exp(shard_total)
@@ -162,8 +168,6 @@
         parts = [whole_b, jnp.broadcast_to(whole_a[:, None, None], (head_count, 1, N))]
         if my_heads is None:
             parts.append(pieces.reshape(head_count, -1, N))
-        else:
-            parts.append(my_heads)
         got = lax.ppermute(jnp.concatenate(parts, axis=1), "seq", pairs)
         valid = seq_index + shift < seq_len
         got_b = jnp.where(valid, got[:, :P_SIZE], 0.0)
@@ -176,8 +180,6 @@
                 my_heads = jnp.take(pieces, order, axis=0).reshape(
                     (head_count,) + partial_state.shape[1:]
                 )
-        else:
-            my_heads = my_heads + rest
         later_b = later_b + later_a[:, None, None] * got_b
         later_a = later_a * got_a
         if shift * 2 < seq_len:

time: 141 us -> 156 us (1.11)
  starting transfers between devices: 9.43 us -> 23.5 us
  waiting for transfers between devices: 33 us -> 37 us
  matrix products: 24.7 us -> 21.6 us
  other arithmetic: 27.4 us -> 29.8 us
    ppermute x0 -> x3, starting transfers between devices: none -> 11.4 us  [on_device(): lax.ppermute(partial_state, 'resp', [(k, k ^ shift) for k in range(resp_l...]
    slice x11 -> x1, local copies, waits for them, and re-layouts: 5.99 us -> 0.15 us  [the longest x5 3.79 us: on_device(): got_b = jnp.where(valid, got[:, :P_SIZE], 0.0)]
    ppermute x5, starting transfers between devices: 2.18 us -> 7.25 us  [on_device(): got = lax.ppermute(jnp.concatenate(parts, axis=1), 'seq', pairs)]
    ppermute x1, waiting for transfers between devices: 0.01 us -> 5.03 us  [on_device(): pieces = lax.ppermute(partial_state, ('seq', 'resp'), pairs)[None]]
    ppermute x5, waiting for transfers between devices: 33 us -> 28.2 us  [on_device(): got = lax.ppermute(jnp.concatenate(parts, axis=1), 'seq', pairs)]
    ppermute x0 -> x3, waiting for transfers between devices: none -> 3.75 us  [on_device(): lax.ppermute(partial_state, 'resp', [(k, k ^ shift) for k in range(resp_l...]
    unnamed x110 -> x75, local copies, waits for them, and re-layouts: 19.7 us -> 17.2 us
    ppermute x1, starting transfers between devices: 7.25 us -> 4.82 us  [on_device(): pieces = lax.ppermute(partial_state, ('seq', 'resp'), pairs)[None]]
  transfers between devices with their start and end apart: 6 -> 9, of which waited for: 5 -> 6; matrix products, arithmetic and copies ran while one was open for 48% -> 48% of each run, Pallas kernels for 0% -> 0%
where the time goes in v10:
time: 156 us; the launch traced here: 155 us
  local copies, waits for them, and re-layouts  41.6 us (27%)
  waiting for transfers between devices  37 us (24%)
  other arithmetic  29.8 us (19%)
  starting transfers between devices  23.5 us (15%)
  matrix products  21.6 us (14%)
    ppermute x5, waiting for transfers between devices, on_device(): got = lax.ppermute(jnp.concatenate(parts, axis=1), 'seq', pairs)  28.2 us
    unnamed x75, local copies, waits for them, and re-layouts  17.2 us
    ppermute x3, starting transfers between devices, on_device(): lax.ppermute(partial_state, 'resp', [(k, k ^ shift) for k in range(resp_l...  11.4 us
    dot_general x2, matrix products, group_output(): jnp.einsum('chst,cshp->cthp', mixing, grad_group, preferred_element_type=...  7.44 us
    ppermute x5, starting transfers between devices, on_device(): got = lax.ppermute(jnp.concatenate(parts, axis=1), 'seq', pairs)  7.25 us
    dot_general x2, matrix products, group_parts(): jnp.einsum('hcd,dhpn->chpn', coef, states, precision=lax.Precision.HIGHEST)  6.68 us
    ppermute x1, waiting for transfers between devices, on_device(): pieces = lax.ppermute(partial_state, ('seq', 'resp'), pairs)[None]  5.03 us
    ppermute x1, starting transfers between devices, on_device(): pieces = lax.ppermute(partial_state, ('seq', 'resp'), pairs)[None]  4.82 us
  transfers between devices with their start and end apart: 9, of which 6 were waited for; matrix products, arithmetic and copies ran while one was open for 48% of the time, Pallas kernels for 0%

profile of v10, /device:TPU:14, one launch (start us, length us, event | category | flops | bytes accessed | tf_op | source)
XLA Modules:
  0.0 154.7 jit_solution(6895249678374861759)
XLA Ops:
  2.3 1.6 %copy.119 = bf16[4096,128]{0,1:T(8,128)(2,1)S(1)} copy(bf16[4096,128]{1,0:T(8,128)(2,1)} %param.13) | data formatting | bytes 2097152 | tf_op args[4]
  6.7 1.9 %collective-permute-start = (f32[2,64,128]{2,1,0:T(8,128)}, f32[2,64,128]{2,1,0:T(8,128)}, u32[]{:S(2)}, u32[]{:S(2)}) collective-permute-start(f32[2,64,128]{2,1,0:T(8,128)} %fusion.20), channel_id=1, source_target_pairs={{0,1},{1,0},{2,3},{3,2},{4,5},{5,4},{6,7},{7,6},{8,9},{9,8},{10,11... | collective-permute-start | bytes 196616 | tf_op jit(solution)/shard_map/ppermute | solution.py:155
  14.9 2.3 %reduce-window.14 = f32[8,8,128]{2,1,0:T(8,128)S(1)} reduce-window(f32[8,8,128]{2,1,0:T(8,128)S(1)} %copy.104, f32[]{:T(128)} %constant.35.clone.1), window={size=1x1x128 pad=0_0x0_0x127_0}, to_apply=%region_0.0 | reduce-window | flops 1040384 | bytes 65540 | tf_op jit(solution)/shard_map/reduce-window
  22.0 2.3 %copy.108 = bf16[1024,512]{0,1:T(8,128)(2,1)} copy(bf16[1024,512]{1,0:T(8,128)(2,1)} %param.9) | data formatting | bytes 2097152 | tf_op args[0]
  24.2 1.9 %reshape.386 = bf16[4,256,8,64]{1,0,3,2:T(4,128)(2,1)S(1)} reshape(bf16[1024,512]{0,1:T(8,128)(2,1)} %copy.108) | data formatting | bytes 2097152 | tf_op jit(solution)/shard_map/reshape | solution.py:24
  27.4 2.4 %copy.156 = bf16[16,8,16,256]{3,2,1,0:T(8,128)(2,1)} copy(bf16[16,8,16,256]{3,1,2,0:T(8,128)(2,1)} %bitcast.190) | data formatting | bytes 2097152
  30.5 1.6 %copy.127 = f32[2,16,256]{1,0,2:T(2,128)} copy(f32[2,16,256]{2,1,0:T(8,128)} %bitcast.217) | data formatting | bytes 65536 | tf_op jit(solution)/shard_map/reshape | solution.py:18
  34.3 2.6 %and_and_fusion = pred[16,256,256]{2,1,0:T(8,128)(4,1)S(1)} fusion(s32[16,256]{1,0:T(8,128)S(1)} %eq.82, pred[16,256]{1,0:T(8,128)(4,1)} %and.129, pred[256,256]{1,0:T(8,128)(4,1)} %iota_compare_fusion.1), kind=kLoop, calls=%fused_computation.16 | loop fusion | flops 3145728 | bytes 1134592 | tf_op jit(solution)/shard_map/and | solution.py:75
  40.8 3.8 %convolution_bitcast_fusion = f32[5,8,64,128]{3,0,2,1:T(8,128)} fusion(f32[8,5,4,1]{1,2,3,0:T(4,128)S(1)} %copy-done.21, f32[4,8,64,128]{3,2,1,0:T(8,128)S(1)} %fusion.28), kind=kOutput, calls=%fused_computation.30 | convolution fusion | flops 15728640 | bytes 2359936 | tf_op jit(solution)/shard_map/hcd,dhpn->chpn/dot_general | solution.py:46
  47.1 3.8 %fusion.3 = f32[16,2,256,64]{2,3,1,0:T(8,128)} fusion(f32[16,2,256]{2,1,0:T(2,128)S(1)} %bitcast.222, f32[16,256,256]{2,1,0:T(8,128)S(1)} %fusion.89, pred[16,256,256]{2,1,0:T(8,128)(4,1)S(1)} %and_and_fusion, bf16[16,256,2,64]{1,0,3,2:T(8,128)(2,1)S(1)} %bitcast.192), kind=kOutput, calls=%fused_computation.6 | convolution fusion | flops 276824064 | bytes 8421376 | tf_op jit(solution)/shard_map/chst,cshp->cthp/dot_general | solution.py:82
  50.9 2.8 %fusion.19 = bf16[17,2,64,128]{3,0,2,1:T(8,128)(2,1)} fusion(f32[16,2,64,128]{3,2,1,0:T(8,128)S(1)} %fusion.24, f32[2,17,16]{1,2,0:T(8,128)S(1)} %select_reduce_fusion.1, f32[17]{0:T(128)S(1)} %pad_maximum_fusion.8, pred[17,16]{0,1:T(8,128)(4,1)S(1)} %copy-done.27), kind=kOutput, calls=%fused_computation.32 | convolution fusion | flops 53756992 | bytes 1608148 | tf_op jit(solution)/shard_map/hcd,dhpn->chpn/dot_general | solution.py:46
  54.6 3.4 %collective-permute-start.1 = (f32[2,64,128]{2,1,0:T(8,128)S(1)}, f32[2,64,128]{2,1,0:T(8,128)S(1)}, u32[]{:S(2)}, u32[]{:S(2)}) collective-permute-start(f32[2,64,128]{2,1,0:T(8,128)S(1)} %add.98), channel_id=1, source_target_pairs={{0,2},{1,3},{2,0},{3,1},{4,6},{5,7},{6,4},{7,5},{8,10},{9,11},{10,... | collective-permute-start | bytes 196616 | tf_op jit(solution)/shard_map/ppermute | solution.py:155
  59.2 1.7 %collective-permute-done.1 = f32[2,64,128]{2,1,0:T(8,128)S(1)} collective-permute-done((f32[2,64,128]{2,1,0:T(8,128)S(1)}, f32[2,64,128]{2,1,0:T(8,128)S(1)}, u32[]{:S(2)}, u32[]{:S(2)}) %collective-permute-start.1) | collective-permute-done | bytes 65568 | tf_op jit(solution)/shard_map/ppermute | solution.py:155
  60.9 6.1 %collective-permute-start.2 = (f32[2,64,128]{2,1,0:T(8,128)S(1)}, f32[2,64,128]{2,1,0:T(8,128)S(1)}, u32[]{:S(2)}, u32[]{:S(2)}) collective-permute-start(f32[2,64,128]{2,1,0:T(8,128)S(1)} %add.99), channel_id=1, source_target_pairs={{0,4},{1,5},{2,6},{3,7},{4,0},{5,1},{6,2},{7,3},{8,12},{9,13},{10,... | collective-permute-start | bytes 196616 | tf_op jit(solution)/shard_map/ppermute | solution.py:155
  67.3 2.1 %collective-permute-done.2 = f32[2,64,128]{2,1,0:T(8,128)S(1)} collective-permute-done((f32[2,64,128]{2,1,0:T(8,128)S(1)}, f32[2,64,128]{2,1,0:T(8,128)S(1)}, u32[]{:S(2)}, u32[]{:S(2)}) %collective-permute-start.2) | collective-permute-done | bytes 65568 | tf_op jit(solution)/shard_map/ppermute | solution.py:155
  69.4 4.8 %collective-permute-start.3 = (f32[2,64,128]{2,1,0:T(8,128)S(1)}, f32[2,64,128]{2,1,0:T(8,128)S(1)}, u32[]{:S(2)}, u32[]{:S(2)}) collective-permute-start(f32[2,64,128]{2,1,0:T(8,128)S(1)} %add.100), channel_id=1, source_target_pairs={{0,0},{1,32},{2,64},{3,96},{4,128},{5,160},{6,192},{7,224},{8,8},{... | collective-permute-start | bytes 196616 | tf_op jit(solution)/shard_map/ppermute | solution.py:159
  74.3 1.8 %slice.143 = f32[1,8,64,128]{3,0,2,1:T(1,128)S(1)} slice(f32[5,8,64,128]{3,0,2,1:T(8,128)} %convolution_bitcast_fusion), slice={[0:1], [0:8], [0:64], [0:128]} | slice | bytes 524288 | tf_op jit(solution)/shard_map/slice | solution.py:49
  76.0 5.0 %collective-permute-done.3 = f32[2,64,128]{2,1,0:T(8,128)S(1)} collective-permute-done((f32[2,64,128]{2,1,0:T(8,128)S(1)}, f32[2,64,128]{2,1,0:T(8,128)S(1)}, u32[]{:S(2)}, u32[]{:S(2)}) %collective-permute-start.3) | collective-permute-done | bytes 65568 | tf_op jit(solution)/shard_map/ppermute | solution.py:159
  81.9 2.7 %slice.259 = bf16[4,8,64,128]{3,0,2,1:T(4,128)(2,1)} slice(f32[5,8,64,128]{3,0,2,1:T(8,128)} %convolution_bitcast_fusion), slice={[1:5], [0:8], [0:64], [0:128]} | slice | bytes 1048576 | tf_op jit(solution)/shard_map/slice | solution.py:50
  85.3 1.4 slice.165
  86.7 1.6 %fusion.33 = f32[4,8,64,256]{3,2,1,0:T(8,128)S(1)} fusion(bf16[4,256,128,1]{2,1,3,0:T(8,128)(2,1)S(1)} %bitcast.196, bf16[4,8,64,128]{3,0,2,1:T(4,128)(2,1)} %slice.259), kind=kOutput, calls=%fused_computation.46 | convolution fusion | flops 134217728 | bytes 2883584 | tf_op jit(solution)/shard_map/chpn,ctn->cthp/dot_general | solution.py:85
  92.3 3.6 %fusion.18 = f32[4,256,8,64]{1,3,2,0:T(8,128)} fusion(f32[4,8,64,256]{3,2,1,0:T(8,128)S(1)} %fusion.33, f32[4,8,256]{2,1,0:T(8,128)S(1)} %copy-done.26, f32[4,256,256]{2,1,0:T(8,128)S(1)} %copy-done.7, pred[256,256]{1,0:T(8,128)(4,1)S(1)} %copy-done.17, bf16[4,256,8,64]{1,0,3,2:T(4,128)(2,1)S(1)} %reshape.386, f32[4,256,8]{1,2,0:T(8,128)S(1)} %copy-done.24), kind=kOutput, calls=%fused_computation.27 | convolution fusion | flops 277872640 | bytes 6422528 | tf_op jit(solution)/shard_map/chst,cshp->cthp/dot_general | solution.py:82
  95.9 9.8 %collective-permute-done.5 = f32[8,97,128]{2,1,0:T(8,128)S(1)} collective-permute-done((f32[8,97,128]{2,1,0:T(8,128)S(1)}, f32[8,97,128]{2,1,0:T(8,128)S(1)}, u32[]{:S(2)}, u32[]{:S(2)}) %collective-permute-start.5) | collective-permute-done | bytes 397344 | tf_op jit(solution)/shard_map/ppermute | solution.py:171
  106.9 1.4 fusion.16
  108.4 10.1 %collective-permute-done.6 = f32[8,65,128]{2,1,0:T(8,128)S(1)} collective-permute-done((f32[8,65,128]{2,1,0:T(8,128)S(1)}, f32[8,65,128]{2,1,0:T(8,128)S(1)}, u32[]{:S(2)}, u32[]{:S(2)}) %collective-permute-start.6) | collective-permute-done | bytes 266272 | tf_op jit(solution)/shard_map/ppermute | solution.py:171
  121.0 8.3 %collective-permute-done.7 = f32[8,65,128]{2,1,0:T(8,128)S(1)} collective-permute-done((f32[8,65,128]{2,1,0:T(8,128)S(1)}, f32[8,65,128]{2,1,0:T(8,128)S(1)}, u32[]{:S(2)}, u32[]{:S(2)}) %collective-permute-start.7) | collective-permute-done | bytes 266272 | tf_op jit(solution)/shard_map/ppermute | solution.py:171
  130.3 6.1 %collective-permute-start.8 = (f32[8,65,128]{2,1,0:T(8,128)}, f32[8,65,128]{2,1,0:T(8,128)}, u32[]{:S(2)}, u32[]{:S(2)}) collective-permute-start(f32[8,65,128]{2,1,0:T(8,128)} %pad_maximum_fusion.4), channel_id=1, source_target_pairs={{128,0},{136,8},{144,16},{152,24},{160,32},{168,40},{176,48},{184,... | collective-permute-start | bytes 798728 | tf_op jit(solution)/shard_map/ppermute | solution.py:171
  136.5 2.9 %copy.117 = f32[4,256,8,64]{1,0,3,2:T(4,128)S(1)} copy(f32[4,256,8,64]{1,3,2,0:T(8,128)} %fusion.18) | data formatting | bytes 4194304 | tf_op jit(solution)/shard_map/add | solution.py:96
  139.5 1.8 %copy.152 = f32[64,8,4,256]{3,1,2,0:T(8,128)} copy(f32[64,8,4,256]{3,2,1,0:T(4,128)S(1)} %bitcast.186) | data formatting | bytes 4194304
  142.0 4.5 %copy.149 = bf16[16,256,2,64]{3,2,1,0:T(2,128)(2,1)S(1)} copy(bf16[16,256,2,64]{1,3,2,0:T(8,128)(2,1)} %fusion.16) | data formatting | bytes 2097152
  146.5 1.8 %reshape.418 = bf16[4096,128]{1,0:T(8,128)(2,1)} reshape(bf16[16,256,2,64]{3,2,1,0:T(2,128)(2,1)S(1)} %copy.149) | data formatting | bytes 2097152
  150.8 1.7 %fusion.40 = bf16[8,64,128]{2,1,0:T(8,128)(2,1)S(1)} fusion(f32[8,65,128]{2,1,0:T(8,128)} %collective-permute-done.8, f32[4,2,64,128]{3,2,1,0:T(8,128)S(1)} %gather_fusion, f32[8,81,128]{2,1,0:T(8,128)} %collective-permute-done.4, f32[8,97,128]{2,1,0:T(8,128)} %copy-done.10, f32[8,65,128]{2,1,0:T(8,128)} %copy-done.12, f32[8,65,128]{2,1,0:T(8,128)} %copy-done.11, ...), kind=kLoop, calls=%fused_computation.60 | loop fusion | flops 1114112 | bytes 1704109 | tf_op jit(solution)/shard_map/convert_element_type | solution.py:193
  (177 shorter events, 43.8 us)
Async XLA Ops:
  0.6 44.1 %copy-start = (bf16[4096,128]{1,0:T(8,128)(2,1)S(1)}, bf16[4096,128]{1,0:T(8,128)(2,1)}, u32[]{:S(2)}) copy-start(bf16[4096,128]{1,0:T(8,128)(2,1)} %param.14) | copy-start | bytes 3145732
  0.7 3.4 %copy-start.14 = (f32[2,4096]{1,0:T(2,128)S(1)}, f32[2,4096]{1,0:T(2,128)}, u32[]{:S(2)}) copy-start(f32[2,4096]{1,0:T(2,128)} %param.16) | copy-start | bytes 98308
  3.9 18.1 %copy-start.3 = (bf16[4096,128]{0,1:T(8,128)(2,1)}, bf16[4096,128]{0,1:T(8,128)(2,1)S(1)}, u32[]{:S(2)}) copy-start(bf16[4096,128]{0,1:T(8,128)(2,1)S(1)} %copy.119) | copy-start | bytes 3145732
  5.1 9.7 %copy-start.20 = (f32[8,1024]{1,0:T(8,128)S(1)}, f32[8,1024]{1,0:T(8,128)}, u32[]{:S(2)}) copy-start(f32[8,1024]{1,0:T(8,128)} %param.12) | copy-start | bytes 98308
  5.6 14.7 %copy-start.31 = (f32[4]{0:T(128)S(1)}, f32[4]{0:T(128)}, u32[]{:S(2)}) copy-start(f32[4]{0:T(128)} %constant.37.clone.1) | copy-start | bytes 52
  5.7 15.5 %copy-start.29 = (f32[5]{0:T(128)S(1)}, f32[5]{0:T(128)}, u32[]{:S(2)}) copy-start(f32[5]{0:T(128)} %constant.63.clone.1) | copy-start | bytes 64
  6.7 47.0 %collective-permute-start = (f32[2,64,128]{2,1,0:T(8,128)}, f32[2,64,128]{2,1,0:T(8,128)}, u32[]{:S(2)}, u32[]{:S(2)}) collective-permute-start(f32[2,64,128]{2,1,0:T(8,128)} %fusion.20), channel_id=1, source_target_pairs={{0,1},{1,0},{2,3},{3,2},{4,5},{5,4},{6,7},{7,6},{8,9},{9,8},{10,11... | collective-permute-start | bytes 196616 | tf_op jit(solution)/shard_map/ppermute | solution.py:155
  17.5 8.6 %copy-start.22 = (f32[8,9]{1,0:T(8,128)}, f32[8,9]{1,0:T(8,128)S(1)}, u32[]{:S(2)}) copy-start(f32[8,9]{1,0:T(8,128)S(1)} %reduce-window.15) | copy-start | bytes 868
  29.9 10.5 %copy-start.8 = (bf16[1024,128]{1,0:T(8,128)(2,1)S(1)}, bf16[1024,128]{1,0:T(8,128)(2,1)}, u32[]{:S(2)}) copy-start(bf16[1024,128]{1,0:T(8,128)(2,1)} %param.11) | copy-start | bytes 786436
  50.9 7.1 %copy-start.5 = (bf16[1024,128]{1,0:T(8,128)(2,1)S(1)}, bf16[1024,128]{1,0:T(8,128)(2,1)}, u32[]{:S(2)}) copy-start(bf16[1024,128]{1,0:T(8,128)(2,1)} %param.10) | copy-start | bytes 786436
  50.9 7.1 %copy-start.9 = (bf16[1024,128]{1,0:T(8,128)(2,1)S(1)}, bf16[1024,128]{1,0:T(8,128)(2,1)}, u32[]{:S(2)}) copy-start(bf16[1024,128]{1,0:T(8,128)(2,1)} %param.11) | copy-start | bytes 786436
  50.9 16.2 %copy-start.23 = (f32[8,9]{1,0:T(8,128)S(1)}, f32[8,9]{1,0:T(8,128)}, u32[]{:S(2)}) copy-start(f32[8,9]{1,0:T(8,128)} %copy-done.22) | copy-start | bytes 868
  54.6 6.3 %collective-permute-start.1 = (f32[2,64,128]{2,1,0:T(8,128)S(1)}, f32[2,64,128]{2,1,0:T(8,128)S(1)}, u32[]{:S(2)}, u32[]{:S(2)}) collective-permute-start(f32[2,64,128]{2,1,0:T(8,128)S(1)} %add.98), channel_id=1, source_target_pairs={{0,2},{1,3},{2,0},{3,1},{4,6},{5,7},{6,4},{7,5},{8,10},{9,11},{10,... | collective-permute-start | bytes 196616 | tf_op jit(solution)/shard_map/ppermute | solution.py:155
  60.9 8.5 %collective-permute-start.2 = (f32[2,64,128]{2,1,0:T(8,128)S(1)}, f32[2,64,128]{2,1,0:T(8,128)S(1)}, u32[]{:S(2)}, u32[]{:S(2)}) collective-permute-start(f32[2,64,128]{2,1,0:T(8,128)S(1)} %add.99), channel_id=1, source_target_pairs={{0,4},{1,5},{2,6},{3,7},{4,0},{5,1},{6,2},{7,3},{8,12},{9,13},{10,... | collective-permute-start | bytes 196616 | tf_op jit(solution)/shard_map/ppermute | solution.py:155
  67.1 21.2 %copy-start.15 = (f32[1,8,8,128]{3,2,1,0:T(8,128)}, f32[1,8,8,128]{3,2,1,0:T(8,128)S(1)}, u32[]{:S(2)}) copy-start(f32[1,8,8,128]{3,2,1,0:T(8,128)S(1)} %fusion.100) | copy-start | bytes 98308
  69.4 11.7 %collective-permute-start.3 = (f32[2,64,128]{2,1,0:T(8,128)S(1)}, f32[2,64,128]{2,1,0:T(8,128)S(1)}, u32[]{:S(2)}, u32[]{:S(2)}) collective-permute-start(f32[2,64,128]{2,1,0:T(8,128)S(1)} %add.100), channel_id=1, source_target_pairs={{0,0},{1,32},{2,64},{3,96},{4,128},{5,160},{6,192},{7,224},{8,8},{... | collective-permute-start | bytes 196616 | tf_op jit(solution)/shard_map/ppermute | solution.py:159
  81.9 6.4 %collective-permute-start.4 = (f32[8,81,128]{2,1,0:T(8,128)}, f32[8,81,128]{2,1,0:T(8,128)}, u32[]{:S(2)}, u32[]{:S(2)}) collective-permute-start(f32[8,81,128]{2,1,0:T(8,128)} %pad_maximum_fusion.1), channel_id=1, source_target_pairs={{8,0},{16,8},{24,16},{32,24},{40,32},{48,40},{56,48},{64,56},{72,6... | collective-permute-start | bytes 995336 | tf_op jit(solution)/shard_map/ppermute | solution.py:171
  86.7 5.5 %copy-start.7 = (f32[4,256,256]{2,1,0:T(8,128)S(1)}, f32[4,256,256]{2,1,0:T(8,128)}, u32[]{:S(2)}) copy-start(f32[4,256,256]{2,1,0:T(8,128)} %fusion.88) | copy-start | bytes 3145732
  86.7 5.5 %copy-start.17 = (pred[256,256]{1,0:T(8,128)(4,1)S(1)}, pred[256,256]{1,0:T(8,128)(4,1)}, u32[]{:S(2)}) copy-start(pred[256,256]{1,0:T(8,128)(4,1)} %iota_compare_fusion.1) | copy-start | bytes 196612
  86.7 5.5 %copy-start.24 = (f32[4,256,8]{1,2,0:T(8,128)S(1)}, f32[4,256,8]{1,2,0:T(8,128)}, u32[]{:S(2)}) copy-start(f32[4,256,8]{1,2,0:T(8,128)} %get-tuple-element.34) | copy-start | bytes 98308
  86.7 5.5 %copy-start.26 = (f32[4,8,256]{2,1,0:T(8,128)S(1)}, f32[4,8,256]{2,1,0:T(8,128)}, u32[]{:S(2)}) copy-start(f32[4,8,256]{2,1,0:T(8,128)} %copy.106) | copy-start | bytes 98308
  91.3 14.4 %collective-permute-start.5 = (f32[8,97,128]{2,1,0:T(8,128)S(1)}, f32[8,97,128]{2,1,0:T(8,128)S(1)}, u32[]{:S(2)}, u32[]{:S(2)}) collective-permute-start(f32[8,97,128]{2,1,0:T(8,128)S(1)} %pad_maximum_fusion), channel_id=1, source_target_pairs={{16,0},{24,8},{32,16},{40,24},{48,32},{56,40},{64,48},{72,56},{80,... | collective-permute-start | bytes 1191944 | tf_op jit(solution)/shard_map/ppermute | solution.py:171
  92.2 14.7 %copy-start.6 = (f32[16,2,256,64]{2,3,1,0:T(8,128)S(1)}, f32[16,2,256,64]{2,3,1,0:T(8,128)}, u32[]{:S(2)}) copy-start(f32[16,2,256,64]{2,3,1,0:T(8,128)} %fusion.3) | copy-start | bytes 6291460
  92.3 14.7 %copy-start.19 = (f32[16,256,2]{1,2,0:T(2,128)S(1)}, f32[16,256,2]{1,2,0:T(2,128)}, u32[]{:S(2)}) copy-start(f32[16,256,2]{1,2,0:T(2,128)} %get-tuple-element.33) | copy-start | bytes 98308
  105.7 12.8 %copy-start.10 = (f32[8,97,128]{2,1,0:T(8,128)}, f32[8,97,128]{2,1,0:T(8,128)S(1)}, u32[]{:S(2)}) copy-start(f32[8,97,128]{2,1,0:T(8,128)S(1)} %collective-permute-done.5) | copy-start | bytes 1191940
  106.8 11.7 %collective-permute-start.6 = (f32[8,65,128]{2,1,0:T(8,128)S(1)}, f32[8,65,128]{2,1,0:T(8,128)S(1)}, u32[]{:S(2)}, u32[]{:S(2)}) collective-permute-start(f32[8,65,128]{2,1,0:T(8,128)S(1)} %pad_maximum_fusion.2), channel_id=1, source_target_pairs={{32,0},{40,8},{48,16},{56,24},{64,32},{72,40},{80,48},{88,56},{96,... | collective-permute-start | bytes 798728 | tf_op jit(solution)/shard_map/ppermute | solution.py:171
  106.9 13.4 %copy-start.16 = (f32[1,8,8,128]{3,2,1,0:T(8,128)S(1)}, f32[1,8,8,128]{3,2,1,0:T(8,128)}, u32[]{:S(2)}) copy-start(f32[1,8,8,128]{3,2,1,0:T(8,128)} %copy-done.15) | copy-start | bytes 98308
  118.5 20.9 %copy-start.12 = (f32[8,65,128]{2,1,0:T(8,128)}, f32[8,65,128]{2,1,0:T(8,128)S(1)}, u32[]{:S(2)}) copy-start(f32[8,65,128]{2,1,0:T(8,128)S(1)} %collective-permute-done.6) | copy-start | bytes 798724
  119.7 9.6 %collective-permute-start.7 = (f32[8,65,128]{2,1,0:T(8,128)S(1)}, f32[8,65,128]{2,1,0:T(8,128)S(1)}, u32[]{:S(2)}, u32[]{:S(2)}) collective-permute-start(f32[8,65,128]{2,1,0:T(8,128)S(1)} %pad_maximum_fusion.3), channel_id=1, source_target_pairs={{64,0},{72,8},{80,16},{88,24},{96,32},{104,40},{112,48},{120,56},{... | collective-permute-start | bytes 798728 | tf_op jit(solution)/shard_map/ppermute | solution.py:171
  129.3 10.2 %copy-start.11 = (f32[8,65,128]{2,1,0:T(8,128)}, f32[8,65,128]{2,1,0:T(8,128)S(1)}, u32[]{:S(2)}) copy-start(f32[8,65,128]{2,1,0:T(8,128)S(1)} %collective-permute-done.7) | copy-start | bytes 798724
  130.3 19.5 %collective-permute-start.8 = (f32[8,65,128]{2,1,0:T(8,128)}, f32[8,65,128]{2,1,0:T(8,128)}, u32[]{:S(2)}, u32[]{:S(2)}) collective-permute-start(f32[8,65,128]{2,1,0:T(8,128)} %pad_maximum_fusion.4), channel_id=1, source_target_pairs={{128,0},{136,8},{144,16},{152,24},{160,32},{168,40},{176,48},{184,... | collective-permute-start | bytes 798728 | tf_op jit(solution)/shard_map/ppermute | solution.py:171
  148.3 4.2 %copy-start.18 = (f32[1024,8]{0,1:T(8,128)S(1)}, f32[1024,8]{0,1:T(8,128)}, u32[]{:S(2)}) copy-start(f32[1024,8]{0,1:T(8,128)} %exponential_bitcast_fusion) | copy-start | bytes 98308
  (9 other events, 15.7 us)
